TPU v7x, 256 devices: a whole 4x4x8 slice. The times are simulated.
256 devices in a mesh: ctx: 32 (over y, z), tp: 8 (over x, core).
Axes of the slice: x: 4, y: 4, z: 8, core: 2. Of those that a mesh axis runs over, the one named last changes fastest.
Arguments:
- residual: bfloat16 [8192, 8192], P('ctx', 'tp'), may hold values from -90 to 90
- hyena_gate: bfloat16 [8192, 8192], P('ctx', 'tp'), may hold values from -6 to 6
- hyena_key: bfloat16 [8192, 8192], P('ctx', 'tp'), may hold values from -6 to 6
- hyena_value: bfloat16 [8192, 8192], P('ctx', 'tp'), may hold values from -6 to 6
- filter_taps: float32 [512, 128], P('tp'), may hold values from -0.45 to 0.45
- norm_gain: float32 [8192], P('tp'), may hold values from 0.5 to 1.5
- att_query: bfloat16 [8192, 8192], P('ctx', 'tp'), may hold values from -180 to 180
- att_key: bfloat16 [8192, 8192], P('ctx', 'tp'), may hold values from -6 to 6
- att_value: bfloat16 [8192, 8192], P('ctx', 'tp'), may hold values from -6 to 6
- doc_lengths: int32 [32], replicated, may hold values from 1 to 768, 8192 in all
Outputs:
- normed: bfloat16 [8192, 8192], P('ctx', 'tp')
- attended: bfloat16 [8192, 8192], P('ctx', 'tp')
Inputs may be any that keep to these rules, and one draw needn't show every extreme that they name: `doc_lengths`: the lengths sum to 8192; the longest document has exactly 768 tokens.
All inputs are finite; a program needn't handle non-finite values.
Results may differ from a plain program's by a relative error of at most 0.0075.
Values may be sent and summed in bfloat16 or wider, within the bound.
No kernel may reach another device: no remote copies, remote signals or barrier semaphores. Data moves between devices by JAX's collectives and lax.ppermute only.
A program may use at most 128 MiB of HBM per device.

v0:
```python
import jax
import jax.numpy as jnp
from jax import lax
from jax.sharding import PartitionSpec as P

D = 8192
HEAD_DIM = 128
REACH = 3


norm_epsilon = 1e-05


def shifted(value, axis, steps):
    count = lax.axis_size(axis)
    first, last = (max(0, -steps), min(count, count - steps))
    return lax.ppermute(value, axis, [(source, source + steps) for source in range(first, last)])


def document_begin(doc_lengths, positions):
    count = doc_lengths.shape[0]
    order = jnp.arange(count, dtype=jnp.int32)
    before = order[None, :] < order[:, None]
    starts = jnp.sum(jnp.where(before, doc_lengths[None, :], 0), axis=1)
    return jnp.max(jnp.where(starts[None, :] <= positions[:, None], starts[None, :], 0), axis=1)


def causal_filter(extended, filter_taps, reach_back, out_rows):
    groups, taps = filter_taps.shape
    channels = extended.shape[1]
    width = channels // groups
    lag_table = (
        jnp.arange(taps, dtype=jnp.int32)[:, None]
        + (taps - 1)
        - jnp.arange(2 * taps - 1, dtype=jnp.int32)[None, :]
    )
    reversed_taps = filter_taps[:, ::-1]
    period = jnp.concatenate([reversed_taps, jnp.zeros((groups, taps), jnp.float32)], axis=1)
    tiled = jnp.tile(period, (1, taps))
    toeplitz = tiled[:, : taps * (2 * taps - 1)].reshape(groups, taps, 2 * taps - 1)
    upper_part = toeplitz.astype(jnp.bfloat16)
    lower_part = (toeplitz - upper_part.astype(jnp.float32)).astype(jnp.bfloat16)
    zero_half = jnp.zeros((), jnp.bfloat16)
    numbers = (((0,), (2,)), ((1,), (0,)))
    results = []
    for block_index in range(out_rows // taps):
        first = block_index * taps
        sources = extended[first : first + 2 * taps - 1].reshape(2 * taps - 1, groups, width)
        limits = reach_back[first : first + taps]
        valid = (lag_table <= limits[:, None])[None]
        kernel_upper = jnp.where(valid, upper_part, zero_half)
        kernel_lower = jnp.where(valid, lower_part, zero_half)
        result = lax.dot_general(sources, kernel_upper, numbers, preferred_element_type=jnp.float32)
        result = result + lax.dot_general(
            sources, kernel_lower, numbers, preferred_element_type=jnp.float32
        )
        results.append(result.transpose(2, 0, 1).reshape(taps, channels))
    return jnp.concatenate(results, axis=0)


def attend_one(query_head, key_head, value_head, visible, scale):
    scores = (
        lax.dot_general(
            query_head, key_head, (((1,), (1,)), ((), ())), preferred_element_type=jnp.float32
        )
        * scale
    )
    scores = jnp.where(visible, scores, jnp.float32(-1e30))
    top = jnp.max(scores, axis=1, keepdims=True)
    expo = jnp.where(visible, jnp.exp(scores - top), jnp.float32(0.0))
    denominator = jnp.sum(expo, axis=1, keepdims=True)
    summed = jnp.dot(expo.astype(jnp.bfloat16), value_head, preferred_element_type=jnp.float32)
    return (summed / denominator).astype(jnp.bfloat16)


def on_device(
    residual,
    hyena_gate,
    hyena_key,
    hyena_value,
    filter_taps,
    norm_gain,
    att_query,
    att_key,
    att_value,
    doc_lengths,
):
    tok_rows = residual.shape[0]
    taps = filter_taps.shape[1]
    shard_index = lax.axis_index("ctx")
    anchor = shard_index * tok_rows
    positions = anchor + jnp.arange(tok_rows, dtype=jnp.int32)
    doc_begin = document_begin(doc_lengths, positions)
    mixed_rows = (hyena_key.astype(jnp.float32) * hyena_value.astype(jnp.float32)).astype(
        jnp.bfloat16
    )
    rim_rows = shifted(mixed_rows[tok_rows - (taps - 1) :], "ctx", 1)
    extended = jnp.concatenate([rim_rows, mixed_rows], axis=0)
    filtered = causal_filter(extended, filter_taps, positions - doc_begin, tok_rows)
    hidden = residual.astype(jnp.float32) + hyena_gate.astype(jnp.float32) * filtered
    local_sum = jnp.sum(hidden * hidden, axis=1)
    mean_square = lax.psum(local_sum, "tp") / D
    normed = (hidden * lax.rsqrt(mean_square + norm_epsilon)[:, None] * norm_gain[None, :]).astype(
        jnp.bfloat16
    )
    key_pair = jnp.stack([att_key, att_value])
    pieces = [shifted(key_pair, "ctx", distance) for distance in range(REACH, 0, -1)]
    key_rows = jnp.concatenate([piece[0] for piece in pieces] + [att_key], axis=0)
    value_rows = jnp.concatenate([piece[1] for piece in pieces] + [att_value], axis=0)
    window = key_rows.shape[0]
    key_pos = anchor - REACH * tok_rows + jnp.arange(window, dtype=jnp.int32)
    visible = (key_pos[None, :] <= positions[:, None]) & (key_pos[None, :] >= doc_begin[:, None])
    scale = jnp.float32(1.0 / HEAD_DIM**0.5)
    head_count = att_query.shape[1] // HEAD_DIM
    outputs = []
    for head_index in range(head_count):
        lower = head_index * HEAD_DIM
        upper = lower + HEAD_DIM
        outputs.append(
            attend_one(
                att_query[:, lower:upper],
                key_rows[:, lower:upper],
                value_rows[:, lower:upper],
                visible,
                scale,
            )
        )
    attended = jnp.concatenate(outputs, axis=1)
    return (normed, attended)


def solution(mesh):
    placed = (
        P("ctx", "tp"),
        P("ctx", "tp"),
        P("ctx", "tp"),
        P("ctx", "tp"),
        P("tp", None),
        P("tp"),
        P("ctx", "tp"),
        P("ctx", "tp"),
        P("ctx", "tp"),
        P(),
    )
    return jax.shard_map(
        on_device,
        mesh=mesh,
        in_specs=placed,
        out_specs=(P("ctx", "tp"), P("ctx", "tp")),
        check_vma=False,
    )
```

profile of v0, /device:TPU:24, one launch (start us, length us, event | category | flops | bytes accessed | tf_op | source)
XLA Modules:
  0.0 204.7 jit_solution(1755644438468193703)
XLA Ops:
  0.6 2.3 %pad_maximum_fusion.2 = bf16[2,256,1024]{2,1,0:T(8,128)(2,1)} fusion(bf16[1,256,1024]{2,1,0:T(8,128)(2,1)} %bitcast.69, bf16[1,256,1024]{2,1,0:T(8,128)(2,1)} %bitcast.68), kind=kLoop, calls=%fused_computation.71 | loop fusion | flops 524288 | bytes 2097152 | tf_op jit(solution)/shard_map/stack | solution.py:106
  2.9 3.8 %collective-permute-start.3 = (bf16[2,256,1024]{2,1,0:T(8,128)(2,1)}, bf16[2,256,1024]{2,1,0:T(8,128)(2,1)}, u32[]{:S(2)}, u32[]{:S(2)}) collective-permute-start(bf16[2,256,1024]{2,1,0:T(8,128)(2,1)} %pad_maximum_fusion.2), channel_id=1, source_target_pairs={{0,8},{8,16},{16,24},{24,32},{32,40},{40,48},{48,56},{56,64},{64,7... | collective-permute-start | bytes 3145736 | tf_op jit(solution)/shard_map/ppermute | solution.py:17
  6.8 5.2 %collective-permute-start.2 = (bf16[2,256,1024]{2,1,0:T(8,128)(2,1)}, bf16[2,256,1024]{2,1,0:T(8,128)(2,1)}, u32[]{:S(2)}, u32[]{:S(2)}) collective-permute-start(bf16[2,256,1024]{2,1,0:T(8,128)(2,1)} %pad_maximum_fusion.2), channel_id=1, source_target_pairs={{0,16},{8,24},{16,32},{24,40},{32,48},{40,56},{48,64},{56,72},{64,... | collective-permute-start | bytes 3145736 | tf_op jit(solution)/shard_map/ppermute | solution.py:17
  12.0 5.9 %collective-permute-start.1 = (bf16[2,256,1024]{2,1,0:T(8,128)(2,1)}, bf16[2,256,1024]{2,1,0:T(8,128)(2,1)}, u32[]{:S(2)}, u32[]{:S(2)}) collective-permute-start(bf16[2,256,1024]{2,1,0:T(8,128)(2,1)} %pad_maximum_fusion.2), channel_id=1, source_target_pairs={{0,24},{8,32},{16,40},{24,48},{32,56},{40,64},{48,72},{56,80},{64,... | collective-permute-start | bytes 3145736 | tf_op jit(solution)/shard_map/ppermute | solution.py:17
  17.9 1.4 multiply_convert_fusion.1
  19.4 2.9 %collective-permute-start = (bf16[127,1024]{1,0:T(8,128)(2,1)S(1)}, bf16[127,1024]{1,0:T(8,128)(2,1)S(1)}, u32[]{:S(2)}, u32[]{:S(2)}) collective-permute-start(bf16[127,1024]{1,0:T(8,128)(2,1)S(1)} %slice.144), channel_id=1, source_target_pairs={{0,8},{8,16},{16,24},{24,32},{32,40},{40,48},{48,56},{56,64},{64,7... | collective-permute-start | bytes 780296 | tf_op jit(solution)/shard_map/ppermute | solution.py:17
  22.7 0.7 tile.4
  23.4 4.7 %copy.27 = f32[8,8,128,256]{3,1,2,0:T(8,128)S(1)} copy(f32[8,8,128,256]{3,2,1,0:T(8,128)S(1)} %bitcast.60) | data formatting | bytes 16777216
  28.1 3.7 %slice.145 = f32[64,32640]{1,0:T(8,128)} slice(f32[64,32768]{1,0:T(8,128)S(1)} %bitcast.61), slice={[0:64], [0:32640]} | slice | bytes 16711680 | tf_op jit(solution)/shard_map/slice | solution.py:40
  31.8 15.9 %reshape.118 = f32[64,128,255]{2,1,0:T(8,128)} reshape(f32[64,32640]{1,0:T(8,128)} %slice.145) | data formatting | bytes 16711680 | tf_op jit(solution)/shard_map/reshape | solution.py:40
  47.9 104.3 %collective-permute-done = bf16[127,1024]{1,0:T(8,128)(2,1)S(1)} collective-permute-done((bf16[127,1024]{1,0:T(8,128)(2,1)S(1)}, bf16[127,1024]{1,0:T(8,128)(2,1)S(1)}, u32[]{:S(2)}, u32[]{:S(2)}) %collective-permute-start) | collective-permute-done | bytes 260128 | tf_op jit(solution)/shard_map/ppermute | solution.py:17
  152.6 7.1 %fusion = f32[64,16,128]{2,1,0:T(8,128)S(1)} fusion(bf16[255,64,16]{0,2,1:T(8,128)(2,1)S(1)} %bitcast.64, pred[128,255]{1,0:T(8,128)(4,1)S(1)} %get-tuple-element.27, f32[64,128,255]{2,1,0:T(8,128)} %reshape.118), kind=kOutput, calls=%fused_computation.1 | convolution fusion | flops 77291520 | bytes 9435008 | tf_op jit(solution)/shard_map/dot_general | solution.py:54
  159.7 1.0 copy-done
  160.8 1.2 fusion.35
  162.2 7.0 %fusion.4 = f32[64,16,128]{2,1,0:T(8,128)S(1)} fusion(bf16[255,64,16]{0,2,1:T(8,128)(2,1)S(1)} %bitcast.62, pred[128,255]{1,0:T(8,128)(4,1)S(1)} %get-tuple-element.26, f32[64,128,255]{2,1,0:T(8,128)} %reshape.118), kind=kOutput, calls=%fused_computation.5 | convolution fusion | flops 77291520 | bytes 9435008 | tf_op jit(solution)/shard_map/dot_general | solution.py:54
  169.1 4.7 %fusion.32 = f32[64,16,128]{2,1,0:T(8,128)S(1)} fusion(f32[64,16,128]{2,1,0:T(8,128)S(1)} %fusion.4, bf16[255,64,16]{0,2,1:T(8,128)(2,1)S(1)} %bitcast.63, pred[128,255]{1,0:T(8,128)(4,1)S(1)} %get-tuple-element.26, f32[64,128,255]{2,1,0:T(8,128)} %reshape.118), kind=kOutput, calls=%fused_computation.43 | convolution fusion | flops 71155712 | bytes 9959296 | tf_op jit(solution)/shard_map/dot_general | solution.py:53
  174.5 14.0 %psum.7 = f32[256]{0:T(256)S(1)} all-reduce(f32[256]{0:T(256)S(1)} %multiply_reduce_fusion), channel_id=1, replica_groups=mesh['ctx'=32,'tp'=8] {'tp'}, use_global_device_ids=true, to_apply=%region_3.4 | all-reduce | flops 256 | bytes 2048 | tf_op jit(solution)/shard_map/psum | solution.py:102
  188.6 1.0 multiply_convert_fusion
  189.6 1.3 slice_bitcast_fusion
  190.9 1.3 slice_bitcast_fusion.1
  192.2 1.3 slice_bitcast_fusion.2
  193.5 0.6 pad_maximum_fusion
  197.7 2.0 fusion.69
  203.7 1.0 copy.26
  (53 shorter events, 9.3 us)
Async XLA Ops:
  0.6 21.7 %copy-start.8 = (s32[32]{0:T(128)S(1)}, s32[32]{0:T(128)}, u32[]{:S(2)}) copy-start(s32[32]{0:T(128)} %param.19) | copy-start | bytes 388
  0.6 22.0 %copy-start.5 = (f32[64,128]{1,0:T(8,128)S(1)}, f32[64,128]{1,0:T(8,128)}, u32[]{:S(2)}) copy-start(f32[64,128]{1,0:T(8,128)} %param.14) | copy-start | bytes 98308
  2.9 186.7 %collective-permute-start.3 = (bf16[2,256,1024]{2,1,0:T(8,128)(2,1)}, bf16[2,256,1024]{2,1,0:T(8,128)(2,1)}, u32[]{:S(2)}, u32[]{:S(2)}) collective-permute-start(bf16[2,256,1024]{2,1,0:T(8,128)(2,1)} %pad_maximum_fusion.2), channel_id=1, source_target_pairs={{0,8},{8,16},{16,24},{24,32},{32,40},{40,48},{48,56},{56,64},{64,7... | collective-permute-start | bytes 3145736 | tf_op jit(solution)/shard_map/ppermute | solution.py:17
  6.8 184.1 %collective-permute-start.2 = (bf16[2,256,1024]{2,1,0:T(8,128)(2,1)}, bf16[2,256,1024]{2,1,0:T(8,128)(2,1)}, u32[]{:S(2)}, u32[]{:S(2)}) collective-permute-start(bf16[2,256,1024]{2,1,0:T(8,128)(2,1)} %pad_maximum_fusion.2), channel_id=1, source_target_pairs={{0,16},{8,24},{16,32},{24,40},{32,48},{40,56},{48,64},{56,72},{64,... | collective-permute-start | bytes 3145736 | tf_op jit(solution)/shard_map/ppermute | solution.py:17
  12.0 180.2 %collective-permute-start.1 = (bf16[2,256,1024]{2,1,0:T(8,128)(2,1)}, bf16[2,256,1024]{2,1,0:T(8,128)(2,1)}, u32[]{:S(2)}, u32[]{:S(2)}) collective-permute-start(bf16[2,256,1024]{2,1,0:T(8,128)(2,1)} %pad_maximum_fusion.2), channel_id=1, source_target_pairs={{0,24},{8,32},{16,40},{24,48},{32,56},{40,64},{48,72},{56,80},{64,... | collective-permute-start | bytes 3145736 | tf_op jit(solution)/shard_map/ppermute | solution.py:17
  19.4 132.8 %collective-permute-start = (bf16[127,1024]{1,0:T(8,128)(2,1)S(1)}, bf16[127,1024]{1,0:T(8,128)(2,1)S(1)}, u32[]{:S(2)}, u32[]{:S(2)}) collective-permute-start(bf16[127,1024]{1,0:T(8,128)(2,1)S(1)} %slice.144), channel_id=1, source_target_pairs={{0,8},{8,16},{16,24},{24,32},{32,40},{40,48},{48,56},{56,64},{64,7... | collective-permute-start | bytes 780296 | tf_op jit(solution)/shard_map/ppermute | solution.py:17
  152.6 8.2 %copy-start = (f32[64,128,255]{2,1,0:T(8,128)S(1)}, f32[64,128,255]{2,1,0:T(8,128)}, u32[]{:S(2)}) copy-start(f32[64,128,255]{2,1,0:T(8,128)} %reshape.118) | copy-start | bytes 25067524
  169.1 5.1 %copy-start.1 = (bf16[256,1024]{1,0:T(8,128)(2,1)S(1)}, bf16[256,1024]{1,0:T(8,128)(2,1)}, u32[]{:S(2)}) copy-start(bf16[256,1024]{1,0:T(8,128)(2,1)} %param.11) | copy-start | bytes 1572868
  169.1 5.1 %copy-start.2 = (bf16[256,1024]{1,0:T(8,128)(2,1)S(1)}, bf16[256,1024]{1,0:T(8,128)(2,1)}, u32[]{:S(2)}) copy-start(bf16[256,1024]{1,0:T(8,128)(2,1)} %param.10) | copy-start | bytes 1572868
  173.8 14.8 %copy-start.6 = (f32[1024]{0:T(1024)S(1)}, f32[1024]{0:T(1024)}, u32[]{:S(2)}) copy-start(f32[1024]{0:T(1024)} %param.15) | copy-start | bytes 12292
  188.6 4.9 %copy-start.3 = (bf16[256,1024]{1,0:T(8,128)(2,1)S(1)}, bf16[256,1024]{1,0:T(8,128)(2,1)}, u32[]{:S(2)}) copy-start(bf16[256,1024]{1,0:T(8,128)(2,1)} %param.17) | copy-start | bytes 1572868
  188.6 4.9 %copy-start.4 = (bf16[256,1024]{1,0:T(8,128)(2,1)S(1)}, bf16[256,1024]{1,0:T(8,128)(2,1)}, u32[]{:S(2)}) copy-start(bf16[256,1024]{1,0:T(8,128)(2,1)} %param.18) | copy-start | bytes 1572868
  193.5 1.0 copy-start.7
where the time goes:
time: 205 us
  waiting for transfers between devices  104 us (51%)
  local copies, waits for them, and re-layouts  32.3 us (16%)
  matrix products  27 us (13%)
  starting transfers between devices  17.9 us (9%)
  blocking collectives  14 us (7%)
  other arithmetic  8.13 us (4%)
    ppermute x4, waiting for transfers between devices, shifted(): lax.ppermute(value, axis, [(source, source + steps) for source in range(f...  104 us
    ppermute x4, starting transfers between devices, shifted(): lax.ppermute(value, axis, [(source, source + steps) for source in range(f...  17.9 us
    reshape x1, local copies, waits for them, and re-layouts, causal_filter(): tiled[:, :taps * (2 * taps - 1)].reshape(groups, taps, 2 * taps - 1)  15.9 us
    dot_general x2, matrix products, causal_filter(): lax.dot_general(sources, kernel_lower, numbers, preferred_element_type=jn...  14.1 us
    psum x1, blocking collectives, on_device(): mean_square = lax.psum(local_sum, 'tp') / D  14 us
    unnamed x20, local copies, waits for them, and re-layouts  7.19 us
    dot_general x2, matrix products, causal_filter(): lax.dot_general(sources, kernel_upper, numbers, preferred_element_type=jn...  5.87 us
  transfers between devices with their start and end apart: 4, of which 1 were waited for; matrix products, arithmetic and copies ran while one was open for 25% of the time, Pallas kernels for 0%

commit v1 on v0

--- a/solution.py
+++ b/solution.py
@@ -104,7 +104,11 @@
         jnp.bfloat16
     )
     key_pair = jnp.stack([att_key, att_value])
-    pieces = [shifted(key_pair, "ctx", distance) for distance in range(REACH, 0, -1)]
+    pieces = []
+    relayed = key_pair
+    for _ in range(REACH):
+        relayed = shifted(relayed, "ctx", 1)
+        pieces.insert(0, relayed)
     key_rows = jnp.concatenate([piece[0] for piece in pieces] + [att_key], axis=0)
     value_rows = jnp.concatenate([piece[1] for piece in pieces] + [att_value], axis=0)
     window = key_rows.shape[0]

time: 205 us -> 114 us (0.56)
  waiting for transfers between devices: 104 us -> 19.4 us
  starting transfers between devices: 17.9 us -> 14.2 us
    ppermute x4, waiting for transfers between devices: 104 us -> 19.4 us  [shifted(): lax.ppermute(value, axis, [(source, source + steps) for source in range(f...]
    ppermute x4, starting transfers between devices: 17.9 us -> 14.2 us  [shifted(): lax.ppermute(value, axis, [(source, source + steps) for source in range(f...]
  transfers between devices with their start and end apart: 4 -> 4, of which waited for: 1 -> 2; matrix products, arithmetic and copies ran while one was open for 25% -> 46% of each run, Pallas kernels for 0% -> 0%
where the time goes in v1:
time: 114 us; the launch traced here: 113 us
  local copies, waits for them, and re-layouts  31.3 us (27%)
  matrix products  27 us (24%)
  waiting for transfers between devices  19.4 us (17%)
  starting transfers between devices  14.2 us (12%)
  blocking collectives  13.3 us (12%)
  other arithmetic  7.14 us (6%)
    ppermute x4, waiting for transfers between devices, shifted(): lax.ppermute(value, axis, [(source, source + steps) for source in range(f...  19.4 us
    reshape x1, local copies, waits for them, and re-layouts, causal_filter(): tiled[:, :taps * (2 * taps - 1)].reshape(groups, taps, 2 * taps - 1)  15.9 us
    ppermute x4, starting transfers between devices, shifted(): lax.ppermute(value, axis, [(source, source + steps) for source in range(f...  14.2 us
    dot_general x2, matrix products, causal_filter(): lax.dot_general(sources, kernel_lower, numbers, preferred_element_type=jn...  14.1 us
    psum x1, blocking collectives, on_device(): mean_square = lax.psum(local_sum, 'tp') / D  13.3 us
    unnamed x20, local copies, waits for them, and re-layouts  6.15 us
    dot_general x2, matrix products, causal_filter(): lax.dot_general(sources, kernel_upper, numbers, preferred_element_type=jn...  5.86 us
    dot_general x8, matrix products, attend_one(): jnp.dot(expo.astype(jnp.bfloat16), value_head, preferred_element_type=jnp...  3.94 us
  transfers between devices with their start and end apart: 4, of which 2 were waited for; matrix products, arithmetic and copies ran while one was open for 46% of the time, Pallas kernels for 0%

profile of v1, /device:TPU:24, one launch (start us, length us, event | category | flops | bytes accessed | tf_op | source)
XLA Modules:
  0.0 113.3 jit_solution(14298272364096176723)
XLA Ops:
  0.7 1.4 %multiply_convert_fusion.1 = bf16[256,1024]{1,0:T(8,128)(2,1)S(1)} fusion(bf16[256,1024]{1,0:T(8,128)(2,1)} %param.13, bf16[256,1024]{1,0:T(8,128)(2,1)} %param.12), kind=kLoop, calls=%fused_computation.82 | loop fusion | flops 1048576 | bytes 1572864 | tf_op jit(solution)/shard_map/convert_element_type | solution.py:94
  2.1 3.8 %collective-permute-start = (bf16[127,1024]{1,0:T(8,128)(2,1)S(1)}, bf16[127,1024]{1,0:T(8,128)(2,1)S(1)}, u32[]{:S(2)}, u32[]{:S(2)}) collective-permute-start(bf16[127,1024]{1,0:T(8,128)(2,1)S(1)} %slice.144), channel_id=1, source_target_pairs={{0,8},{8,16},{16,24},{24,32},{32,40},{40,48},{48,56},{56,64},{64,7... | collective-permute-start | bytes 780296 | tf_op jit(solution)/shard_map/ppermute | solution.py:17
  6.0 1.3 %pad_maximum_fusion.2 = bf16[2,256,1024]{2,1,0:T(8,128)(2,1)S(1)} fusion(bf16[1,256,1024]{2,1,0:T(8,128)(2,1)} %bitcast.69, bf16[1,256,1024]{2,1,0:T(8,128)(2,1)} %bitcast.68), kind=kLoop, calls=%fused_computation.71 | loop fusion | flops 524288 | bytes 2097152 | tf_op jit(solution)/shard_map/stack | solution.py:106
  7.3 3.8 %collective-permute-start.1 = (bf16[2,256,1024]{2,1,0:T(8,128)(2,1)S(1)}, bf16[2,256,1024]{2,1,0:T(8,128)(2,1)}, u32[]{:S(2)}, u32[]{:S(2)}) collective-permute-start(bf16[2,256,1024]{2,1,0:T(8,128)(2,1)S(1)} %pad_maximum_fusion.2), channel_id=1, source_target_pairs={{0,8},{8,16},{16,24},{24,32},{32,40},{40,48},{48,56},{56,64},{64,7... | collective-permute-start | bytes 3145736 | tf_op jit(solution)/shard_map/ppermute | solution.py:17
  11.5 0.7 tile.4
  12.1 4.7 %copy.27 = f32[8,8,128,256]{3,1,2,0:T(8,128)S(1)} copy(f32[8,8,128,256]{3,2,1,0:T(8,128)S(1)} %bitcast.60) | data formatting | bytes 16777216
  16.9 3.7 %slice.145 = f32[64,32640]{1,0:T(8,128)} slice(f32[64,32768]{1,0:T(8,128)S(1)} %bitcast.61), slice={[0:64], [0:32640]} | slice | bytes 16711680 | tf_op jit(solution)/shard_map/slice | solution.py:40
  20.6 15.9 %reshape.118 = f32[64,128,255]{2,1,0:T(8,128)} reshape(f32[64,32640]{1,0:T(8,128)} %slice.145) | data formatting | bytes 16711680 | tf_op jit(solution)/shard_map/reshape | solution.py:40
  37.1 7.1 %fusion = f32[64,16,128]{2,1,0:T(8,128)S(1)} fusion(bf16[255,64,16]{0,2,1:T(8,128)(2,1)S(1)} %bitcast.62, pred[128,255]{1,0:T(8,128)(4,1)S(1)} %get-tuple-element.27, f32[64,128,255]{2,1,0:T(8,128)} %reshape.118), kind=kOutput, calls=%fused_computation.1 | convolution fusion | flops 77291520 | bytes 9435008 | tf_op jit(solution)/shard_map/dot_general | solution.py:54
  44.2 4.1 %collective-permute-start.2 = (bf16[2,256,1024]{2,1,0:T(8,128)(2,1)}, bf16[2,256,1024]{2,1,0:T(8,128)(2,1)}, u32[]{:S(2)}, u32[]{:S(2)}) collective-permute-start(bf16[2,256,1024]{2,1,0:T(8,128)(2,1)} %collective-permute-done.1), channel_id=1, source_target_pairs={{0,8},{8,16},{16,24},{24,32},{32,40},{40,48},{48,56},{56,64},{64,7... | collective-permute-start | bytes 3145736 | tf_op jit(solution)/shard_map/ppermute | solution.py:17
  48.4 1.2 %fusion.35 = f32[64,16,128]{2,1,0:T(8,128)S(1)} fusion(f32[64,16,128]{2,1,0:T(8,128)S(1)} %fusion, bf16[255,64,16]{0,2,1:T(8,128)(2,1)S(1)} %bitcast.63, pred[128,255]{1,0:T(8,128)(4,1)S(1)} %get-tuple-element.27, f32[64,128,255]{2,1,0:T(8,128)S(1)} %copy-done), kind=kOutput, calls=%fused_computation.44 | convolution fusion | flops 71155712 | bytes 9959296 | tf_op jit(solution)/shard_map/dot_general | solution.py:53
  50.0 7.0 %fusion.4 = f32[64,16,128]{2,1,0:T(8,128)S(1)} fusion(bf16[255,64,16]{0,2,1:T(8,128)(2,1)S(1)} %bitcast.64, pred[128,255]{1,0:T(8,128)(4,1)S(1)} %get-tuple-element.26, f32[64,128,255]{2,1,0:T(8,128)} %reshape.118), kind=kOutput, calls=%fused_computation.5 | convolution fusion | flops 77291520 | bytes 9435008 | tf_op jit(solution)/shard_map/dot_general | solution.py:54
  57.0 4.7 %fusion.32 = f32[64,16,128]{2,1,0:T(8,128)S(1)} fusion(f32[64,16,128]{2,1,0:T(8,128)S(1)} %fusion.4, bf16[255,64,16]{0,2,1:T(8,128)(2,1)S(1)} %bitcast.65, pred[128,255]{1,0:T(8,128)(4,1)S(1)} %get-tuple-element.26, f32[64,128,255]{2,1,0:T(8,128)} %reshape.118), kind=kOutput, calls=%fused_computation.43 | convolution fusion | flops 71155712 | bytes 9959296 | tf_op jit(solution)/shard_map/dot_general | solution.py:53
  61.8 11.2 %collective-permute-done.2 = bf16[2,256,1024]{2,1,0:T(8,128)(2,1)} collective-permute-done((bf16[2,256,1024]{2,1,0:T(8,128)(2,1)}, bf16[2,256,1024]{2,1,0:T(8,128)(2,1)}, u32[]{:S(2)}, u32[]{:S(2)}) %collective-permute-start.2) | collective-permute-done | bytes 1048608 | tf_op jit(solution)/shard_map/ppermute | solution.py:17
  73.0 2.4 %collective-permute-start.3 = (bf16[2,256,1024]{2,1,0:T(8,128)(2,1)}, bf16[2,256,1024]{2,1,0:T(8,128)(2,1)}, u32[]{:S(2)}, u32[]{:S(2)}) collective-permute-start(bf16[2,256,1024]{2,1,0:T(8,128)(2,1)} %collective-permute-done.2), channel_id=1, source_target_pairs={{0,8},{8,16},{16,24},{24,32},{32,40},{40,48},{48,56},{56,64},{64,7... | collective-permute-start | bytes 3145736 | tf_op jit(solution)/shard_map/ppermute | solution.py:17
  75.7 13.3 %psum.7 = f32[256]{0:T(256)S(1)} all-reduce(f32[256]{0:T(256)S(1)} %multiply_reduce_fusion), channel_id=1, replica_groups=mesh['ctx'=32,'tp'=8] {'tp'}, use_global_device_ids=true, to_apply=%region_3.4 | all-reduce | flops 256 | bytes 2048 | tf_op jit(solution)/shard_map/psum | solution.py:102
  89.0 1.0 multiply_convert_fusion
  90.0 1.3 %slice_bitcast_fusion = (bf16[256,1024]{1,0:T(8,128)(2,1)S(1)}, bf16[256,1024]{1,0:T(8,128)(2,1)S(1)}) fusion(bf16[2,256,1024]{2,1,0:T(8,128)(2,1)} %collective-permute-done.1), kind=kLoop, calls=%fused_computation.100 | loop fusion | bytes 2097152 | tf_op jit(solution)/shard_map/squeeze | solution.py:113
  91.3 1.3 %slice_bitcast_fusion.1 = (bf16[256,1024]{1,0:T(8,128)(2,1)S(1)}, bf16[256,1024]{1,0:T(8,128)(2,1)S(1)}) fusion(bf16[2,256,1024]{2,1,0:T(8,128)(2,1)} %collective-permute-done.2), kind=kLoop, calls=%fused_computation.101 | loop fusion | bytes 2097152 | tf_op jit(solution)/shard_map/squeeze | solution.py:113
  92.6 8.2 %collective-permute-done.3 = bf16[2,256,1024]{2,1,0:T(8,128)(2,1)} collective-permute-done((bf16[2,256,1024]{2,1,0:T(8,128)(2,1)}, bf16[2,256,1024]{2,1,0:T(8,128)(2,1)}, u32[]{:S(2)}, u32[]{:S(2)}) %collective-permute-start.3) | collective-permute-done | bytes 1048608 | tf_op jit(solution)/shard_map/ppermute | solution.py:17
  100.8 1.3 %slice_bitcast_fusion.2 = (bf16[256,1024]{1,0:T(8,128)(2,1)S(1)}, bf16[256,1024]{1,0:T(8,128)(2,1)S(1)}) fusion(bf16[2,256,1024]{2,1,0:T(8,128)(2,1)} %collective-permute-done.3), kind=kLoop, calls=%fused_computation.102 | loop fusion | bytes 2097152 | tf_op jit(solution)/shard_map/squeeze | solution.py:113
  102.1 0.6 pad_maximum_fusion
  106.3 2.0 %fusion.69 = (f32[256]{0:T(256)S(1)}, f32[256]{0:T(256)S(1)}, f32[256]{0:T(256)S(1)}, f32[256]{0:T(256)S(1)}, f32[256]{0:T(256)S(1)}, /*index=5*/f32[256]{0:T(256)S(1)}, f32[256]{0:T(256)S(1)}, f32[256]{0:T(256)S(1)}) fusion(f32[256,1024]{0,1:T(8,128)S(1)} %get-tuple-element.31, f32[256]{0:T(256)S(1)} %get-tuple-element.30, s32[256]{0:T(256)S(1)} %select_reduce_fusion, ...), kind=kLoop, calls=%fused_computation.98 | loop fusion | flops 7075840 | bytes 8411136 | tf_op jit(solution)/shard_map/reduce_sum | solution.py:71
  112.3 1.0 copy.26
  (53 shorter events, 9.3 us)
Async XLA Ops:
  0.6 10.5 %copy-start.8 = (s32[32]{0:T(128)S(1)}, s32[32]{0:T(128)}, u32[]{:S(2)}) copy-start(s32[32]{0:T(128)} %param.19) | copy-start | bytes 388
  0.6 10.7 %copy-start.5 = (f32[64,128]{1,0:T(8,128)S(1)}, f32[64,128]{1,0:T(8,128)}, u32[]{:S(2)}) copy-start(f32[64,128]{1,0:T(8,128)} %param.14) | copy-start | bytes 98308
  2.1 34.6 %collective-permute-start = (bf16[127,1024]{1,0:T(8,128)(2,1)S(1)}, bf16[127,1024]{1,0:T(8,128)(2,1)S(1)}, u32[]{:S(2)}, u32[]{:S(2)}) collective-permute-start(bf16[127,1024]{1,0:T(8,128)(2,1)S(1)} %slice.144), channel_id=1, source_target_pairs={{0,8},{8,16},{16,24},{24,32},{32,40},{40,48},{48,56},{56,64},{64,7... | collective-permute-start | bytes 780296 | tf_op jit(solution)/shard_map/ppermute | solution.py:17
  7.3 36.9 %collective-permute-start.1 = (bf16[2,256,1024]{2,1,0:T(8,128)(2,1)S(1)}, bf16[2,256,1024]{2,1,0:T(8,128)(2,1)}, u32[]{:S(2)}, u32[]{:S(2)}) collective-permute-start(bf16[2,256,1024]{2,1,0:T(8,128)(2,1)S(1)} %pad_maximum_fusion.2), channel_id=1, source_target_pairs={{0,8},{8,16},{16,24},{24,32},{32,40},{40,48},{48,56},{56,64},{64,7... | collective-permute-start | bytes 3145736 | tf_op jit(solution)/shard_map/ppermute | solution.py:17
  37.1 11.3 %copy-start = (f32[64,128,255]{2,1,0:T(8,128)S(1)}, f32[64,128,255]{2,1,0:T(8,128)}, u32[]{:S(2)}) copy-start(f32[64,128,255]{2,1,0:T(8,128)} %reshape.118) | copy-start | bytes 25067524
  44.2 28.8 %collective-permute-start.2 = (bf16[2,256,1024]{2,1,0:T(8,128)(2,1)}, bf16[2,256,1024]{2,1,0:T(8,128)(2,1)}, u32[]{:S(2)}, u32[]{:S(2)}) collective-permute-start(bf16[2,256,1024]{2,1,0:T(8,128)(2,1)} %collective-permute-done.1), channel_id=1, source_target_pairs={{0,8},{8,16},{16,24},{24,32},{32,40},{40,48},{48,56},{56,64},{64,7... | collective-permute-start | bytes 3145736 | tf_op jit(solution)/shard_map/ppermute | solution.py:17
  56.9 18.4 %copy-start.1 = (bf16[256,1024]{1,0:T(8,128)(2,1)S(1)}, bf16[256,1024]{1,0:T(8,128)(2,1)}, u32[]{:S(2)}) copy-start(bf16[256,1024]{1,0:T(8,128)(2,1)} %param.11) | copy-start | bytes 1572868
  56.9 18.4 %copy-start.2 = (bf16[256,1024]{1,0:T(8,128)(2,1)S(1)}, bf16[256,1024]{1,0:T(8,128)(2,1)}, u32[]{:S(2)}) copy-start(bf16[256,1024]{1,0:T(8,128)(2,1)} %param.10) | copy-start | bytes 1572868
  56.9 32.0 %copy-start.6 = (f32[1024]{0:T(1024)S(1)}, f32[1024]{0:T(1024)}, u32[]{:S(2)}) copy-start(f32[1024]{0:T(1024)} %param.15) | copy-start | bytes 12292
  73.0 27.8 %collective-permute-start.3 = (bf16[2,256,1024]{2,1,0:T(8,128)(2,1)}, bf16[2,256,1024]{2,1,0:T(8,128)(2,1)}, u32[]{:S(2)}, u32[]{:S(2)}) collective-permute-start(bf16[2,256,1024]{2,1,0:T(8,128)(2,1)} %collective-permute-done.2), channel_id=1, source_target_pairs={{0,8},{8,16},{16,24},{24,32},{32,40},{40,48},{48,56},{56,64},{64,7... | collective-permute-start | bytes 3145736 | tf_op jit(solution)/shard_map/ppermute | solution.py:17
  89.0 13.1 %copy-start.3 = (bf16[256,1024]{1,0:T(8,128)(2,1)S(1)}, bf16[256,1024]{1,0:T(8,128)(2,1)}, u32[]{:S(2)}) copy-start(bf16[256,1024]{1,0:T(8,128)(2,1)} %param.17) | copy-start | bytes 1572868
  89.0 13.1 %copy-start.4 = (bf16[256,1024]{1,0:T(8,128)(2,1)S(1)}, bf16[256,1024]{1,0:T(8,128)(2,1)}, u32[]{:S(2)}) copy-start(bf16[256,1024]{1,0:T(8,128)(2,1)} %param.18) | copy-start | bytes 1572868
  102.1 1.0 copy-start.7

commit v2 on v0

--- a/solution.py
+++ b/solution.py
@@ -58,7 +58,7 @@
     return jnp.concatenate(results, axis=0)
 
 
-def attend_one(query_head, key_head, value_head, visible, scale):
+def attend_part(query_head, key_head, value_head, visible, scale):
     scores = (
         lax.dot_general(
             query_head, key_head, (((1,), (1,)), ((), ())), preferred_element_type=jnp.float32
@@ -70,7 +70,22 @@
     expo = jnp.where(visible, jnp.exp(scores - top), jnp.float32(0.0))
     denominator = jnp.sum(expo, axis=1, keepdims=True)
     summed = jnp.dot(expo.astype(jnp.bfloat16), value_head, preferred_element_type=jnp.float32)
-    return (summed / denominator).astype(jnp.bfloat16)
+    return summed, top, denominator
+
+
+def attend_block(queries, keys, values, visible, scale):
+    head_count = queries.shape[1] // HEAD_DIM
+    sums, tops, dens = [], [], []
+    for head_index in range(head_count):
+        lower = head_index * HEAD_DIM
+        upper = lower + HEAD_DIM
+        summed, top, den = attend_part(
+            queries[:, lower:upper], keys[:, lower:upper], values[:, lower:upper], visible, scale
+        )
+        sums.append(summed)
+        tops.append(top)
+        dens.append(den)
+    return jnp.stack(sums, axis=1), jnp.concatenate(tops, axis=1), jnp.concatenate(dens, axis=1)
 
 
 def on_device(
@@ -95,6 +110,21 @@
         jnp.bfloat16
     )
     rim_rows = shifted(mixed_rows[tok_rows - (taps - 1) :], "ctx", 1)
+    key_pair = jnp.stack([att_key, att_value])
+    previous = shifted(key_pair, "ctx", 1)
+    later_query = shifted(att_query, "ctx", -2)
+    key_rows = jnp.concatenate([previous[0], att_key], axis=0)
+    value_rows = jnp.concatenate([previous[1], att_value], axis=0)
+    window = key_rows.shape[0]
+    key_pos = anchor - tok_rows + jnp.arange(window, dtype=jnp.int32)
+    scale = jnp.float32(1.0 / HEAD_DIM**0.5)
+    far_pos = positions + 2 * tok_rows
+    far_begin = document_begin(doc_lengths, far_pos)
+    far_visible = (key_pos[None, :] <= far_pos[:, None]) & (key_pos[None, :] >= far_begin[:, None])
+    far_sum, far_top, far_den = attend_block(later_query, key_rows, value_rows, far_visible, scale)
+    far_packet = (far_sum.astype(jnp.bfloat16), far_top, far_den)
+    far_packet, mixed_rows = lax.optimization_barrier((far_packet, mixed_rows))
+    far_sum, far_top, far_den = shifted(far_packet, "ctx", 2)
     extended = jnp.concatenate([rim_rows, mixed_rows], axis=0)
     filtered = causal_filter(extended, filter_taps, positions - doc_begin, tok_rows)
     hidden = residual.astype(jnp.float32) + hyena_gate.astype(jnp.float32) * filtered
@@ -103,29 +133,15 @@
     normed = (hidden * lax.rsqrt(mean_square + norm_epsilon)[:, None] * norm_gain[None, :]).astype(
         jnp.bfloat16
     )
-    key_pair = jnp.stack([att_key, att_value])
-    pieces = [shifted(key_pair, "ctx", distance) for distance in range(REACH, 0, -1)]
-    key_rows = jnp.concatenate([piece[0] for piece in pieces] + [att_key], axis=0)
-    value_rows = jnp.concatenate([piece[1] for piece in pieces] + [att_value], axis=0)
-    window = key_rows.shape[0]
-    key_pos = anchor - REACH * tok_rows + jnp.arange(window, dtype=jnp.int32)
     visible = (key_pos[None, :] <= positions[:, None]) & (key_pos[None, :] >= doc_begin[:, None])
-    scale = jnp.float32(1.0 / HEAD_DIM**0.5)
-    head_count = att_query.shape[1] // HEAD_DIM
-    outputs = []
-    for head_index in range(head_count):
-        lower = head_index * HEAD_DIM
-        upper = lower + HEAD_DIM
-        outputs.append(
-            attend_one(
-                att_query[:, lower:upper],
-                key_rows[:, lower:upper],
-                value_rows[:, lower:upper],
-                visible,
-                scale,
-            )
-        )
-    attended = jnp.concatenate(outputs, axis=1)
+    near_sum, near_top, near_den = attend_block(att_query, key_rows, value_rows, visible, scale)
+    far_top = jnp.where(far_den > 0, far_top, jnp.float32(-1e30))
+    top = jnp.maximum(near_top, far_top)
+    near_scale = jnp.exp(near_top - top)
+    far_scale = jnp.exp(far_top - top)
+    denominator = near_den * near_scale + far_den * far_scale
+    summed = near_sum * near_scale[:, :, None] + far_sum.astype(jnp.float32) * far_scale[:, :, None]
+    attended = (summed / denominator[:, :, None]).astype(jnp.bfloat16).reshape(tok_rows, -1)
     return (normed, attended)
 
 

time: 205 us -> 138 us (0.67)
  waiting for transfers between devices: 104 us -> 0.97 us
  matrix products: 27 us -> 49.1 us
  starting transfers between devices: 17.9 us -> 24.3 us
  other arithmetic: 8.13 us -> 13.9 us
    ppermute x4 -> x6, waiting for transfers between devices: 104 us -> 0.97 us  [shifted(): lax.ppermute(value, axis, [(source, source + steps) for source in range(f...]
    dot_general x16 -> x32, matrix products: 7.12 us -> 25.2 us  [the longest x16 18.6 us: attend_part(): lax.dot_general(query_head, key_head, (((1,), (1,)), ((), ())), preferred...]
    ppermute x4 -> x6, starting transfers between devices: 17.9 us -> 24.3 us  [shifted(): lax.ppermute(value, axis, [(source, source + steps) for source in range(f...]
    dot_general x2, matrix products: 5.87 us -> 9.99 us  [causal_filter(): lax.dot_general(sources, kernel_upper, numbers, preferred_element_type=jn...]
    squeeze x3 -> x1, local copies, waits for them, and re-layouts: 3.81 us -> 0.07 us  [on_device(): value_rows = jnp.concatenate([previous[1], att_value], axis=0)]
    reshape x2, local copies, waits for them, and re-layouts: 0.41 us -> 3.07 us  [causal_filter(): results.append(result.transpose(2, 0, 1).reshape(taps, channels))]
    convert_element_type x0 -> x1, other arithmetic: none -> 2.13 us  [on_device(): (summed / denominator[:, :, None]).astype(jnp.bfloat16)]
    unnamed x20 -> x36, local copies, waits for them, and re-layouts: 7.19 us -> 6.79 us
  transfers between devices with their start and end apart: 4 -> 6, of which waited for: 1 -> 1; matrix products, arithmetic and copies ran while one was open for 25% -> 66% of each run, Pallas kernels for 0% -> 0%
where the time goes in v2:
time: 138 us; the launch traced here: 136 us
  matrix products  49.1 us (36%)
  local copies, waits for them, and re-layouts  34.2 us (25%)
  starting transfers between devices  24.3 us (18%)
  other arithmetic  13.9 us (10%)
  blocking collectives  12.9 us (9%)
    ppermute x6, starting transfers between devices, shifted(): lax.ppermute(value, axis, [(source, source + steps) for source in range(f...  24.3 us
    dot_general x16, matrix products, attend_part(): lax.dot_general(query_head, key_head, (((1,), (1,)), ((), ())), preferred...  18.6 us
    reshape x1, local copies, waits for them, and re-layouts, causal_filter(): tiled[:, :taps * (2 * taps - 1)].reshape(groups, taps, 2 * taps - 1)  16 us
    dot_general x2, matrix products, causal_filter(): lax.dot_general(sources, kernel_lower, numbers, preferred_element_type=jn...  13.9 us
    psum x1, blocking collectives, on_device(): mean_square = lax.psum(local_sum, 'tp') / D  12.9 us
    dot_general x2, matrix products, causal_filter(): lax.dot_general(sources, kernel_upper, numbers, preferred_element_type=jn...  9.99 us
    unnamed x36, local copies, waits for them, and re-layouts  6.79 us
    dot_general x16, matrix products, attend_part(): jnp.dot(expo.astype(jnp.bfloat16), value_head, preferred_element_type=jnp...  6.62 us
  transfers between devices with their start and end apart: 6, of which 1 were waited for; matrix products, arithmetic and copies ran while one was open for 66% of the time, Pallas kernels for 0%

profile of v2, /device:TPU:24, one launch (start us, length us, event | category | flops | bytes accessed | tf_op | source)
XLA Modules:
  0.0 136.5 jit_solution(9986038495159426855)
XLA Ops:
  0.6 1.4 %multiply_convert_fusion.1 = bf16[256,1024]{1,0:T(8,128)(2,1)S(1)} fusion(bf16[256,1024]{1,0:T(8,128)(2,1)} %param.13, bf16[256,1024]{1,0:T(8,128)(2,1)} %param.12), kind=kLoop, calls=%fused_computation.141 | loop fusion | flops 1048576 | bytes 1572864 | tf_op jit(solution)/shard_map/convert_element_type | solution.py:109
  2.8 3.8 %collective-permute-start = (bf16[127,1024]{1,0:T(8,128)(2,1)}, bf16[127,1024]{1,0:T(8,128)(2,1)S(1)}, u32[]{:S(2)}, u32[]{:S(2)}) collective-permute-start(bf16[127,1024]{1,0:T(8,128)(2,1)} %slice.176), channel_id=1, source_target_pairs={{0,8},{8,16},{16,24},{24,32},{32,40},{40,48},{48,56},{56,64},{64,7... | collective-permute-start | bytes 780296 | tf_op jit(solution)/shard_map/ppermute | solution.py:17
  6.6 7.5 %collective-permute-start.2 = (bf16[256,1024]{1,0:T(8,128)(2,1)}, bf16[256,1024]{1,0:T(8,128)(2,1)}, u32[]{:S(2)}, u32[]{:S(2)}) collective-permute-start(bf16[256,1024]{1,0:T(8,128)(2,1)} %param.16), channel_id=1, source_target_pairs={{16,0},{24,8},{32,16},{40,24},{48,32},{56,40},{64,48},{72,56},{80,... | collective-permute-start | bytes 1572872 | tf_op jit(solution)/shard_map/ppermute | solution.py:17
  14.1 2.3 %pad_maximum_fusion = bf16[2,256,1024]{2,1,0:T(8,128)(2,1)} fusion(bf16[1,256,1024]{2,1,0:T(8,128)(2,1)} %bitcast.185, bf16[1,256,1024]{2,1,0:T(8,128)(2,1)} %bitcast.186), kind=kLoop, calls=%fused_computation.135 | loop fusion | flops 524288 | bytes 2097152 | tf_op jit(solution)/shard_map/stack | solution.py:113
  16.4 1.9 %collective-permute-start.1 = (bf16[2,256,1024]{2,1,0:T(8,128)(2,1)}, bf16[2,256,1024]{2,1,0:T(8,128)(2,1)S(1)}, u32[]{:S(2)}, u32[]{:S(2)}) collective-permute-start(bf16[2,256,1024]{2,1,0:T(8,128)(2,1)} %pad_maximum_fusion), channel_id=1, source_target_pairs={{0,8},{8,16},{16,24},{24,32},{32,40},{40,48},{48,56},{56,64},{64,7... | collective-permute-start | bytes 3145736 | tf_op jit(solution)/shard_map/ppermute | solution.py:17
  19.1 4.7 %copy.60 = f32[8,8,128,256]{3,1,2,0:T(8,128)S(1)} copy(f32[8,8,128,256]{3,2,1,0:T(8,128)S(1)} %bitcast.187) | data formatting | bytes 16777216
  23.9 3.7 %slice.215 = f32[64,32640]{1,0:T(8,128)} slice(f32[64,32768]{1,0:T(8,128)S(1)} %bitcast.188), slice={[0:64], [0:32640]} | slice | bytes 16711680 | tf_op jit(solution)/shard_map/slice | solution.py:40
  27.6 16.0 %reshape.128 = f32[64,128,255]{2,1,0:T(8,128)} reshape(f32[64,32640]{1,0:T(8,128)} %slice.215) | data formatting | bytes 16711680 | tf_op jit(solution)/shard_map/reshape | solution.py:40
  48.4 1.1 fusion.258
  63.7 1.4 %fusion.93 = (f32[256]{0:T(256)}, f32[256]{0:T(256)}, f32[256]{0:T(256)}, f32[256]{0:T(256)}, f32[256]{0:T(256)}, /*index=5*/f32[256]{0:T(256)}, f32[256]{0:T(256)}, f32[256]{0:T(256)}) fusion(f32[256,512]{0,1:T(8,128)S(1)} %get-tuple-element.58, f32[256]{0:T(256)S(1)} %get-tuple-element.57, s32[256]{0:T(256)S(1)} %get-tuple-element.31, ...), kind=kLoop, calls=%fused_computation.177 | loop fusion | flops 3536896 | bytes 4214784 | tf_op jit(solution)/shard_map/reduce_sum | solution.py:71
  68.0 1.9 %collective-permute-start.3 = (f32[256,8]{0,1:T(8,128)S(1)}, f32[256,8]{0,1:T(8,128)S(1)}, u32[]{:S(2)}, u32[]{:S(2)}) collective-permute-start(f32[256,8]{0,1:T(8,128)S(1)} %concatenate.30), channel_id=1, source_target_pairs={{0,16},{8,24},{16,32},{24,40},{32,48},{40,56},{48,64},{56,72},{64,... | collective-permute-start | bytes 24584 | tf_op jit(solution)/shard_map/ppermute | solution.py:17
  69.9 5.9 %collective-permute-start.4 = (f32[256,8]{0,1:T(8,128)}, f32[256,8]{0,1:T(8,128)S(1)}, u32[]{:S(2)}, u32[]{:S(2)}) collective-permute-start(f32[256,8]{0,1:T(8,128)} %concatenate.29), channel_id=1, source_target_pairs={{0,16},{8,24},{16,32},{24,40},{32,48},{40,56},{48,64},{56,72},{64,... | collective-permute-start | bytes 24584 | tf_op jit(solution)/shard_map/ppermute | solution.py:17
  75.8 2.0 %fusion.263 = (f32[256]{0:T(256)S(1)}, f32[256,512]{0,1:T(8,128)}) fusion(bf16[512,128]{1,0:T(8,128)(2,1)} %copy-done.12, bf16[256,1024]{1,0:T(8,128)(2,1)} %param.16, s32[256]{0:T(256)S(1)} %get-tuple-element.30, s32[256]{0:T(256)S(1)} %iota_add_fusion.1, s32[512]{0:T(512)S(1)} %iota_add_fusion), kind=kOutput, calls=%fused_computation.316 | convolution fusion | flops 34340608 | bytes 726016 | tf_op jit(solution)/shard_map/dot_general | solution.py:63
  79.0 1.2 copy.39
  80.2 3.2 %collective-permute-start.5 = (bf16[256,8,128]{2,0,1:T(8,128)(2,1)}, bf16[256,8,128]{2,0,1:T(8,128)(2,1)}, u32[]{:S(2)}, u32[]{:S(2)}) collective-permute-start(bf16[256,8,128]{2,0,1:T(8,128)(2,1)} %copy-done.14), channel_id=1, source_target_pairs={{0,16},{8,24},{16,32},{24,40},{32,48},{40,56},{48,64},{56,72},{64,... | collective-permute-start | bytes 1572872 | tf_op jit(solution)/shard_map/ppermute | solution.py:17
  83.4 7.0 %fusion = f32[64,16,128]{2,1,0:T(8,128)S(1)} fusion(bf16[255,64,16]{0,2,1:T(8,128)(2,1)S(1)} %bitcast.191, pred[128,255]{1,0:T(8,128)(4,1)S(1)} %get-tuple-element.42, f32[64,128,255]{2,1,0:T(8,128)} %reshape.128), kind=kOutput, calls=%fused_computation.1 | convolution fusion | flops 77291520 | bytes 9435008 | tf_op jit(solution)/shard_map/dot_general | solution.py:54
  90.4 5.4 %fusion.51 = f32[64,16,128]{2,1,0:T(8,128)} fusion(f32[64,16,128]{2,1,0:T(8,128)S(1)} %fusion, bf16[255,64,16]{0,2,1:T(8,128)(2,1)S(1)} %bitcast.192, pred[128,255]{1,0:T(8,128)(4,1)S(1)} %get-tuple-element.42, f32[64,128,255]{2,1,0:T(8,128)} %reshape.128), kind=kOutput, calls=%fused_computation.94 | convolution fusion | flops 71155712 | bytes 9959296 | tf_op jit(solution)/shard_map/dot_general | solution.py:53
  95.8 2.1 %copy.41 = f32[128,1024]{1,0:T(8,128)} copy(f32[128,1024]{0,1:T(8,128)} %bitcast.194) | data formatting | bytes 1048576 | tf_op jit(solution)/shard_map/reshape | solution.py:57
  97.9 7.0 %fusion.4 = f32[64,16,128]{2,1,0:T(8,128)S(1)} fusion(bf16[255,64,16]{0,2,1:T(8,128)(2,1)S(1)} %bitcast.189, pred[128,255]{1,0:T(8,128)(4,1)S(1)} %get-tuple-element.41, f32[64,128,255]{2,1,0:T(8,128)} %reshape.128), kind=kOutput, calls=%fused_computation.5 | convolution fusion | flops 77291520 | bytes 9435008 | tf_op jit(solution)/shard_map/dot_general | solution.py:54
  104.8 4.6 %fusion.48 = f32[64,16,128]{2,1,0:T(8,128)S(1)} fusion(f32[64,16,128]{2,1,0:T(8,128)S(1)} %fusion.4, bf16[255,64,16]{0,2,1:T(8,128)(2,1)S(1)} %bitcast.190, pred[128,255]{1,0:T(8,128)(4,1)S(1)} %get-tuple-element.41, f32[64,128,255]{2,1,0:T(8,128)} %reshape.128), kind=kOutput, calls=%fused_computation.93 | convolution fusion | flops 71155712 | bytes 9959296 | tf_op jit(solution)/shard_map/dot_general | solution.py:53
  110.4 1.9 %multiply_reduce_fusion = f32[256]{0:T(256)S(1)} fusion(f32[128,1024]{1,0:T(8,128)} %copy.41, f32[128,1024]{1,0:T(8,128)} %copy.40, bf16[256,1024]{1,0:T(8,128)(2,1)} %param.11, bf16[256,1024]{1,0:T(8,128)(2,1)} %param.10), kind=kLoop, calls=%fused_computation.140 | loop fusion | flops 1834752 | bytes 2098176 | tf_op jit(solution)/shard_map/reduce_sum | solution.py:131
  112.3 12.9 %psum.7 = f32[256]{0:T(256)S(1)} all-reduce(f32[256]{0:T(256)S(1)} %multiply_reduce_fusion), channel_id=1, replica_groups=mesh['ctx'=32,'tp'=8] {'tp'}, use_global_device_ids=true, to_apply=%region_20.21 | all-reduce | flops 256 | bytes 2048 | tf_op jit(solution)/shard_map/psum | solution.py:132
  125.6 2.6 %multiply_convert_fusion = bf16[256,1024]{1,0:T(8,128)(2,1)} fusion(f32[1024]{0:T(1024)S(1)} %copy-done.15, f32[256]{0:T(256)S(1)} %add_rsqrt_fusion, f32[128,1024]{1,0:T(8,128)} %copy.41, f32[128,1024]{1,0:T(8,128)} %copy.40, bf16[256,1024]{1,0:T(8,128)(2,1)} %param.11, bf16[256,1024]{1,0:T(8,128)(2,1)} %param.10), kind=kLoop, calls=%fused_computation.139 | loop fusion | flops 2097152 | bytes 2626560 | tf_op jit(solution)/shard_map/convert_element_type | solution.py:133
  133.1 2.1 %divide_convert_fusion = bf16[256,8,128]{2,0,1:T(8,128)(2,1)S(1)} fusion(bf16[256,8,128]{2,0,1:T(8,128)(2,1)} %collective-permute-done.5, f32[256,8,128]{2,0,1:T(8,128)} %copy-done.7, f32[256,8]{0,1:T(8,128)S(1)} %get-tuple-element.32, f32[256,8]{0,1:T(8,128)S(1)} %get-tuple-element.34, f32[256,8]{0,1:T(8,128)S(1)} %get-tuple-element.33), kind=kLoop, calls=%fused_computation.138 | loop fusion | flops 1572864 | bytes 2121728 | tf_op jit(solution)/shard_map/convert_element_type | solution.py:144
  (96 shorter events, 31.7 us)
Async XLA Ops:
  0.6 17.7 %copy-start.13 = (f32[64,128]{1,0:T(8,128)S(1)}, f32[64,128]{1,0:T(8,128)}, u32[]{:S(2)}) copy-start(f32[64,128]{1,0:T(8,128)} %param.14) | copy-start | bytes 98308
  2.8 75.0 %collective-permute-start = (bf16[127,1024]{1,0:T(8,128)(2,1)}, bf16[127,1024]{1,0:T(8,128)(2,1)S(1)}, u32[]{:S(2)}, u32[]{:S(2)}) collective-permute-start(bf16[127,1024]{1,0:T(8,128)(2,1)} %slice.176), channel_id=1, source_target_pairs={{0,8},{8,16},{16,24},{24,32},{32,40},{40,48},{48,56},{56,64},{64,7... | collective-permute-start | bytes 780296 | tf_op jit(solution)/shard_map/ppermute | solution.py:17
  6.6 45.1 %collective-permute-start.2 = (bf16[256,1024]{1,0:T(8,128)(2,1)}, bf16[256,1024]{1,0:T(8,128)(2,1)}, u32[]{:S(2)}, u32[]{:S(2)}) collective-permute-start(bf16[256,1024]{1,0:T(8,128)(2,1)} %param.16), channel_id=1, source_target_pairs={{16,0},{24,8},{32,16},{40,24},{48,32},{56,40},{64,48},{72,56},{80,... | collective-permute-start | bytes 1572872 | tf_op jit(solution)/shard_map/ppermute | solution.py:17
  16.4 28.5 %collective-permute-start.1 = (bf16[2,256,1024]{2,1,0:T(8,128)(2,1)}, bf16[2,256,1024]{2,1,0:T(8,128)(2,1)S(1)}, u32[]{:S(2)}, u32[]{:S(2)}) collective-permute-start(bf16[2,256,1024]{2,1,0:T(8,128)(2,1)} %pad_maximum_fusion), channel_id=1, source_target_pairs={{0,8},{8,16},{16,24},{24,32},{32,40},{40,48},{48,56},{56,64},{64,7... | collective-permute-start | bytes 3145736 | tf_op jit(solution)/shard_map/ppermute | solution.py:17
  27.6 16.0 %copy-start.16 = (s32[32]{0:T(128)S(1)}, s32[32]{0:T(128)}, u32[]{:S(2)}) copy-start(s32[32]{0:T(128)} %param.19) | copy-start | bytes 388
  27.6 17.4 %copy-start.1 = (bf16[256,1024]{1,0:T(8,128)(2,1)S(1)}, bf16[256,1024]{1,0:T(8,128)(2,1)}, u32[]{:S(2)}) copy-start(bf16[256,1024]{1,0:T(8,128)(2,1)} %param.17) | copy-start | bytes 1572868
  43.6 3.7 %copy-start.9 = (bf16[256,1024]{1,0:T(8,128)(2,1)S(1)}, bf16[256,1024]{1,0:T(8,128)(2,1)}, u32[]{:S(2)}) copy-start(bf16[256,1024]{1,0:T(8,128)(2,1)} %param.16) | copy-start | bytes 1572868
  44.0 5.6 %copy-start = (bf16[256,1024]{1,0:T(8,128)(2,1)S(1)}, bf16[256,1024]{1,0:T(8,128)(2,1)}, u32[]{:S(2)}) copy-start(bf16[256,1024]{1,0:T(8,128)(2,1)} %param.18) | copy-start | bytes 1572868
  49.6 13.0 %copy-start.12 = (bf16[512,128]{1,0:T(8,128)(2,1)}, bf16[512,128]{1,0:T(8,128)(2,1)S(1)}, u32[]{:S(2)}) copy-start(bf16[512,128]{1,0:T(8,128)(2,1)S(1)} %get-tuple-element.76) | copy-start | bytes 393220
  49.6 15.5 %copy-start.10 = (bf16[512,128]{1,0:T(8,128)(2,1)}, bf16[512,128]{1,0:T(8,128)(2,1)S(1)}, u32[]{:S(2)}) copy-start(bf16[512,128]{1,0:T(8,128)(2,1)S(1)} %get-tuple-element.75) | copy-start | bytes 393220
  65.5 1.1 copy-start.14
  68.0 65.1 %collective-permute-start.3 = (f32[256,8]{0,1:T(8,128)S(1)}, f32[256,8]{0,1:T(8,128)S(1)}, u32[]{:S(2)}, u32[]{:S(2)}) collective-permute-start(f32[256,8]{0,1:T(8,128)S(1)} %concatenate.30), channel_id=1, source_target_pairs={{0,16},{8,24},{16,32},{24,40},{32,48},{40,56},{48,64},{56,72},{64,... | collective-permute-start | bytes 24584 | tf_op jit(solution)/shard_map/ppermute | solution.py:17
  69.9 63.2 %collective-permute-start.4 = (f32[256,8]{0,1:T(8,128)}, f32[256,8]{0,1:T(8,128)S(1)}, u32[]{:S(2)}, u32[]{:S(2)}) collective-permute-start(f32[256,8]{0,1:T(8,128)} %concatenate.29), channel_id=1, source_target_pairs={{0,16},{8,24},{16,32},{24,40},{32,48},{40,56},{48,64},{56,72},{64,... | collective-permute-start | bytes 24584 | tf_op jit(solution)/shard_map/ppermute | solution.py:17
  80.2 52.9 %collective-permute-start.5 = (bf16[256,8,128]{2,0,1:T(8,128)(2,1)}, bf16[256,8,128]{2,0,1:T(8,128)(2,1)}, u32[]{:S(2)}, u32[]{:S(2)}) collective-permute-start(bf16[256,8,128]{2,0,1:T(8,128)(2,1)} %copy-done.14), channel_id=1, source_target_pairs={{0,16},{8,24},{16,32},{24,40},{32,48},{40,56},{48,64},{56,72},{64,... | collective-permute-start | bytes 1572872 | tf_op jit(solution)/shard_map/ppermute | solution.py:17
  109.4 16.2 %copy-start.15 = (f32[1024]{0:T(1024)S(1)}, f32[1024]{0:T(1024)}, u32[]{:S(2)}) copy-start(f32[1024]{0:T(1024)} %param.15) | copy-start | bytes 12292
  109.4 18.8 %copy-start.2 = (f32[256,512]{0,1:T(8,128)S(1)}, f32[256,512]{0,1:T(8,128)}, u32[]{:S(2)}) copy-start(f32[256,512]{0,1:T(8,128)} %get-tuple-element.62) | copy-start | bytes 1572868
  110.4 18.2 %copy-start.3 = (f32[256,512]{0,1:T(8,128)S(1)}, f32[256,512]{0,1:T(8,128)}, u32[]{:S(2)}) copy-start(f32[256,512]{0,1:T(8,128)} %get-tuple-element.64) | copy-start | bytes 1572868
  125.2 3.9 %copy-start.4 = (f32[256,512]{0,1:T(8,128)S(1)}, f32[256,512]{0,1:T(8,128)}, u32[]{:S(2)}) copy-start(f32[256,512]{0,1:T(8,128)} %get-tuple-element.66) | copy-start | bytes 1572868
  125.6 3.9 %copy-start.5 = (f32[256,512]{0,1:T(8,128)S(1)}, f32[256,512]{0,1:T(8,128)}, u32[]{:S(2)}) copy-start(f32[256,512]{0,1:T(8,128)} %get-tuple-element.68) | copy-start | bytes 1572868
  125.6 4.3 %copy-start.6 = (f32[256,512]{0,1:T(8,128)S(1)}, f32[256,512]{0,1:T(8,128)}, u32[]{:S(2)}) copy-start(f32[256,512]{0,1:T(8,128)} %get-tuple-element.70) | copy-start | bytes 1572868
  128.2 2.1 %copy-start.8 = (f32[256,512]{0,1:T(8,128)S(1)}, f32[256,512]{0,1:T(8,128)}, u32[]{:S(2)}) copy-start(f32[256,512]{0,1:T(8,128)} %get-tuple-element.74) | copy-start | bytes 1572868
  129.9 1.7 %copy-start.11 = (bf16[512,128]{1,0:T(8,128)(2,1)S(1)}, bf16[512,128]{1,0:T(8,128)(2,1)}, u32[]{:S(2)}) copy-start(bf16[512,128]{1,0:T(8,128)(2,1)} %copy-done.10) | copy-start | bytes 393220
  132.0 1.0 copy-start.7

commit v3 on v2

--- a/solution.py
+++ b/solution.py
@@ -1,6 +1,8 @@
 import jax
 import jax.numpy as jnp
 from jax import lax
+from jax.experimental import pallas as pl
+from jax.experimental.pallas import tpu as pltpu
 from jax.sharding import PartitionSpec as P
 
 D = 8192
@@ -25,27 +27,49 @@
     return jnp.max(jnp.where(starts[None, :] <= positions[:, None], starts[None, :], 0), axis=1)
 
 
+def toeplitz_rows(reversed_ref, out_ref):
+    rows = out_ref.shape[1]
+    for group in range(out_ref.shape[0]):
+        line = jnp.broadcast_to(reversed_ref[group : group + 1, :], (rows, reversed_ref.shape[1]))
+        out_ref[group] = pltpu.roll(line, 0, 1, stride=1, stride_axis=0)
+
+
+def build_toeplitz(filter_taps):
+    groups, taps = filter_taps.shape
+    span = 2 * taps
+    reversed_taps = jnp.concatenate(
+        [filter_taps[:, ::-1], jnp.zeros((groups, span - taps), jnp.float32)], axis=1
+    )
+    step = 8
+    return pl.pallas_call(
+        toeplitz_rows,
+        grid=(groups // step,),
+        in_specs=[pl.BlockSpec((step, span), lambda i: (i, 0))],
+        out_specs=pl.BlockSpec((step, taps, span), lambda i: (i, 0, 0)),
+        out_shape=jax.ShapeDtypeStruct((groups, taps, span), jnp.float32),
+    )(reversed_taps)
+
+
 def causal_filter(extended, filter_taps, reach_back, out_rows):
     groups, taps = filter_taps.shape
     channels = extended.shape[1]
     width = channels // groups
+    span = 2 * taps
     lag_table = (
         jnp.arange(taps, dtype=jnp.int32)[:, None]
         + (taps - 1)
-        - jnp.arange(2 * taps - 1, dtype=jnp.int32)[None, :]
-    )
-    reversed_taps = filter_taps[:, ::-1]
-    period = jnp.concatenate([reversed_taps, jnp.zeros((groups, taps), jnp.float32)], axis=1)
-    tiled = jnp.tile(period, (1, taps))
-    toeplitz = tiled[:, : taps * (2 * taps - 1)].reshape(groups, taps, 2 * taps - 1)
+        - jnp.arange(span, dtype=jnp.int32)[None, :]
+    )
+    toeplitz = build_toeplitz(filter_taps)
     upper_part = toeplitz.astype(jnp.bfloat16)
     lower_part = (toeplitz - upper_part.astype(jnp.float32)).astype(jnp.bfloat16)
     zero_half = jnp.zeros((), jnp.bfloat16)
     numbers = (((0,), (2,)), ((1,), (0,)))
+    extended = jnp.concatenate([extended, jnp.zeros((1, channels), extended.dtype)], axis=0)
     results = []
     for block_index in range(out_rows // taps):
         first = block_index * taps
-        sources = extended[first : first + 2 * taps - 1].reshape(2 * taps - 1, groups, width)
+        sources = extended[first : first + span].reshape(span, groups, width)
         limits = reach_back[first : first + taps]
         valid = (lag_table <= limits[:, None])[None]
         kernel_upper = jnp.where(valid, upper_part, zero_half)
@@ -56,6 +80,15 @@
         )
         results.append(result.transpose(2, 0, 1).reshape(taps, channels))
     return jnp.concatenate(results, axis=0)
+
+
+def tp_sum(value):
+    count = lax.axis_size("tp")
+    stride = 1
+    while stride < count:
+        value = value + lax.ppermute(value, "tp", [(i, i ^ stride) for i in range(count)])
+        stride *= 2
+    return value
 
 
 def attend_part(query_head, key_head, value_head, visible, scale):
@@ -118,21 +151,23 @@
     window = key_rows.shape[0]
     key_pos = anchor - tok_rows + jnp.arange(window, dtype=jnp.int32)
     scale = jnp.float32(1.0 / HEAD_DIM**0.5)
+    extended = jnp.concatenate([rim_rows, mixed_rows], axis=0)
+    filtered = causal_filter(extended, filter_taps, positions - doc_begin, tok_rows)
+    hidden = residual.astype(jnp.float32) + hyena_gate.astype(jnp.float32) * filtered
+    local_sum = jnp.sum(hidden * hidden, axis=1)
+    local_sum, later_query = lax.optimization_barrier((local_sum, later_query))
+    mean_square = tp_sum(local_sum) / D
+    normed = (hidden * lax.rsqrt(mean_square + norm_epsilon)[:, None] * norm_gain[None, :]).astype(
+        jnp.bfloat16
+    )
     far_pos = positions + 2 * tok_rows
     far_begin = document_begin(doc_lengths, far_pos)
     far_visible = (key_pos[None, :] <= far_pos[:, None]) & (key_pos[None, :] >= far_begin[:, None])
     far_sum, far_top, far_den = attend_block(later_query, key_rows, value_rows, far_visible, scale)
-    far_packet = (far_sum.astype(jnp.bfloat16), far_top, far_den)
-    far_packet, mixed_rows = lax.optimization_barrier((far_packet, mixed_rows))
-    far_sum, far_top, far_den = shifted(far_packet, "ctx", 2)
-    extended = jnp.concatenate([rim_rows, mixed_rows], axis=0)
-    filtered = causal_filter(extended, filter_taps, positions - doc_begin, tok_rows)
-    hidden = residual.astype(jnp.float32) + hyena_gate.astype(jnp.float32) * filtered
-    local_sum = jnp.sum(hidden * hidden, axis=1)
-    mean_square = lax.psum(local_sum, "tp") / D
-    normed = (hidden * lax.rsqrt(mean_square + norm_epsilon)[:, None] * norm_gain[None, :]).astype(
-        jnp.bfloat16
-    )
+    far_stats = jnp.concatenate([far_top, far_den], axis=1)
+    far_sum, far_stats = shifted((far_sum.astype(jnp.bfloat16), far_stats), "ctx", 2)
+    head_count = far_top.shape[1]
+    far_top, far_den = far_stats[:, :head_count], far_stats[:, head_count:]
     visible = (key_pos[None, :] <= positions[:, None]) & (key_pos[None, :] >= doc_begin[:, None])
     near_sum, near_top, near_den = attend_block(att_query, key_rows, value_rows, visible, scale)
     far_top = jnp.where(far_den > 0, far_top, jnp.float32(-1e30))

time: 138 us -> 122 us (0.88)
  the two profiles are of different devices: /device:TPU:24 before, /device:TPU:62 now
where the time goes in v3:
time: 122 us; the launch traced here: 120 us
  matrix products  48.8 us (40%)
  waiting for transfers between devices  25.7 us (21%)
  starting transfers between devices  23.1 us (19%)
  other arithmetic  8.89 us (7%)
  Pallas kernels  6.74 us (6%)
  local copies, waits for them, and re-layouts  6.13 us (5%)
    ppermute x5, starting transfers between devices, shifted(): lax.ppermute(value, axis, [(source, source + steps) for source in range(f...  20.8 us
    ppermute x5, waiting for transfers between devices, shifted(): lax.ppermute(value, axis, [(source, source + steps) for source in range(f...  18.1 us
    dot_general x16, matrix products, attend_part(): lax.dot_general(query_head, key_head, (((1,), (1,)), ((), ())), preferred...  15.5 us
    dot_general x2, matrix products, causal_filter(): lax.dot_general(sources, kernel_lower, numbers, preferred_element_type=jn...  14.1 us
    dot_general x16, matrix products, attend_part(): jnp.dot(expo.astype(jnp.bfloat16), value_head, preferred_element_type=jnp...  13.3 us
    ppermute x3, waiting for transfers between devices, tp_sum(): lax.ppermute(value, 'tp', [(i, i ^ stride) for i in range(count)])  7.56 us
    pallas_call x1, Pallas kernels, build_toeplitz(): pl.pallas_call(toeplitz_rows, grid=(groups // step,), in_specs=[pl.BlockS...  6.74 us
    dot_general x2, matrix products, causal_filter(): lax.dot_general(sources, kernel_upper, numbers, preferred_element_type=jn...  5.87 us
  transfers between devices with their start and end apart: 8, of which 4 were waited for; matrix products, arithmetic and copies ran while one was open for 32% of the time, Pallas kernels for 6%

profile of v3, /device:TPU:62, one launch (start us, length us, event | category | flops | bytes accessed | tf_op | source)
XLA Modules:
  0.0 120.5 jit_solution(4985888289857626589)
XLA Ops:
  0.7 1.4 %multiply_convert_fusion.1 = bf16[256,1024]{1,0:T(8,128)(2,1)S(1)} fusion(bf16[256,1024]{1,0:T(8,128)(2,1)} %param.13, bf16[256,1024]{1,0:T(8,128)(2,1)} %param.12), kind=kLoop, calls=%fused_computation.133 | loop fusion | flops 1048576 | bytes 1572864 | tf_op jit(solution)/shard_map/convert_element_type | solution.py:142
  2.1 3.8 %collective-permute-start = (bf16[127,1024]{1,0:T(8,128)(2,1)S(1)}, bf16[127,1024]{1,0:T(8,128)(2,1)S(1)}, u32[]{:S(2)}, u32[]{:S(2)}) collective-permute-start(bf16[127,1024]{1,0:T(8,128)(2,1)S(1)} %slice.181), channel_id=1, source_target_pairs={{0,8},{8,16},{16,24},{24,32},{32,40},{40,48},{48,56},{56,64},{64,7... | collective-permute-start | bytes 780296 | tf_op jit(solution)/shard_map/ppermute | solution.py:19
  6.0 5.6 %collective-permute-start.1 = (bf16[256,1024]{1,0:T(8,128)(2,1)}, bf16[256,1024]{1,0:T(8,128)(2,1)}, u32[]{:S(2)}, u32[]{:S(2)}) collective-permute-start(bf16[256,1024]{1,0:T(8,128)(2,1)} %param.16), channel_id=1, source_target_pairs={{16,0},{24,8},{32,16},{40,24},{48,32},{56,40},{64,48},{72,56},{80,... | collective-permute-start | bytes 1572872 | tf_op jit(solution)/shard_map/ppermute | solution.py:19
  11.6 2.4 %pad_maximum_fusion = bf16[2,256,1024]{2,1,0:T(8,128)(2,1)} fusion(bf16[1,256,1024]{2,1,0:T(8,128)(2,1)} %bitcast.151, bf16[1,256,1024]{2,1,0:T(8,128)(2,1)} %bitcast.152), kind=kLoop, calls=%fused_computation.129 | loop fusion | flops 524288 | bytes 2097152 | tf_op jit(solution)/shard_map/stack | solution.py:146
  13.9 1.9 %collective-permute-start.5 = (bf16[2,256,1024]{2,1,0:T(8,128)(2,1)}, bf16[2,256,1024]{2,1,0:T(8,128)(2,1)}, u32[]{:S(2)}, u32[]{:S(2)}) collective-permute-start(bf16[2,256,1024]{2,1,0:T(8,128)(2,1)} %pad_maximum_fusion), channel_id=1, source_target_pairs={{0,8},{8,16},{16,24},{24,32},{32,40},{40,48},{48,56},{56,64},{64,7... | collective-permute-start | bytes 3145736 | tf_op jit(solution)/shard_map/ppermute | solution.py:19
  16.8 6.7 %shard_map.113 = f32[64,128,256]{2,1,0:T(8,128)} custom-call(f32[64,256]{1,0:T(8,128)} %concatenate.30.reversed_ref), custom_call_target="tpu_custom_call" | custom-call | tf_op jit(solution)/shard_map/pallas_call | solution.py:44
  24.1 7.1 %fusion.4 = f32[64,16,128]{2,1,0:T(8,128)S(1)} fusion(bf16[256,64,16]{0,2,1:T(8,128)(2,1)S(1)} %bitcast.155, pred[128,256]{1,0:T(8,128)(4,1)S(1)} %get-tuple-element.37, f32[64,128,256]{2,1,0:T(8,128)} %shard_map.113), kind=kOutput, calls=%fused_computation.5 | convolution fusion | flops 77594624 | bytes 9469952 | tf_op jit(solution)/shard_map/dot_general | solution.py:78
  32.3 1.2 fusion.40
  33.9 7.0 %fusion = f32[64,16,128]{2,1,0:T(8,128)S(1)} fusion(bf16[256,64,16]{0,2,1:T(8,128)(2,1)S(1)} %bitcast.153, pred[128,256]{1,0:T(8,128)(4,1)S(1)} %get-tuple-element.38, f32[64,128,256]{2,1,0:T(8,128)} %shard_map.113), kind=kOutput, calls=%fused_computation.1 | convolution fusion | flops 77594624 | bytes 9469952 | tf_op jit(solution)/shard_map/dot_general | solution.py:78
  40.9 4.7 %fusion.43 = f32[64,16,128]{2,1,0:T(8,128)S(1)} fusion(f32[64,16,128]{2,1,0:T(8,128)S(1)} %fusion, bf16[256,64,16]{0,2,1:T(8,128)(2,1)S(1)} %bitcast.154, pred[128,256]{1,0:T(8,128)(4,1)S(1)} %get-tuple-element.38, f32[64,128,256]{2,1,0:T(8,128)} %shard_map.113), kind=kOutput, calls=%fused_computation.86 | convolution fusion | flops 71434240 | bytes 9994240 | tf_op jit(solution)/shard_map/dot_general | solution.py:77
  48.2 2.7 %collective-permute-done.3 = f32[256]{0:T(256)S(1)} collective-permute-done((f32[256]{0:T(256)S(1)}, f32[256]{0:T(256)S(1)}, u32[]{:S(2)}, u32[]{:S(2)}) %collective-permute-start.3) | collective-permute-done | bytes 1056 | tf_op jit(solution)/shard_map/ppermute | solution.py:89
  50.9 1.4 %collective-permute-start.4 = (f32[256]{0:T(256)S(1)}, f32[256]{0:T(256)S(1)}, u32[]{:S(2)}, u32[]{:S(2)}) collective-permute-start(f32[256]{0:T(256)S(1)} %add.99), channel_id=1, source_target_pairs={{0,4},{1,5},{2,6},{3,7},{4,0},{5,1},{6,2},{7,3},{8,12},{9,13},{10,... | collective-permute-start | bytes 3080 | tf_op jit(solution)/shard_map/ppermute | solution.py:89
  52.3 3.7 %collective-permute-done.4 = f32[256]{0:T(256)S(1)} collective-permute-done((f32[256]{0:T(256)S(1)}, f32[256]{0:T(256)S(1)}, u32[]{:S(2)}, u32[]{:S(2)}) %collective-permute-start.4) | collective-permute-done | bytes 1056 | tf_op jit(solution)/shard_map/ppermute | solution.py:89
  57.0 1.3 %slice_bitcast_fusion = (bf16[256,1024]{1,0:T(8,128)(2,1)S(1)}, bf16[256,1024]{1,0:T(8,128)(2,1)S(1)}) fusion(bf16[2,256,1024]{2,1,0:T(8,128)(2,1)} %collective-permute-done.5), kind=kLoop, calls=%fused_computation.135 | loop fusion | bytes 2097152 | tf_op jit(solution)/shard_map/squeeze | solution.py:150
  61.8 1.2 %fusion.243 = (f32[256]{0:T(256)S(1)}, f32[256,512]{0,1:T(8,128)S(1)}) fusion(bf16[256,1024]{1,0:T(8,128)(2,1)S(1)} %get-tuple-element.32, bf16[256,1024]{1,0:T(8,128)(2,1)S(1)} %copy-done.2, bf16[256,1024]{1,0:T(8,128)(2,1)} %collective-permute-done.1, s32[256]{0:T(256)S(1)} %get-tuple-element.26, s32[256]{0:T(256)S(1)} %get-tuple-element.72, ...), kind=kOutput, calls=%fused_computation.297 | convolution fusion | flops 34602752 | bytes 1643520 | tf_op jit(solution)/shard_map/dot_general | solution.py:96
  65.4 1.2 fusion.246
  66.6 1.2 fusion.247
  75.8 4.4 %collective-permute-start.6 = (f32[256,16]{0,1:T(8,128)S(1)}, f32[256,16]{0,1:T(8,128)S(1)}, u32[]{:S(2)}, u32[]{:S(2)}) collective-permute-start(f32[256,16]{0,1:T(8,128)S(1)} %concatenate.36), channel_id=1, source_target_pairs={{0,16},{8,24},{16,32},{24,40},{32,48},{40,56},{48,64},{56,72},{64,... | collective-permute-start | bytes 49160 | tf_op jit(solution)/shard_map/ppermute | solution.py:19
  80.3 2.0 %fusion.57 = bf16[256,8,128]{0,2,1:T(8,128)(2,1)} fusion(bf16[256,8,128]{0,2,1:T(8,128)(2,1)} %fusion.55, f32[256,512]{0,1:T(8,128)} %copy-done.15, f32[256]{0:T(256)S(1)} %get-tuple-element.41, bf16[256,1024]{1,0:T(8,128)(2,1)S(1)} %get-tuple-element.31, bf16[256,1024]{1,0:T(8,128)(2,1)S(1)} %copy-done.1, s32[256]{0:T(256)S(1)} %get-tuple-element.26, ...), kind=kOutput, calls=%fused_computation.114 | convolution fusion | flops 34635776 | bytes 1643520 | tf_op jit(solution)/shard_map/dot_general | solution.py:105
  82.3 2.0 %fusion.59 = bf16[256,8,128]{0,2,1:T(8,128)(2,1)} fusion(bf16[256,8,128]{0,2,1:T(8,128)(2,1)} %fusion.57, f32[256,512]{0,1:T(8,128)} %copy-done.14, f32[256]{0:T(256)S(1)} %get-tuple-element.43, bf16[256,1024]{1,0:T(8,128)(2,1)S(1)} %get-tuple-element.31, bf16[256,1024]{1,0:T(8,128)(2,1)S(1)} %copy-done.1, s32[256]{0:T(256)S(1)} %get-tuple-element.26, ...), kind=kOutput, calls=%fused_computation.116 | convolution fusion | flops 34635776 | bytes 1643520 | tf_op jit(solution)/shard_map/dot_general | solution.py:105
  84.3 2.0 %fusion.61 = bf16[256,8,128]{0,2,1:T(8,128)(2,1)} fusion(bf16[256,8,128]{0,2,1:T(8,128)(2,1)} %fusion.59, f32[256,512]{0,1:T(8,128)} %copy-done.13, f32[256]{0:T(256)S(1)} %get-tuple-element.45, bf16[256,1024]{1,0:T(8,128)(2,1)S(1)} %get-tuple-element.31, bf16[256,1024]{1,0:T(8,128)(2,1)S(1)} %copy-done.1, s32[256]{0:T(256)S(1)} %get-tuple-element.26, ...), kind=kOutput, calls=%fused_computation.118 | convolution fusion | flops 34635776 | bytes 1643520 | tf_op jit(solution)/shard_map/dot_general | solution.py:105
  90.1 5.1 %collective-permute-start.7 = (bf16[256,8,128]{0,2,1:T(8,128)(2,1)}, bf16[256,8,128]{0,2,1:T(8,128)(2,1)}, u32[]{:S(2)}, u32[]{:S(2)}) collective-permute-start(bf16[256,8,128]{0,2,1:T(8,128)(2,1)} %fusion.69), channel_id=1, source_target_pairs={{0,16},{8,24},{16,32},{24,40},{32,48},{40,56},{48,64},{56,72},{64,... | collective-permute-start | bytes 1572872 | tf_op jit(solution)/shard_map/ppermute | solution.py:19
  99.8 18.1 %collective-permute-done.7 = bf16[256,8,128]{0,2,1:T(8,128)(2,1)} collective-permute-done((bf16[256,8,128]{0,2,1:T(8,128)(2,1)}, bf16[256,8,128]{0,2,1:T(8,128)(2,1)}, u32[]{:S(2)}, u32[]{:S(2)}) %collective-permute-start.7) | collective-permute-done | bytes 524320 | tf_op jit(solution)/shard_map/ppermute | solution.py:19
  117.9 1.6 %divide_convert_fusion = bf16[256,8,128]{0,2,1:T(8,128)(2,1)S(1)} fusion(bf16[256,8,128]{0,2,1:T(8,128)(2,1)} %collective-permute-done.7, f32[256,8,128]{0,2,1:T(8,128)} %copy-done.18, f32[256,8]{0,1:T(8,128)S(1)} %get-tuple-element.28, f32[256,8]{0,1:T(8,128)S(1)} %get-tuple-element.30, f32[256,8]{0,1:T(8,128)S(1)} %get-tuple-element.29), kind=kLoop, calls=%fused_computation.130 | loop fusion | flops 1572864 | bytes 2121728 | tf_op jit(solution)/shard_map/convert_element_type | solution.py:179
  (115 shorter events, 29.7 us)
Async XLA Ops:
  0.6 15.2 %copy-start.25 = (s32[32]{0:T(128)S(1)}, s32[32]{0:T(128)}, u32[]{:S(2)}) copy-start(s32[32]{0:T(128)} %param.19) | copy-start | bytes 388
  0.6 15.5 %copy-start.23 = (f32[64,128]{1,0:T(8,128)S(1)}, f32[64,128]{1,0:T(8,128)}, u32[]{:S(2)}) copy-start(f32[64,128]{1,0:T(8,128)} %param.14) | copy-start | bytes 98308
  2.1 21.6 %collective-permute-start = (bf16[127,1024]{1,0:T(8,128)(2,1)S(1)}, bf16[127,1024]{1,0:T(8,128)(2,1)S(1)}, u32[]{:S(2)}, u32[]{:S(2)}) collective-permute-start(bf16[127,1024]{1,0:T(8,128)(2,1)S(1)} %slice.181), channel_id=1, source_target_pairs={{0,8},{8,16},{16,24},{24,32},{32,40},{40,48},{48,56},{56,64},{64,7... | collective-permute-start | bytes 780296 | tf_op jit(solution)/shard_map/ppermute | solution.py:19
  6.0 40.1 %collective-permute-start.1 = (bf16[256,1024]{1,0:T(8,128)(2,1)}, bf16[256,1024]{1,0:T(8,128)(2,1)}, u32[]{:S(2)}, u32[]{:S(2)}) collective-permute-start(bf16[256,1024]{1,0:T(8,128)(2,1)} %param.16), channel_id=1, source_target_pairs={{16,0},{24,8},{32,16},{40,24},{48,32},{56,40},{64,48},{72,56},{80,... | collective-permute-start | bytes 1572872 | tf_op jit(solution)/shard_map/ppermute | solution.py:19
  13.9 43.1 %collective-permute-start.5 = (bf16[2,256,1024]{2,1,0:T(8,128)(2,1)}, bf16[2,256,1024]{2,1,0:T(8,128)(2,1)}, u32[]{:S(2)}, u32[]{:S(2)}) collective-permute-start(bf16[2,256,1024]{2,1,0:T(8,128)(2,1)} %pad_maximum_fusion), channel_id=1, source_target_pairs={{0,8},{8,16},{16,24},{24,32},{32,40},{40,48},{48,56},{56,64},{64,7... | collective-permute-start | bytes 3145736 | tf_op jit(solution)/shard_map/ppermute | solution.py:19
  24.1 8.2 %copy-start = (f32[64,128,256]{2,1,0:T(8,128)S(1)}, f32[64,128,256]{2,1,0:T(8,128)}, u32[]{:S(2)}) copy-start(f32[64,128,256]{2,1,0:T(8,128)} %shard_map.113) | copy-start | bytes 25165828
  40.9 15.1 %copy-start.24 = (f32[1024]{0:T(1024)S(1)}, f32[1024]{0:T(1024)}, u32[]{:S(2)}) copy-start(f32[1024]{0:T(1024)} %param.15) | copy-start | bytes 12292
  45.5 12.8 %copy-start.2 = (bf16[256,1024]{1,0:T(8,128)(2,1)S(1)}, bf16[256,1024]{1,0:T(8,128)(2,1)}, u32[]{:S(2)}) copy-start(bf16[256,1024]{1,0:T(8,128)(2,1)} %param.17) | copy-start | bytes 1572868
  46.1 1.2 %collective-permute-start.2 = (f32[256]{0:T(256)S(1)}, f32[256]{0:T(256)S(1)}, u32[]{:S(2)}, u32[]{:S(2)}) collective-permute-start(f32[256]{0:T(256)S(1)} %multiply_reduce_fusion), channel_id=1, source_target_pairs={{0,1},{1,0},{2,3},{3,2},{4,5},{5,4},{6,7},{7,6},{8,9},{9,8},{10,11... | collective-permute-start | bytes 3080 | tf_op jit(solution)/shard_map/ppermute | solution.py:89
  47.3 3.6 %collective-permute-start.3 = (f32[256]{0:T(256)S(1)}, f32[256]{0:T(256)S(1)}, u32[]{:S(2)}, u32[]{:S(2)}) collective-permute-start(f32[256]{0:T(256)S(1)} %add.98), channel_id=1, source_target_pairs={{0,2},{1,3},{2,0},{3,1},{4,6},{5,7},{6,4},{7,5},{8,10},{9,11},{10,... | collective-permute-start | bytes 3080 | tf_op jit(solution)/shard_map/ppermute | solution.py:89
  50.9 5.1 %collective-permute-start.4 = (f32[256]{0:T(256)S(1)}, f32[256]{0:T(256)S(1)}, u32[]{:S(2)}, u32[]{:S(2)}) collective-permute-start(f32[256]{0:T(256)S(1)} %add.99), channel_id=1, source_target_pairs={{0,4},{1,5},{2,6},{3,7},{4,0},{5,1},{6,2},{7,3},{8,12},{9,13},{10,... | collective-permute-start | bytes 3080 | tf_op jit(solution)/shard_map/ppermute | solution.py:89
  60.6 14.3 %copy-start.15 = (f32[256,512]{0,1:T(8,128)}, f32[256,512]{0,1:T(8,128)S(1)}, u32[]{:S(2)}) copy-start(f32[256,512]{0,1:T(8,128)S(1)} %get-tuple-element.42) | copy-start | bytes 1572868
  61.8 13.2 %copy-start.14 = (f32[256,512]{0,1:T(8,128)}, f32[256,512]{0,1:T(8,128)S(1)}, u32[]{:S(2)}) copy-start(f32[256,512]{0,1:T(8,128)S(1)} %get-tuple-element.44) | copy-start | bytes 1572868
  63.0 11.9 %copy-start.13 = (f32[256,512]{0,1:T(8,128)}, f32[256,512]{0,1:T(8,128)S(1)}, u32[]{:S(2)}) copy-start(f32[256,512]{0,1:T(8,128)S(1)} %get-tuple-element.46) | copy-start | bytes 1572868
  64.2 10.7 %copy-start.11 = (f32[256,512]{0,1:T(8,128)}, f32[256,512]{0,1:T(8,128)S(1)}, u32[]{:S(2)}) copy-start(f32[256,512]{0,1:T(8,128)S(1)} %get-tuple-element.48) | copy-start | bytes 1572868
  65.4 9.6 %copy-start.9 = (f32[256,512]{0,1:T(8,128)}, f32[256,512]{0,1:T(8,128)S(1)}, u32[]{:S(2)}) copy-start(f32[256,512]{0,1:T(8,128)S(1)} %get-tuple-element.50) | copy-start | bytes 1572868
  66.5 8.4 %copy-start.7 = (f32[256,512]{0,1:T(8,128)}, f32[256,512]{0,1:T(8,128)S(1)}, u32[]{:S(2)}) copy-start(f32[256,512]{0,1:T(8,128)S(1)} %get-tuple-element.52) | copy-start | bytes 1572868
  75.8 11.5 %copy-start.10 = (f32[256,512]{0,1:T(8,128)S(1)}, f32[256,512]{0,1:T(8,128)}, u32[]{:S(2)}) copy-start(f32[256,512]{0,1:T(8,128)} %copy-done.9) | copy-start | bytes 1572868
  75.8 10.5 %copy-start.12 = (f32[256,512]{0,1:T(8,128)S(1)}, f32[256,512]{0,1:T(8,128)}, u32[]{:S(2)}) copy-start(f32[256,512]{0,1:T(8,128)} %copy-done.11) | copy-start | bytes 1572868
  75.8 12.4 %copy-start.8 = (f32[256,512]{0,1:T(8,128)S(1)}, f32[256,512]{0,1:T(8,128)}, u32[]{:S(2)}) copy-start(f32[256,512]{0,1:T(8,128)} %copy-done.7) | copy-start | bytes 1572868
  75.8 23.9 %collective-permute-start.6 = (f32[256,16]{0,1:T(8,128)S(1)}, f32[256,16]{0,1:T(8,128)S(1)}, u32[]{:S(2)}, u32[]{:S(2)}) collective-permute-start(f32[256,16]{0,1:T(8,128)S(1)} %concatenate.36), channel_id=1, source_target_pairs={{0,16},{8,24},{16,32},{24,40},{32,48},{40,56},{48,64},{56,72},{64,... | collective-permute-start | bytes 49160 | tf_op jit(solution)/shard_map/ppermute | solution.py:19
  88.2 8.0 %copy-start.3 = (f32[256,512]{0,1:T(8,128)S(1)}, f32[256,512]{0,1:T(8,128)}, u32[]{:S(2)}) copy-start(f32[256,512]{0,1:T(8,128)} %get-tuple-element.62) | copy-start | bytes 1572868
  89.1 7.4 %copy-start.4 = (f32[256,512]{0,1:T(8,128)S(1)}, f32[256,512]{0,1:T(8,128)}, u32[]{:S(2)}) copy-start(f32[256,512]{0,1:T(8,128)} %get-tuple-element.64) | copy-start | bytes 1572868
  90.1 27.8 %collective-permute-start.7 = (bf16[256,8,128]{0,2,1:T(8,128)(2,1)}, bf16[256,8,128]{0,2,1:T(8,128)(2,1)}, u32[]{:S(2)}, u32[]{:S(2)}) collective-permute-start(bf16[256,8,128]{0,2,1:T(8,128)(2,1)} %fusion.69), channel_id=1, source_target_pairs={{0,16},{8,24},{16,32},{24,40},{32,48},{40,56},{48,64},{56,72},{64,... | collective-permute-start | bytes 1572872 | tf_op jit(solution)/shard_map/ppermute | solution.py:19
  (10 other events, 40.6 us)

commit v4 on v3

--- a/solution.py
+++ b/solution.py
@@ -91,34 +91,23 @@
     return value
 
 
-def attend_part(query_head, key_head, value_head, visible, scale):
+def attend_block(queries, keys, values, visible, scale):
+    head_count = queries.shape[1] // HEAD_DIM
+    query_heads = queries.reshape(queries.shape[0], head_count, HEAD_DIM)
+    key_heads = keys.reshape(keys.shape[0], head_count, HEAD_DIM)
+    value_heads = values.reshape(values.shape[0], head_count, HEAD_DIM)
     scores = (
-        lax.dot_general(
-            query_head, key_head, (((1,), (1,)), ((), ())), preferred_element_type=jnp.float32
-        )
+        jnp.einsum("qhd,khd->hqk", query_heads, key_heads, preferred_element_type=jnp.float32)
         * scale
     )
-    scores = jnp.where(visible, scores, jnp.float32(-1e30))
-    top = jnp.max(scores, axis=1, keepdims=True)
-    expo = jnp.where(visible, jnp.exp(scores - top), jnp.float32(0.0))
-    denominator = jnp.sum(expo, axis=1, keepdims=True)
-    summed = jnp.dot(expo.astype(jnp.bfloat16), value_head, preferred_element_type=jnp.float32)
-    return summed, top, denominator
-
-
-def attend_block(queries, keys, values, visible, scale):
-    head_count = queries.shape[1] // HEAD_DIM
-    sums, tops, dens = [], [], []
-    for head_index in range(head_count):
-        lower = head_index * HEAD_DIM
-        upper = lower + HEAD_DIM
-        summed, top, den = attend_part(
-            queries[:, lower:upper], keys[:, lower:upper], values[:, lower:upper], visible, scale
-        )
-        sums.append(summed)
-        tops.append(top)
-        dens.append(den)
-    return jnp.stack(sums, axis=1), jnp.concatenate(tops, axis=1), jnp.concatenate(dens, axis=1)
+    scores = jnp.where(visible[None], scores, jnp.float32(-1e30))
+    top = jnp.max(scores, axis=2, keepdims=True)
+    expo = jnp.where(visible[None], jnp.exp(scores - top), jnp.float32(0.0))
+    denominator = jnp.sum(expo, axis=2)
+    summed = jnp.einsum(
+        "hqk,khd->qhd", expo.astype(jnp.bfloat16), value_heads, preferred_element_type=jnp.float32
+    )
+    return summed, top[:, :, 0].T, denominator.T
 
 
 def on_device(
@@ -156,20 +145,22 @@
     hidden = residual.astype(jnp.float32) + hyena_gate.astype(jnp.float32) * filtered
     local_sum = jnp.sum(hidden * hidden, axis=1)
     local_sum, later_query = lax.optimization_barrier((local_sum, later_query))
-    mean_square = tp_sum(local_sum) / D
-    normed = (hidden * lax.rsqrt(mean_square + norm_epsilon)[:, None] * norm_gain[None, :]).astype(
-        jnp.bfloat16
-    )
     far_pos = positions + 2 * tok_rows
     far_begin = document_begin(doc_lengths, far_pos)
     far_visible = (key_pos[None, :] <= far_pos[:, None]) & (key_pos[None, :] >= far_begin[:, None])
     far_sum, far_top, far_den = attend_block(later_query, key_rows, value_rows, far_visible, scale)
     far_stats = jnp.concatenate([far_top, far_den], axis=1)
-    far_sum, far_stats = shifted((far_sum.astype(jnp.bfloat16), far_stats), "ctx", 2)
+    far_packet = (far_sum.astype(jnp.bfloat16), far_stats)
+    far_packet, local_sum, near_query = lax.optimization_barrier((far_packet, local_sum, att_query))
+    far_sum, far_stats = shifted(far_packet, "ctx", 2)
+    mean_square = tp_sum(local_sum) / D
+    normed = (hidden * lax.rsqrt(mean_square + norm_epsilon)[:, None] * norm_gain[None, :]).astype(
+        jnp.bfloat16
+    )
     head_count = far_top.shape[1]
     far_top, far_den = far_stats[:, :head_count], far_stats[:, head_count:]
     visible = (key_pos[None, :] <= positions[:, None]) & (key_pos[None, :] >= doc_begin[:, None])
-    near_sum, near_top, near_den = attend_block(att_query, key_rows, value_rows, visible, scale)
+    near_sum, near_top, near_den = attend_block(near_query, key_rows, value_rows, visible, scale)
     far_top = jnp.where(far_den > 0, far_top, jnp.float32(-1e30))
     top = jnp.maximum(near_top, far_top)
     near_scale = jnp.exp(near_top - top)

time: 122 us -> 95.2 us (0.78)
  the two profiles are of different devices: /device:TPU:62 before, /device:TPU:59 now
where the time goes in v4:
time: 95.2 us; the launch traced here: 94.6 us
  matrix products  26.5 us (28%)
  starting transfers between devices  23.2 us (24%)
  waiting for transfers between devices  19.2 us (20%)
  local copies, waits for them, and re-layouts  10.2 us (11%)
  other arithmetic  7.75 us (8%)
  Pallas kernels  6.73 us (7%)
  between operations  0.96 us (1%)
    ppermute x5, starting transfers between devices, shifted(): lax.ppermute(value, axis, [(source, source + steps) for source in range(f...  19.8 us
    ppermute x5, waiting for transfers between devices, shifted(): lax.ppermute(value, axis, [(source, source + steps) for source in range(f...  17.1 us
    dot_general x2, matrix products, causal_filter(): lax.dot_general(sources, kernel_lower, numbers, preferred_element_type=jn...  14.1 us
    pallas_call x1, Pallas kernels, build_toeplitz(): pl.pallas_call(toeplitz_rows, grid=(groups // step,), in_specs=[pl.BlockS...  6.73 us
    dot_general x2, matrix products, causal_filter(): lax.dot_general(sources, kernel_upper, numbers, preferred_element_type=jn...  5.88 us
    unnamed x23, local copies, waits for them, and re-layouts  4.57 us
    ppermute x3, starting transfers between devices, tp_sum(): lax.ppermute(value, 'tp', [(i, i ^ stride) for i in range(count)])  3.41 us
    dot_general x2, matrix products, attend_block(): jnp.einsum('qhd,khd->hqk', query_heads, key_heads, preferred_element_type...  3.27 us
  transfers between devices with their start and end apart: 8, of which 3 were waited for; matrix products, arithmetic and copies ran while one was open for 32% of the time, Pallas kernels for 7%

profile of v4, /device:TPU:59, one launch (start us, length us, event | category | flops | bytes accessed | tf_op | source)
XLA Modules:
  0.0 94.6 jit_solution(12796603175854339733)
XLA Ops:
  0.7 1.4 %multiply_convert_fusion.1 = bf16[256,1024]{1,0:T(8,128)(2,1)S(1)} fusion(bf16[256,1024]{1,0:T(8,128)(2,1)} %param.13, bf16[256,1024]{1,0:T(8,128)(2,1)} %param.12), kind=kLoop, calls=%fused_computation.46 | loop fusion | flops 1048576 | bytes 1572864 | tf_op jit(solution)/shard_map/convert_element_type | solution.py:131
  2.1 3.5 %collective-permute-start = (bf16[127,1024]{1,0:T(8,128)(2,1)S(1)}, bf16[127,1024]{1,0:T(8,128)(2,1)S(1)}, u32[]{:S(2)}, u32[]{:S(2)}) collective-permute-start(bf16[127,1024]{1,0:T(8,128)(2,1)S(1)} %slice.37), channel_id=1, source_target_pairs={{0,8},{8,16},{16,24},{24,32},{32,40},{40,48},{48,56},{56,64},{64,7... | collective-permute-start | bytes 780296 | tf_op jit(solution)/shard_map/ppermute | solution.py:19
  5.7 5.6 %collective-permute-start.2 = (bf16[256,1024]{1,0:T(8,128)(2,1)}, bf16[256,1024]{1,0:T(8,128)(2,1)}, u32[]{:S(2)}, u32[]{:S(2)}) collective-permute-start(bf16[256,1024]{1,0:T(8,128)(2,1)} %param.16), channel_id=1, source_target_pairs={{16,0},{24,8},{32,16},{40,24},{48,32},{56,40},{64,48},{72,56},{80,... | collective-permute-start | bytes 1572872 | tf_op jit(solution)/shard_map/ppermute | solution.py:19
  11.3 1.2 %copy.38 = bf16[256,1024]{0,1:T(8,128)(2,1)S(1)} copy(bf16[256,1024]{1,0:T(8,128)(2,1)} %param.17) | data formatting | bytes 1048576 | tf_op args[7]
  12.5 1.2 %copy.39 = bf16[256,1024]{0,1:T(8,128)(2,1)S(1)} copy(bf16[256,1024]{1,0:T(8,128)(2,1)} %param.18) | data formatting | bytes 1048576 | tf_op args[8]
  13.8 1.1 %pad_maximum_fusion = bf16[2,256,1024]{1,2,0:T(8,128)(2,1)} fusion(bf16[1,256,1024]{1,2,0:T(8,128)(2,1)S(1)} %bitcast.66, bf16[1,256,1024]{1,2,0:T(8,128)(2,1)S(1)} %bitcast.62), kind=kLoop, calls=%fused_computation.40 | loop fusion | flops 524288 | bytes 2097152 | tf_op jit(solution)/shard_map/stack | solution.py:135
  14.9 1.9 %collective-permute-start.1 = (bf16[2,256,1024]{1,2,0:T(8,128)(2,1)}, bf16[2,256,1024]{1,2,0:T(8,128)(2,1)}, u32[]{:S(2)}, u32[]{:S(2)}) collective-permute-start(bf16[2,256,1024]{1,2,0:T(8,128)(2,1)} %pad_maximum_fusion), channel_id=1, source_target_pairs={{0,8},{8,16},{16,24},{24,32},{32,40},{40,48},{48,56},{56,64},{64,7... | collective-permute-start | bytes 3145736 | tf_op jit(solution)/shard_map/ppermute | solution.py:19
  18.0 6.7 %shard_map.113 = f32[64,128,256]{2,1,0:T(8,128)} custom-call(f32[64,256]{1,0:T(8,128)} %concatenate.34.reversed_ref), custom_call_target="tpu_custom_call" | custom-call | tf_op jit(solution)/shard_map/pallas_call | solution.py:44
  26.4 7.1 %fusion.4 = f32[64,16,128]{2,1,0:T(8,128)S(1)} fusion(bf16[256,64,16]{0,2,1:T(8,128)(2,1)S(1)} %bitcast.60, pred[128,256]{1,0:T(8,128)(4,1)S(1)} %get-tuple-element.33, f32[64,128,256]{2,1,0:T(8,128)} %shard_map.113), kind=kOutput, calls=%fused_computation.9 | convolution fusion | flops 77594624 | bytes 9469952 | tf_op jit(solution)/shard_map/dot_general | solution.py:78
  34.5 1.2 %fusion.43 = f32[64,16,128]{2,1,0:T(8,128)S(1)} fusion(f32[64,16,128]{2,1,0:T(8,128)S(1)} %fusion.4, bf16[256,64,16]{0,2,1:T(8,128)(2,1)S(1)} %bitcast.61, pred[128,256]{1,0:T(8,128)(4,1)S(1)} %get-tuple-element.33, f32[64,128,256]{2,1,0:T(8,128)S(1)} %copy-done), kind=kOutput, calls=%fused_computation.36 | convolution fusion | flops 71434240 | bytes 9994240 | tf_op jit(solution)/shard_map/dot_general | solution.py:77
  36.2 7.0 %fusion = f32[64,16,128]{2,1,0:T(8,128)S(1)} fusion(bf16[256,64,16]{0,2,1:T(8,128)(2,1)S(1)} %bitcast.58, pred[128,256]{1,0:T(8,128)(4,1)S(1)} %get-tuple-element.34, f32[64,128,256]{2,1,0:T(8,128)} %shard_map.113), kind=kOutput, calls=%fused_computation.5 | convolution fusion | flops 77594624 | bytes 9469952 | tf_op jit(solution)/shard_map/dot_general | solution.py:78
  43.1 4.7 %fusion.46 = f32[64,16,128]{2,1,0:T(8,128)S(1)} fusion(f32[64,16,128]{2,1,0:T(8,128)S(1)} %fusion, bf16[256,64,16]{0,2,1:T(8,128)(2,1)S(1)} %bitcast.59, pred[128,256]{1,0:T(8,128)(4,1)S(1)} %get-tuple-element.34, f32[64,128,256]{2,1,0:T(8,128)} %shard_map.113), kind=kOutput, calls=%fused_computation.37 | convolution fusion | flops 71434240 | bytes 9994240 | tf_op jit(solution)/shard_map/dot_general | solution.py:77
  48.4 2.1 %fusion.83 = (bf16[1,256,1024]{1,2,0:T(8,128)(2,1)}, bf16[1,256,1024]{1,2,0:T(8,128)(2,1)S(1)}) fusion(bf16[2,256,1024]{1,2,0:T(8,128)(2,1)} %collective-permute-done.1), kind=kLoop, calls=%fused_computation.94 | loop fusion | bytes 2097152 | tf_op jit(solution)/shard_map/slice | solution.py:139
  51.4 2.3 %fusion.12 = (f32[8,256]{1,0:T(8,128)S(1)}, f32[8,256,512]{2,1,0:T(8,128)S(1)}) fusion(pred[256,512]{1,0:T(8,128)(4,1)S(1)} %get-tuple-element.30, bf16[256,8,128]{2,0,1:T(8,128)(2,1)} %copy.43, bf16[256,8,128]{2,0,1:T(8,128)(2,1)} %copy.42, bf16[256,1024]{1,0:T(8,128)(2,1)} %collective-permute-done.2), kind=kOutput, calls=%fused_computation.17 | convolution fusion | flops 273676288 | bytes 5906432 | tf_op jit(solution)/shard_map/qhd,khd->hqk/dot_general | solution.py:100
  53.8 1.6 %fusion.14 = f32[8,256]{1,0:T(8,128)S(1)} fusion(f32[8,256,512]{2,1,0:T(8,128)S(1)} %get-tuple-element.36, f32[8,256]{1,0:T(8,128)S(1)} %get-tuple-element.35, pred[256,512]{1,0:T(8,128)(4,1)S(1)} %get-tuple-element.30), kind=kLoop, calls=%fused_computation.19 | loop fusion | flops 5240832 | bytes 4341760 | tf_op jit(solution)/shard_map/reduce_sum | solution.py:106
  55.4 1.6 %fusion.40 = bf16[256,8,128]{0,2,1:T(8,128)(2,1)S(1)} fusion(f32[8,256,512]{2,1,0:T(8,128)S(1)} %get-tuple-element.36, f32[8,256]{1,0:T(8,128)S(1)} %get-tuple-element.35, pred[256,512]{1,0:T(8,128)(4,1)S(1)} %get-tuple-element.30, bf16[256,8,128]{0,2,1:T(8,128)(2,1)S(1)} %bitcast.67, bf16[256,8,128]{0,2,1:T(8,128)(2,1)S(1)} %bitcast.71), kind=kOutput, calls=%fused_computation.35 | convolution fusion | flops 276037632 | bytes 5906432 | tf_op jit(solution)/shard_map/hqk,khd->qhd/dot_general | solution.py:107
  57.0 1.0 %collective-permute-start.3 = (f32[256]{0:T(256)S(1)}, f32[256]{0:T(256)S(1)}, u32[]{:S(2)}, u32[]{:S(2)}) collective-permute-start(f32[256]{0:T(256)S(1)} %multiply_reduce_fusion), channel_id=1, source_target_pairs={{0,1},{1,0},{2,3},{3,2},{4,5},{5,4},{6,7},{7,6},{8,9},{9,8},{10,11... | collective-permute-start | bytes 3080 | tf_op jit(solution)/shard_map/ppermute | solution.py:89
  58.0 4.0 %collective-permute-start.6 = (f32[256,16]{0,1:T(8,128)S(1)}, f32[256,16]{0,1:T(8,128)S(1)}, u32[]{:S(2)}, u32[]{:S(2)}) collective-permute-start(f32[256,16]{0,1:T(8,128)S(1)} %pad_maximum_fusion.8), channel_id=1, source_target_pairs={{0,16},{8,24},{16,32},{24,40},{32,48},{40,56},{48,64},{56,72},{64,... | collective-permute-start | bytes 49160 | tf_op jit(solution)/shard_map/ppermute | solution.py:19
  62.0 4.8 %collective-permute-start.7 = (bf16[256,8,128]{0,2,1:T(8,128)(2,1)S(1)}, bf16[256,8,128]{0,2,1:T(8,128)(2,1)S(1)}, u32[]{:S(2)}, u32[]{:S(2)}) collective-permute-start(bf16[256,8,128]{0,2,1:T(8,128)(2,1)S(1)} %fusion.40), channel_id=1, source_target_pairs={{0,16},{8,24},{16,32},{24,40},{32,48},{40,56},{48,64},{56,72},{64,... | collective-permute-start | bytes 1572872 | tf_op jit(solution)/shard_map/ppermute | solution.py:19
  68.3 1.2 %collective-permute-done.4 = f32[256]{0:T(256)S(1)} collective-permute-done((f32[256]{0:T(256)S(1)}, f32[256]{0:T(256)S(1)}, u32[]{:S(2)}, u32[]{:S(2)}) %collective-permute-start.4) | collective-permute-done | bytes 1056 | tf_op jit(solution)/shard_map/ppermute | solution.py:89
  69.5 1.8 %collective-permute-start.5 = (f32[256]{0:T(256)S(1)}, f32[256]{0:T(256)S(1)}, u32[]{:S(2)}, u32[]{:S(2)}) collective-permute-start(f32[256]{0:T(256)S(1)} %add.103), channel_id=1, source_target_pairs={{0,4},{1,5},{2,6},{3,7},{4,0},{5,1},{6,2},{7,3},{8,12},{9,13},{10,... | collective-permute-start | bytes 3080 | tf_op jit(solution)/shard_map/ppermute | solution.py:89
  71.4 1.5 %fusion.16 = f32[8,256]{1,0:T(8,128)S(1)} fusion(f32[8,256,512]{2,1,0:T(8,128)S(1)} %get-tuple-element.38, f32[8,256]{1,0:T(8,128)S(1)} %get-tuple-element.37, pred[256,512]{1,0:T(8,128)(4,1)S(1)} %get-tuple-element.29), kind=kLoop, calls=%fused_computation.21 | loop fusion | flops 5240832 | bytes 4341760 | tf_op jit(solution)/shard_map/reduce_sum | solution.py:106
  74.8 17.1 %collective-permute-done.7 = bf16[256,8,128]{0,2,1:T(8,128)(2,1)S(1)} collective-permute-done((bf16[256,8,128]{0,2,1:T(8,128)(2,1)S(1)}, bf16[256,8,128]{0,2,1:T(8,128)(2,1)S(1)}, u32[]{:S(2)}, u32[]{:S(2)}) %collective-permute-start.7) | collective-permute-done | bytes 524320 | tf_op jit(solution)/shard_map/ppermute | solution.py:19
  91.9 1.6 %divide_convert_fusion = bf16[256,8,128]{0,2,1:T(8,128)(2,1)S(1)} fusion(bf16[256,8,128]{0,2,1:T(8,128)(2,1)S(1)} %collective-permute-done.7, f32[8,256,512]{2,1,0:T(8,128)S(1)} %get-tuple-element.38, f32[8,256]{1,0:T(8,128)S(1)} %get-tuple-element.37, pred[256,512]{1,0:T(8,128)(4,1)S(1)} %get-tuple-element.29, bf16[256,8,128]{0,2,1:T(8,128)(2,1)S(1)} %bitcast.68, ...), kind=kOutput, calls=%fused_computation.43 | convolution fusion | flops 277348352 | bytes 6455296 | tf_op jit(solution)/shard_map/hqk,khd->qhd/dot_general | solution.py:107
  (55 shorter events, 10.1 us)
Async XLA Ops:
  0.6 16.2 %copy-start.9 = (s32[32]{0:T(128)S(1)}, s32[32]{0:T(128)}, u32[]{:S(2)}) copy-start(s32[32]{0:T(128)} %param.19) | copy-start | bytes 388
  0.6 16.6 %copy-start.6 = (f32[64,128]{1,0:T(8,128)S(1)}, f32[64,128]{1,0:T(8,128)}, u32[]{:S(2)}) copy-start(f32[64,128]{1,0:T(8,128)} %param.14) | copy-start | bytes 98308
  2.1 23.9 %collective-permute-start = (bf16[127,1024]{1,0:T(8,128)(2,1)S(1)}, bf16[127,1024]{1,0:T(8,128)(2,1)S(1)}, u32[]{:S(2)}, u32[]{:S(2)}) collective-permute-start(bf16[127,1024]{1,0:T(8,128)(2,1)S(1)} %slice.37), channel_id=1, source_target_pairs={{0,8},{8,16},{16,24},{24,32},{32,40},{40,48},{48,56},{56,64},{64,7... | collective-permute-start | bytes 780296 | tf_op jit(solution)/shard_map/ppermute | solution.py:19
  5.7 42.7 %collective-permute-start.2 = (bf16[256,1024]{1,0:T(8,128)(2,1)}, bf16[256,1024]{1,0:T(8,128)(2,1)}, u32[]{:S(2)}, u32[]{:S(2)}) collective-permute-start(bf16[256,1024]{1,0:T(8,128)(2,1)} %param.16), channel_id=1, source_target_pairs={{16,0},{24,8},{32,16},{40,24},{48,32},{56,40},{64,48},{72,56},{80,... | collective-permute-start | bytes 1572872 | tf_op jit(solution)/shard_map/ppermute | solution.py:19
  14.9 33.4 %collective-permute-start.1 = (bf16[2,256,1024]{1,2,0:T(8,128)(2,1)}, bf16[2,256,1024]{1,2,0:T(8,128)(2,1)}, u32[]{:S(2)}, u32[]{:S(2)}) collective-permute-start(bf16[2,256,1024]{1,2,0:T(8,128)(2,1)} %pad_maximum_fusion), channel_id=1, source_target_pairs={{0,8},{8,16},{16,24},{24,32},{32,40},{40,48},{48,56},{56,64},{64,7... | collective-permute-start | bytes 3145736 | tf_op jit(solution)/shard_map/ppermute | solution.py:19
  26.4 8.2 %copy-start = (f32[64,128,256]{2,1,0:T(8,128)S(1)}, f32[64,128,256]{2,1,0:T(8,128)}, u32[]{:S(2)}) copy-start(f32[64,128,256]{2,1,0:T(8,128)} %shard_map.113) | copy-start | bytes 25165828
  43.1 4.9 %copy-start.1 = (bf16[256,1024]{1,0:T(8,128)(2,1)S(1)}, bf16[256,1024]{1,0:T(8,128)(2,1)}, u32[]{:S(2)}) copy-start(bf16[256,1024]{1,0:T(8,128)(2,1)} %param.11) | copy-start | bytes 1572868
  43.1 4.9 %copy-start.2 = (bf16[256,1024]{1,0:T(8,128)(2,1)S(1)}, bf16[256,1024]{1,0:T(8,128)(2,1)}, u32[]{:S(2)}) copy-start(bf16[256,1024]{1,0:T(8,128)(2,1)} %param.10) | copy-start | bytes 1572868
  51.4 3.9 %copy-start.5 = (bf16[1,256,1024]{1,2,0:T(8,128)(2,1)S(1)}, bf16[1,256,1024]{1,2,0:T(8,128)(2,1)}, u32[]{:S(2)}) copy-start(bf16[1,256,1024]{1,2,0:T(8,128)(2,1)} %get-tuple-element.25) | copy-start | bytes 1572868
  55.3 12.0 %copy-start.3 = (bf16[256,8,128]{2,0,1:T(8,128)(2,1)S(1)}, bf16[256,8,128]{2,0,1:T(8,128)(2,1)}, u32[]{:S(2)}) copy-start(bf16[256,8,128]{2,0,1:T(8,128)(2,1)} %copy.43) | copy-start | bytes 1572868
  55.4 12.0 %copy-start.4 = (bf16[256,8,128]{2,0,1:T(8,128)(2,1)S(1)}, bf16[256,8,128]{2,0,1:T(8,128)(2,1)}, u32[]{:S(2)}) copy-start(bf16[256,8,128]{2,0,1:T(8,128)(2,1)} %copy.42) | copy-start | bytes 1572868
  55.4 12.0 %copy-start.8 = (bf16[256,1024]{1,0:T(8,128)(2,1)S(1)}, bf16[256,1024]{1,0:T(8,128)(2,1)}, u32[]{:S(2)}) copy-start(bf16[256,1024]{1,0:T(8,128)(2,1)} %param.16) | copy-start | bytes 1572868
  57.0 9.8 %collective-permute-start.3 = (f32[256]{0:T(256)S(1)}, f32[256]{0:T(256)S(1)}, u32[]{:S(2)}, u32[]{:S(2)}) collective-permute-start(f32[256]{0:T(256)S(1)} %multiply_reduce_fusion), channel_id=1, source_target_pairs={{0,1},{1,0},{2,3},{3,2},{4,5},{5,4},{6,7},{7,6},{8,9},{9,8},{10,11... | collective-permute-start | bytes 3080 | tf_op jit(solution)/shard_map/ppermute | solution.py:89
  58.0 16.8 %collective-permute-start.6 = (f32[256,16]{0,1:T(8,128)S(1)}, f32[256,16]{0,1:T(8,128)S(1)}, u32[]{:S(2)}, u32[]{:S(2)}) collective-permute-start(f32[256,16]{0,1:T(8,128)S(1)} %pad_maximum_fusion.8), channel_id=1, source_target_pairs={{0,16},{8,24},{16,32},{24,40},{32,48},{40,56},{48,64},{56,72},{64,... | collective-permute-start | bytes 49160 | tf_op jit(solution)/shard_map/ppermute | solution.py:19
  62.0 29.9 %collective-permute-start.7 = (bf16[256,8,128]{0,2,1:T(8,128)(2,1)S(1)}, bf16[256,8,128]{0,2,1:T(8,128)(2,1)S(1)}, u32[]{:S(2)}, u32[]{:S(2)}) collective-permute-start(bf16[256,8,128]{0,2,1:T(8,128)(2,1)S(1)} %fusion.40), channel_id=1, source_target_pairs={{0,16},{8,24},{16,32},{24,40},{32,48},{40,56},{48,64},{56,72},{64,... | collective-permute-start | bytes 1572872 | tf_op jit(solution)/shard_map/ppermute | solution.py:19
  66.9 2.7 %collective-permute-start.4 = (f32[256]{0:T(256)S(1)}, f32[256]{0:T(256)S(1)}, u32[]{:S(2)}, u32[]{:S(2)}) collective-permute-start(f32[256]{0:T(256)S(1)} %add.102), channel_id=1, source_target_pairs={{0,2},{1,3},{2,0},{3,1},{4,6},{5,7},{6,4},{7,5},{8,10},{9,11},{10,... | collective-permute-start | bytes 3080 | tf_op jit(solution)/shard_map/ppermute | solution.py:89
  67.4 6.4 %copy-start.7 = (f32[1024]{0:T(1024)S(1)}, f32[1024]{0:T(1024)}, u32[]{:S(2)}) copy-start(f32[1024]{0:T(1024)} %param.15) | copy-start | bytes 12292
  69.5 4.2 %collective-permute-start.5 = (f32[256]{0:T(256)S(1)}, f32[256]{0:T(256)S(1)}, u32[]{:S(2)}, u32[]{:S(2)}) collective-permute-start(f32[256]{0:T(256)S(1)} %add.103), channel_id=1, source_target_pairs={{0,4},{1,5},{2,6},{3,7},{4,0},{5,1},{6,2},{7,3},{8,12},{9,13},{10,... | collective-permute-start | bytes 3080 | tf_op jit(solution)/shard_map/ppermute | solution.py:89

commit v5 on v4

--- a/solution.py
+++ b/solution.py
@@ -150,9 +150,24 @@
     far_visible = (key_pos[None, :] <= far_pos[:, None]) & (key_pos[None, :] >= far_begin[:, None])
     far_sum, far_top, far_den = attend_block(later_query, key_rows, value_rows, far_visible, scale)
     far_stats = jnp.concatenate([far_top, far_den], axis=1)
-    far_packet = (far_sum.astype(jnp.bfloat16), far_stats)
+    stat_cols = far_stats.shape[1]
+    stat_high = far_stats.astype(jnp.bfloat16)
+    stat_rest = far_stats - stat_high.astype(jnp.float32)
+    stat_mid = stat_rest.astype(jnp.bfloat16)
+    stat_low = (stat_rest - stat_mid.astype(jnp.float32)).astype(jnp.bfloat16)
+    stat_pad = jnp.zeros((tok_rows, 128 - 3 * stat_cols), jnp.bfloat16)
+    far_packet = jnp.concatenate(
+        [far_sum.astype(jnp.bfloat16).reshape(tok_rows, -1), stat_high, stat_mid, stat_low, stat_pad],
+        axis=1,
+    )
     far_packet, local_sum, near_query = lax.optimization_barrier((far_packet, local_sum, att_query))
-    far_sum, far_stats = shifted(far_packet, "ctx", 2)
+    far_packet = shifted(far_packet, "ctx", 2)
+    sum_cols = far_sum.shape[1] * far_sum.shape[2]
+    far_sum = far_packet[:, :sum_cols].reshape(far_sum.shape)
+    stat_parts = far_packet[:, sum_cols : sum_cols + 3 * stat_cols].astype(jnp.float32)
+    far_stats = stat_parts[:, :stat_cols] + (
+        stat_parts[:, stat_cols : 2 * stat_cols] + stat_parts[:, 2 * stat_cols :]
+    )
     mean_square = tp_sum(local_sum) / D
     normed = (hidden * lax.rsqrt(mean_square + norm_epsilon)[:, None] * norm_gain[None, :]).astype(
         jnp.bfloat16

time: 95.2 us -> 96.2 us (1.011)
  the two profiles are of different devices: /device:TPU:59 before, /device:TPU:24 now
where the time goes in v5:
time: 96.2 us; the launch traced here: 95.6 us
  matrix products  26.5 us (28%)
  waiting for transfers between devices  22.4 us (23%)
  starting transfers between devices  20.8 us (22%)
  local copies, waits for them, and re-layouts  10.3 us (11%)
  other arithmetic  7.79 us (8%)
  Pallas kernels  6.72 us (7%)
  between operations  1 us (1%)
    ppermute x4, waiting for transfers between devices, shifted(): lax.ppermute(value, axis, [(source, source + steps) for source in range(f...  20.8 us
    ppermute x4, starting transfers between devices, shifted(): lax.ppermute(value, axis, [(source, source + steps) for source in range(f...  16 us
    dot_general x2, matrix products, causal_filter(): lax.dot_general(sources, kernel_lower, numbers, preferred_element_type=jn...  14.1 us
    pallas_call x1, Pallas kernels, build_toeplitz(): pl.pallas_call(toeplitz_rows, grid=(groups // step,), in_specs=[pl.BlockS...  6.72 us
    dot_general x2, matrix products, causal_filter(): lax.dot_general(sources, kernel_upper, numbers, preferred_element_type=jn...  5.88 us
    ppermute x3, starting transfers between devices, tp_sum(): lax.ppermute(value, 'tp', [(i, i ^ stride) for i in range(count)])  4.87 us
    unnamed x24, local copies, waits for them, and re-layouts  4.61 us
    dot_general x2, matrix products, attend_block(): jnp.einsum('qhd,khd->hqk', query_heads, key_heads, preferred_element_type...  3.29 us
  transfers between devices with their start and end apart: 7, of which 3 were waited for; matrix products, arithmetic and copies ran while one was open for 32% of the time, Pallas kernels for 7%

profile of v5, /device:TPU:24, one launch (start us, length us, event | category | flops | bytes accessed | tf_op | source)
XLA Modules:
  0.0 95.6 jit_solution(12972391512102224647)
XLA Ops:
  0.7 1.4 %multiply_convert_fusion.1 = bf16[256,1024]{1,0:T(8,128)(2,1)S(1)} fusion(bf16[256,1024]{1,0:T(8,128)(2,1)} %param.13, bf16[256,1024]{1,0:T(8,128)(2,1)} %param.12), kind=kLoop, calls=%fused_computation.46 | loop fusion | flops 1048576 | bytes 1572864 | tf_op jit(solution)/shard_map/convert_element_type | solution.py:131
  2.1 3.8 %collective-permute-start = (bf16[127,1024]{1,0:T(8,128)(2,1)S(1)}, bf16[127,1024]{1,0:T(8,128)(2,1)S(1)}, u32[]{:S(2)}, u32[]{:S(2)}) collective-permute-start(bf16[127,1024]{1,0:T(8,128)(2,1)S(1)} %slice.57), channel_id=1, source_target_pairs={{0,8},{8,16},{16,24},{24,32},{32,40},{40,48},{48,56},{56,64},{64,7... | collective-permute-start | bytes 780296 | tf_op jit(solution)/shard_map/ppermute | solution.py:19
  6.0 7.5 %collective-permute-start.2 = (bf16[256,1024]{1,0:T(8,128)(2,1)}, bf16[256,1024]{1,0:T(8,128)(2,1)}, u32[]{:S(2)}, u32[]{:S(2)}) collective-permute-start(bf16[256,1024]{1,0:T(8,128)(2,1)} %param.16), channel_id=1, source_target_pairs={{16,0},{24,8},{32,16},{40,24},{48,32},{56,40},{64,48},{72,56},{80,... | collective-permute-start | bytes 1572872 | tf_op jit(solution)/shard_map/ppermute | solution.py:19
  13.5 1.2 %copy.38 = bf16[256,1024]{0,1:T(8,128)(2,1)S(1)} copy(bf16[256,1024]{1,0:T(8,128)(2,1)} %param.17) | data formatting | bytes 1048576 | tf_op args[7]
  14.7 1.2 %copy.39 = bf16[256,1024]{0,1:T(8,128)(2,1)S(1)} copy(bf16[256,1024]{1,0:T(8,128)(2,1)} %param.18) | data formatting | bytes 1048576 | tf_op args[8]
  16.0 1.1 %pad_maximum_fusion = bf16[2,256,1024]{1,2,0:T(8,128)(2,1)} fusion(bf16[1,256,1024]{1,2,0:T(8,128)(2,1)S(1)} %bitcast.69, bf16[1,256,1024]{1,2,0:T(8,128)(2,1)S(1)} %bitcast.65), kind=kLoop, calls=%fused_computation.39 | loop fusion | flops 524288 | bytes 2097152 | tf_op jit(solution)/shard_map/stack | solution.py:135
  17.1 1.9 %collective-permute-start.1 = (bf16[2,256,1024]{1,2,0:T(8,128)(2,1)}, bf16[2,256,1024]{1,2,0:T(8,128)(2,1)}, u32[]{:S(2)}, u32[]{:S(2)}) collective-permute-start(bf16[2,256,1024]{1,2,0:T(8,128)(2,1)} %pad_maximum_fusion), channel_id=1, source_target_pairs={{0,8},{8,16},{16,24},{24,32},{32,40},{40,48},{48,56},{56,64},{64,7... | collective-permute-start | bytes 3145736 | tf_op jit(solution)/shard_map/ppermute | solution.py:19
  20.2 6.7 %shard_map.113 = f32[64,128,256]{2,1,0:T(8,128)} custom-call(f32[64,256]{1,0:T(8,128)} %concatenate.37.reversed_ref), custom_call_target="tpu_custom_call" | custom-call | tf_op jit(solution)/shard_map/pallas_call | solution.py:44
  28.6 7.1 %fusion.4 = f32[64,16,128]{2,1,0:T(8,128)S(1)} fusion(bf16[256,64,16]{0,2,1:T(8,128)(2,1)S(1)} %bitcast.63, pred[128,256]{1,0:T(8,128)(4,1)S(1)} %get-tuple-element.31, f32[64,128,256]{2,1,0:T(8,128)} %shard_map.113), kind=kOutput, calls=%fused_computation.9 | convolution fusion | flops 77594624 | bytes 9469952 | tf_op jit(solution)/shard_map/dot_general | solution.py:78
  35.7 1.0 %copy-done = f32[64,128,256]{2,1,0:T(8,128)S(1)} copy-done((f32[64,128,256]{2,1,0:T(8,128)S(1)}, f32[64,128,256]{2,1,0:T(8,128)}, u32[]{:S(2)}) %copy-start) | copy-done | bytes 8388632
  36.7 1.2 %fusion.40 = f32[64,16,128]{2,1,0:T(8,128)S(1)} fusion(f32[64,16,128]{2,1,0:T(8,128)S(1)} %fusion.4, bf16[256,64,16]{0,2,1:T(8,128)(2,1)S(1)} %bitcast.64, pred[128,256]{1,0:T(8,128)(4,1)S(1)} %get-tuple-element.31, f32[64,128,256]{2,1,0:T(8,128)S(1)} %copy-done), kind=kOutput, calls=%fused_computation.35 | convolution fusion | flops 71434240 | bytes 9994240 | tf_op jit(solution)/shard_map/dot_general | solution.py:77
  38.4 7.0 %fusion = f32[64,16,128]{2,1,0:T(8,128)S(1)} fusion(bf16[256,64,16]{0,2,1:T(8,128)(2,1)S(1)} %bitcast.61, pred[128,256]{1,0:T(8,128)(4,1)S(1)} %get-tuple-element.32, f32[64,128,256]{2,1,0:T(8,128)} %shard_map.113), kind=kOutput, calls=%fused_computation.5 | convolution fusion | flops 77594624 | bytes 9469952 | tf_op jit(solution)/shard_map/dot_general | solution.py:78
  45.3 4.7 %fusion.43 = f32[64,16,128]{2,1,0:T(8,128)S(1)} fusion(f32[64,16,128]{2,1,0:T(8,128)S(1)} %fusion, bf16[256,64,16]{0,2,1:T(8,128)(2,1)S(1)} %bitcast.62, pred[128,256]{1,0:T(8,128)(4,1)S(1)} %get-tuple-element.32, f32[64,128,256]{2,1,0:T(8,128)} %shard_map.113), kind=kOutput, calls=%fused_computation.36 | convolution fusion | flops 71434240 | bytes 9994240 | tf_op jit(solution)/shard_map/dot_general | solution.py:77
  50.5 2.1 %fusion.83 = (bf16[1,256,1024]{1,2,0:T(8,128)(2,1)}, bf16[1,256,1024]{1,2,0:T(8,128)(2,1)S(1)}) fusion(bf16[2,256,1024]{1,2,0:T(8,128)(2,1)} %collective-permute-done.1), kind=kLoop, calls=%fused_computation.106 | loop fusion | bytes 2097152 | tf_op jit(solution)/shard_map/slice | solution.py:139
  53.6 2.3 %fusion.12 = (f32[8,256]{1,0:T(8,128)S(1)}, f32[8,256,512]{2,1,0:T(8,128)S(1)}) fusion(pred[256,512]{1,0:T(8,128)(4,1)S(1)} %get-tuple-element.28, bf16[256,8,128]{2,0,1:T(8,128)(2,1)} %copy.43, bf16[256,8,128]{2,0,1:T(8,128)(2,1)} %copy.42, bf16[256,1024]{1,0:T(8,128)(2,1)} %collective-permute-done.2), kind=kOutput, calls=%fused_computation.17 | convolution fusion | flops 273676288 | bytes 5906432 | tf_op jit(solution)/shard_map/qhd,khd->hqk/dot_general | solution.py:100
  55.9 1.6 %fusion.14 = f32[8,256]{1,0:T(8,128)S(1)} fusion(f32[8,256,512]{2,1,0:T(8,128)S(1)} %get-tuple-element.34, f32[8,256]{1,0:T(8,128)S(1)} %get-tuple-element.33, pred[256,512]{1,0:T(8,128)(4,1)S(1)} %get-tuple-element.28), kind=kLoop, calls=%fused_computation.19 | loop fusion | flops 5240832 | bytes 4341760 | tf_op jit(solution)/shard_map/reduce_sum | solution.py:106
  57.5 1.6 %fusion.37 = bf16[8,128,256]{2,1,0:T(8,128)(2,1)S(1)} fusion(f32[8,256,512]{2,1,0:T(8,128)S(1)} %get-tuple-element.34, f32[8,256]{1,0:T(8,128)S(1)} %get-tuple-element.33, pred[256,512]{1,0:T(8,128)(4,1)S(1)} %get-tuple-element.28, bf16[256,8,128]{0,2,1:T(8,128)(2,1)S(1)} %bitcast.70, bf16[256,8,128]{0,2,1:T(8,128)(2,1)S(1)} %bitcast.76), kind=kOutput, calls=%fused_computation.34 | convolution fusion | flops 276037632 | bytes 5906432 | tf_op jit(solution)/shard_map/hqk,khd->qhd/dot_general | solution.py:107
  59.4 2.7 %collective-permute-start.6 = (bf16[256,1152]{0,1:T(8,128)(2,1)S(1)}, bf16[256,1152]{0,1:T(8,128)(2,1)S(1)}, u32[]{:S(2)}, u32[]{:S(2)}) collective-permute-start(bf16[256,1152]{0,1:T(8,128)(2,1)S(1)} %broadcast_dynamic-update-slice_fusion), channel_id=1, source_target_pairs={{0,16},{8,24},{16,32},{24,40},{32,48},{40,56},{48,64},{56,72},{64,... | collective-permute-start | bytes 1769480 | tf_op jit(solution)/shard_map/ppermute | solution.py:19
  62.1 1.8 %collective-permute-start.4 = (f32[256]{0:T(256)S(1)}, f32[256]{0:T(256)S(1)}, u32[]{:S(2)}, u32[]{:S(2)}) collective-permute-start(f32[256]{0:T(256)S(1)} %add.108), channel_id=1, source_target_pairs={{0,2},{1,3},{2,0},{3,1},{4,6},{5,7},{6,4},{7,5},{8,10},{9,11},{10,... | collective-permute-start | bytes 3080 | tf_op jit(solution)/shard_map/ppermute | solution.py:89
  64.8 1.1 %collective-permute-done.4 = f32[256]{0:T(256)S(1)} collective-permute-done((f32[256]{0:T(256)S(1)}, f32[256]{0:T(256)S(1)}, u32[]{:S(2)}, u32[]{:S(2)}) %collective-permute-start.4) | collective-permute-done | bytes 1056 | tf_op jit(solution)/shard_map/ppermute | solution.py:89
  66.0 3.0 %collective-permute-start.5 = (f32[256]{0:T(256)S(1)}, f32[256]{0:T(256)S(1)}, u32[]{:S(2)}, u32[]{:S(2)}) collective-permute-start(f32[256]{0:T(256)S(1)} %add.109), channel_id=1, source_target_pairs={{0,4},{1,5},{2,6},{3,7},{4,0},{5,1},{6,2},{7,3},{8,12},{9,13},{10,... | collective-permute-start | bytes 3080 | tf_op jit(solution)/shard_map/ppermute | solution.py:89
  69.0 1.5 %fusion.16 = f32[8,256]{1,0:T(8,128)S(1)} fusion(f32[8,256,512]{2,1,0:T(8,128)S(1)} %get-tuple-element.36, f32[8,256]{1,0:T(8,128)S(1)} %get-tuple-element.35, pred[256,512]{1,0:T(8,128)(4,1)S(1)} %get-tuple-element.27), kind=kLoop, calls=%fused_computation.21 | loop fusion | flops 5240832 | bytes 4341760 | tf_op jit(solution)/shard_map/reduce_sum | solution.py:106
  72.1 20.8 %collective-permute-done.6 = bf16[256,1152]{0,1:T(8,128)(2,1)S(1)} collective-permute-done((bf16[256,1152]{0,1:T(8,128)(2,1)S(1)}, bf16[256,1152]{0,1:T(8,128)(2,1)S(1)}, u32[]{:S(2)}, u32[]{:S(2)}) %collective-permute-start.6) | collective-permute-done | bytes 589856 | tf_op jit(solution)/shard_map/ppermute | solution.py:19
  92.9 1.7 %divide_convert_fusion = bf16[256,8,128]{0,2,1:T(8,128)(2,1)S(1)} fusion(bf16[256,8,128]{0,2,1:T(8,128)(2,1)S(1)} %bitcast.73, f32[8,256,512]{2,1,0:T(8,128)S(1)} %get-tuple-element.36, f32[8,256]{1,0:T(8,128)S(1)} %get-tuple-element.35, pred[256,512]{1,0:T(8,128)(4,1)S(1)} %get-tuple-element.27, bf16[256,8,128]{0,2,1:T(8,128)(2,1)S(1)} %bitcast.71, ...), kind=kOutput, calls=%fused_computation.43 | convolution fusion | flops 277348352 | bytes 6455296 | tf_op jit(solution)/shard_map/hqk,khd->qhd/dot_general | solution.py:107
  (60 shorter events, 8.5 us)
Async XLA Ops:
  0.6 18.4 %copy-start.9 = (s32[32]{0:T(128)S(1)}, s32[32]{0:T(128)}, u32[]{:S(2)}) copy-start(s32[32]{0:T(128)} %param.19) | copy-start | bytes 388
  0.6 18.8 %copy-start.6 = (f32[64,128]{1,0:T(8,128)S(1)}, f32[64,128]{1,0:T(8,128)}, u32[]{:S(2)}) copy-start(f32[64,128]{1,0:T(8,128)} %param.14) | copy-start | bytes 98308
  2.1 26.0 %collective-permute-start = (bf16[127,1024]{1,0:T(8,128)(2,1)S(1)}, bf16[127,1024]{1,0:T(8,128)(2,1)S(1)}, u32[]{:S(2)}, u32[]{:S(2)}) collective-permute-start(bf16[127,1024]{1,0:T(8,128)(2,1)S(1)} %slice.57), channel_id=1, source_target_pairs={{0,8},{8,16},{16,24},{24,32},{32,40},{40,48},{48,56},{56,64},{64,7... | collective-permute-start | bytes 780296 | tf_op jit(solution)/shard_map/ppermute | solution.py:19
  6.0 44.6 %collective-permute-start.2 = (bf16[256,1024]{1,0:T(8,128)(2,1)}, bf16[256,1024]{1,0:T(8,128)(2,1)}, u32[]{:S(2)}, u32[]{:S(2)}) collective-permute-start(bf16[256,1024]{1,0:T(8,128)(2,1)} %param.16), channel_id=1, source_target_pairs={{16,0},{24,8},{32,16},{40,24},{48,32},{56,40},{64,48},{72,56},{80,... | collective-permute-start | bytes 1572872 | tf_op jit(solution)/shard_map/ppermute | solution.py:19
  17.1 33.4 %collective-permute-start.1 = (bf16[2,256,1024]{1,2,0:T(8,128)(2,1)}, bf16[2,256,1024]{1,2,0:T(8,128)(2,1)}, u32[]{:S(2)}, u32[]{:S(2)}) collective-permute-start(bf16[2,256,1024]{1,2,0:T(8,128)(2,1)} %pad_maximum_fusion), channel_id=1, source_target_pairs={{0,8},{8,16},{16,24},{24,32},{32,40},{40,48},{48,56},{56,64},{64,7... | collective-permute-start | bytes 3145736 | tf_op jit(solution)/shard_map/ppermute | solution.py:19
  28.6 8.2 %copy-start = (f32[64,128,256]{2,1,0:T(8,128)S(1)}, f32[64,128,256]{2,1,0:T(8,128)}, u32[]{:S(2)}) copy-start(f32[64,128,256]{2,1,0:T(8,128)} %shard_map.113) | copy-start | bytes 25165828
  45.3 4.9 %copy-start.1 = (bf16[256,1024]{1,0:T(8,128)(2,1)S(1)}, bf16[256,1024]{1,0:T(8,128)(2,1)}, u32[]{:S(2)}) copy-start(bf16[256,1024]{1,0:T(8,128)(2,1)} %param.11) | copy-start | bytes 1572868
  45.3 4.9 %copy-start.2 = (bf16[256,1024]{1,0:T(8,128)(2,1)S(1)}, bf16[256,1024]{1,0:T(8,128)(2,1)}, u32[]{:S(2)}) copy-start(bf16[256,1024]{1,0:T(8,128)(2,1)} %param.10) | copy-start | bytes 1572868
  53.6 3.9 %copy-start.5 = (bf16[1,256,1024]{1,2,0:T(8,128)(2,1)S(1)}, bf16[1,256,1024]{1,2,0:T(8,128)(2,1)}, u32[]{:S(2)}) copy-start(bf16[1,256,1024]{1,2,0:T(8,128)(2,1)} %get-tuple-element.23) | copy-start | bytes 1572868
  57.5 6.4 %copy-start.3 = (bf16[256,8,128]{2,0,1:T(8,128)(2,1)S(1)}, bf16[256,8,128]{2,0,1:T(8,128)(2,1)}, u32[]{:S(2)}) copy-start(bf16[256,8,128]{2,0,1:T(8,128)(2,1)} %copy.43) | copy-start | bytes 1572868
  57.5 6.4 %copy-start.4 = (bf16[256,8,128]{2,0,1:T(8,128)(2,1)S(1)}, bf16[256,8,128]{2,0,1:T(8,128)(2,1)}, u32[]{:S(2)}) copy-start(bf16[256,8,128]{2,0,1:T(8,128)(2,1)} %copy.42) | copy-start | bytes 1572868
  57.5 6.3 %copy-start.8 = (bf16[256,1024]{1,0:T(8,128)(2,1)S(1)}, bf16[256,1024]{1,0:T(8,128)(2,1)}, u32[]{:S(2)}) copy-start(bf16[256,1024]{1,0:T(8,128)(2,1)} %param.16) | copy-start | bytes 1572868
  59.3 2.8 %collective-permute-start.3 = (f32[256]{0:T(256)S(1)}, f32[256]{0:T(256)S(1)}, u32[]{:S(2)}, u32[]{:S(2)}) collective-permute-start(f32[256]{0:T(256)S(1)} %multiply_reduce_fusion), channel_id=1, source_target_pairs={{0,1},{1,0},{2,3},{3,2},{4,5},{5,4},{6,7},{7,6},{8,9},{9,8},{10,11... | collective-permute-start | bytes 3080 | tf_op jit(solution)/shard_map/ppermute | solution.py:89
  59.4 33.5 %collective-permute-start.6 = (bf16[256,1152]{0,1:T(8,128)(2,1)S(1)}, bf16[256,1152]{0,1:T(8,128)(2,1)S(1)}, u32[]{:S(2)}, u32[]{:S(2)}) collective-permute-start(bf16[256,1152]{0,1:T(8,128)(2,1)S(1)} %broadcast_dynamic-update-slice_fusion), channel_id=1, source_target_pairs={{0,16},{8,24},{16,32},{24,40},{32,48},{40,56},{48,64},{56,72},{64,... | collective-permute-start | bytes 1769480 | tf_op jit(solution)/shard_map/ppermute | solution.py:19
  62.1 3.8 %collective-permute-start.4 = (f32[256]{0:T(256)S(1)}, f32[256]{0:T(256)S(1)}, u32[]{:S(2)}, u32[]{:S(2)}) collective-permute-start(f32[256]{0:T(256)S(1)} %add.108), channel_id=1, source_target_pairs={{0,2},{1,3},{2,0},{3,1},{4,6},{5,7},{6,4},{7,5},{8,10},{9,11},{10,... | collective-permute-start | bytes 3080 | tf_op jit(solution)/shard_map/ppermute | solution.py:89
  63.9 7.2 %copy-start.7 = (f32[1024]{0:T(1024)S(1)}, f32[1024]{0:T(1024)}, u32[]{:S(2)}) copy-start(f32[1024]{0:T(1024)} %param.15) | copy-start | bytes 12292
  66.0 5.1 %collective-permute-start.5 = (f32[256]{0:T(256)S(1)}, f32[256]{0:T(256)S(1)}, u32[]{:S(2)}, u32[]{:S(2)}) collective-permute-start(f32[256]{0:T(256)S(1)} %add.109), channel_id=1, source_target_pairs={{0,4},{1,5},{2,6},{3,7},{4,0},{5,1},{6,2},{7,3},{8,12},{9,13},{10,... | collective-permute-start | bytes 3080 | tf_op jit(solution)/shard_map/ppermute | solution.py:89

commit v6 on v4

--- a/solution.py
+++ b/solution.py
@@ -50,7 +50,7 @@
     )(reversed_taps)
 
 
-def causal_filter(extended, filter_taps, reach_back, out_rows):
+def causal_filter(extended, filter_taps, reach_back, out_rows, between):
     groups, taps = filter_taps.shape
     channels = extended.shape[1]
     width = channels // groups
@@ -68,6 +68,8 @@
     extended = jnp.concatenate([extended, jnp.zeros((1, channels), extended.dtype)], axis=0)
     results = []
     for block_index in range(out_rows // taps):
+        if block_index == 1:
+            extended = between(results[0], extended)
         first = block_index * taps
         sources = extended[first : first + span].reshape(span, groups, width)
         limits = reach_back[first : first + taps]
@@ -140,24 +142,50 @@
     window = key_rows.shape[0]
     key_pos = anchor - tok_rows + jnp.arange(window, dtype=jnp.int32)
     scale = jnp.float32(1.0 / HEAD_DIM**0.5)
-    extended = jnp.concatenate([rim_rows, mixed_rows], axis=0)
-    filtered = causal_filter(extended, filter_taps, positions - doc_begin, tok_rows)
-    hidden = residual.astype(jnp.float32) + hyena_gate.astype(jnp.float32) * filtered
-    local_sum = jnp.sum(hidden * hidden, axis=1)
-    local_sum, later_query = lax.optimization_barrier((local_sum, later_query))
     far_pos = positions + 2 * tok_rows
     far_begin = document_begin(doc_lengths, far_pos)
     far_visible = (key_pos[None, :] <= far_pos[:, None]) & (key_pos[None, :] >= far_begin[:, None])
-    far_sum, far_top, far_den = attend_block(later_query, key_rows, value_rows, far_visible, scale)
-    far_stats = jnp.concatenate([far_top, far_den], axis=1)
-    far_packet = (far_sum.astype(jnp.bfloat16), far_stats)
-    far_packet, local_sum, near_query = lax.optimization_barrier((far_packet, local_sum, att_query))
-    far_sum, far_stats = shifted(far_packet, "ctx", 2)
+    held = {}
+
+    def far_part(first_rows, extended):
+        first_rows, queries = lax.optimization_barrier((first_rows, later_query))
+        far_sum, far_top, far_den = attend_block(queries, key_rows, value_rows, far_visible, scale)
+        far_stats = jnp.concatenate([far_top, far_den], axis=1)
+        stat_cols = far_stats.shape[1]
+        stat_high = far_stats.astype(jnp.bfloat16)
+        stat_rest = far_stats - stat_high.astype(jnp.float32)
+        stat_mid = stat_rest.astype(jnp.bfloat16)
+        stat_low = (stat_rest - stat_mid.astype(jnp.float32)).astype(jnp.bfloat16)
+        stat_pad = jnp.zeros((tok_rows, 128 - 3 * stat_cols), jnp.bfloat16)
+        far_packet = jnp.concatenate(
+            [far_sum.astype(jnp.bfloat16).reshape(tok_rows, -1), stat_high, stat_mid, stat_low, stat_pad],
+            axis=1,
+        )
+        far_packet, extended, held["query"] = lax.optimization_barrier(
+            (far_packet, extended, att_query)
+        )
+        held["packet"] = shifted(far_packet, "ctx", 2)
+        held["shape"] = far_sum.shape
+        held["stat_cols"] = stat_cols
+        return extended
+
+    extended = jnp.concatenate([rim_rows, mixed_rows], axis=0)
+    filtered = causal_filter(extended, filter_taps, positions - doc_begin, tok_rows, far_part)
+    hidden = residual.astype(jnp.float32) + hyena_gate.astype(jnp.float32) * filtered
+    local_sum = jnp.sum(hidden * hidden, axis=1)
     mean_square = tp_sum(local_sum) / D
     normed = (hidden * lax.rsqrt(mean_square + norm_epsilon)[:, None] * norm_gain[None, :]).astype(
         jnp.bfloat16
     )
-    head_count = far_top.shape[1]
+    far_packet, near_query, stat_cols = held["packet"], held["query"], held["stat_cols"]
+    sum_shape = held["shape"]
+    sum_cols = sum_shape[1] * sum_shape[2]
+    far_sum = far_packet[:, :sum_cols].reshape(sum_shape)
+    stat_parts = far_packet[:, sum_cols : sum_cols + 3 * stat_cols].astype(jnp.float32)
+    far_stats = stat_parts[:, :stat_cols] + (
+        stat_parts[:, stat_cols : 2 * stat_cols] + stat_parts[:, 2 * stat_cols :]
+    )
+    head_count = sum_shape[1]
     far_top, far_den = far_stats[:, :head_count], far_stats[:, head_count:]
     visible = (key_pos[None, :] <= positions[:, None]) & (key_pos[None, :] >= doc_begin[:, None])
     near_sum, near_top, near_den = attend_block(near_query, key_rows, value_rows, visible, scale)

time: 95.2 us -> 107 us (1.12)
  the two profiles are of different devices: /device:TPU:59 before, /device:TPU:24 now
where the time goes in v6:
time: 107 us; the launch traced here: 106 us
  waiting for transfers between devices  29.5 us (28%)
  matrix products  27.7 us (26%)
  starting transfers between devices  19.8 us (19%)
  local copies, waits for them, and re-layouts  11.2 us (10%)
  other arithmetic  9.72 us (9%)
  Pallas kernels  6.73 us (6%)
    ppermute x4, waiting for transfers between devices, shifted(): lax.ppermute(value, axis, [(source, source + steps) for source in range(f...  28.7 us
    ppermute x4, starting transfers between devices, shifted(): lax.ppermute(value, axis, [(source, source + steps) for source in range(f...  15.1 us
    dot_general x2, matrix products, causal_filter(): lax.dot_general(sources, kernel_lower, numbers, preferred_element_type=jn...  14.1 us
    pallas_call x1, Pallas kernels, build_toeplitz(): pl.pallas_call(toeplitz_rows, grid=(groups // step,), in_specs=[pl.BlockS...  6.73 us
    dot_general x2, matrix products, causal_filter(): lax.dot_general(sources, kernel_upper, numbers, preferred_element_type=jn...  5.88 us
    unnamed x22, local copies, waits for them, and re-layouts  5.45 us
    ppermute x3, starting transfers between devices, tp_sum(): lax.ppermute(value, 'tp', [(i, i ^ stride) for i in range(count)])  4.66 us
    dot_general x2, matrix products, attend_block(): jnp.einsum('qhd,khd->hqk', query_heads, key_heads, preferred_element_type...  4.47 us
  transfers between devices with their start and end apart: 7, of which 3 were waited for; matrix products, arithmetic and copies ran while one was open for 18% of the time, Pallas kernels for 6%

profile of v6, /device:TPU:24, one launch (start us, length us, event | category | flops | bytes accessed | tf_op | source)
XLA Modules:
  0.0 105.7 jit_solution(7117075195241472997)
XLA Ops:
  0.7 1.4 %multiply_convert_fusion.1 = bf16[256,1024]{1,0:T(8,128)(2,1)S(1)} fusion(bf16[256,1024]{1,0:T(8,128)(2,1)} %param.13, bf16[256,1024]{1,0:T(8,128)(2,1)} %param.12), kind=kLoop, calls=%fused_computation.46 | loop fusion | flops 1048576 | bytes 1572864 | tf_op jit(solution)/shard_map/convert_element_type | solution.py:133
  2.1 3.8 %collective-permute-start = (bf16[127,1024]{1,0:T(8,128)(2,1)S(1)}, bf16[127,1024]{1,0:T(8,128)(2,1)S(1)}, u32[]{:S(2)}, u32[]{:S(2)}) collective-permute-start(bf16[127,1024]{1,0:T(8,128)(2,1)S(1)} %slice.56), channel_id=1, source_target_pairs={{0,8},{8,16},{16,24},{24,32},{32,40},{40,48},{48,56},{56,64},{64,7... | collective-permute-start | bytes 780296 | tf_op jit(solution)/shard_map/ppermute | solution.py:19
  6.0 7.5 %collective-permute-start.2 = (bf16[256,1024]{1,0:T(8,128)(2,1)}, bf16[256,1024]{1,0:T(8,128)(2,1)}, u32[]{:S(2)}, u32[]{:S(2)}) collective-permute-start(bf16[256,1024]{1,0:T(8,128)(2,1)} %param.16), channel_id=1, source_target_pairs={{16,0},{24,8},{32,16},{40,24},{48,32},{56,40},{64,48},{72,56},{80,... | collective-permute-start | bytes 1572872 | tf_op jit(solution)/shard_map/ppermute | solution.py:19
  13.5 1.2 %copy.35 = bf16[256,1024]{0,1:T(8,128)(2,1)S(1)} copy(bf16[256,1024]{1,0:T(8,128)(2,1)} %param.17) | data formatting | bytes 1048576 | tf_op args[7]
  14.7 1.2 %copy.36 = bf16[256,1024]{0,1:T(8,128)(2,1)S(1)} copy(bf16[256,1024]{1,0:T(8,128)(2,1)} %param.18) | data formatting | bytes 1048576 | tf_op args[8]
  16.0 1.1 %pad_maximum_fusion = bf16[2,256,1024]{1,2,0:T(8,128)(2,1)} fusion(bf16[1,256,1024]{1,2,0:T(8,128)(2,1)S(1)} %bitcast.70, bf16[1,256,1024]{1,2,0:T(8,128)(2,1)S(1)} %bitcast.66), kind=kLoop, calls=%fused_computation.37 | loop fusion | flops 524288 | bytes 2097152 | tf_op jit(solution)/shard_map/stack | solution.py:137
  17.1 1.9 %collective-permute-start.1 = (bf16[2,256,1024]{1,2,0:T(8,128)(2,1)}, bf16[2,256,1024]{1,2,0:T(8,128)(2,1)}, u32[]{:S(2)}, u32[]{:S(2)}) collective-permute-start(bf16[2,256,1024]{1,2,0:T(8,128)(2,1)} %pad_maximum_fusion), channel_id=1, source_target_pairs={{0,8},{8,16},{16,24},{24,32},{32,40},{40,48},{48,56},{56,64},{64,7... | collective-permute-start | bytes 3145736 | tf_op jit(solution)/shard_map/ppermute | solution.py:19
  20.5 6.7 %shard_map.113 = f32[64,128,256]{2,1,0:T(8,128)} custom-call(f32[64,256]{1,0:T(8,128)} %concatenate.36.reversed_ref), custom_call_target="tpu_custom_call" | custom-call | tf_op jit(solution)/shard_map/pallas_call | solution.py:44
  27.9 7.1 %fusion.4 = f32[64,16,128]{2,1,0:T(8,128)S(1)} fusion(bf16[256,64,16]{0,2,1:T(8,128)(2,1)S(1)} %bitcast.64, pred[128,256]{1,0:T(8,128)(4,1)S(1)} %get-tuple-element.28, f32[64,128,256]{2,1,0:T(8,128)} %shard_map.113), kind=kOutput, calls=%fused_computation.9 | convolution fusion | flops 77594624 | bytes 9469952 | tf_op jit(solution)/shard_map/dot_general | solution.py:80
  36.0 1.2 %fusion.40 = f32[64,16,128]{2,1,0:T(8,128)S(1)} fusion(f32[64,16,128]{2,1,0:T(8,128)S(1)} %fusion.4, bf16[256,64,16]{0,2,1:T(8,128)(2,1)S(1)} %bitcast.65, pred[128,256]{1,0:T(8,128)(4,1)S(1)} %get-tuple-element.28, f32[64,128,256]{2,1,0:T(8,128)S(1)} %copy-done), kind=kOutput, calls=%fused_computation.35 | convolution fusion | flops 71434240 | bytes 9994240 | tf_op jit(solution)/shard_map/dot_general | solution.py:79
  37.7 8.0 %collective-permute-done.1 = bf16[2,256,1024]{1,2,0:T(8,128)(2,1)} collective-permute-done((bf16[2,256,1024]{1,2,0:T(8,128)(2,1)}, bf16[2,256,1024]{1,2,0:T(8,128)(2,1)}, u32[]{:S(2)}, u32[]{:S(2)}) %collective-permute-start.1) | collective-permute-done | bytes 1048608 | tf_op jit(solution)/shard_map/ppermute | solution.py:19
  45.8 2.1 %fusion.83 = (bf16[1,256,1024]{1,2,0:T(8,128)(2,1)}, bf16[1,256,1024]{1,2,0:T(8,128)(2,1)S(1)}) fusion(bf16[2,256,1024]{1,2,0:T(8,128)(2,1)} %collective-permute-done.1), kind=kLoop, calls=%fused_computation.106 | loop fusion | bytes 2097152 | tf_op jit(solution)/shard_map/slice | solution.py:141
  48.8 2.2 %fusion.12 = (f32[8,256]{1,0:T(8,128)S(1)}, f32[8,256,512]{2,1,0:T(8,128)S(1)}) fusion(pred[256,512]{1,0:T(8,128)(4,1)S(1)} %get-tuple-element.24, bf16[256,8,128]{2,0,1:T(8,128)(2,1)S(1)} %copy.40, bf16[256,8,128]{2,0,1:T(8,128)(2,1)} %copy.39, bf16[256,1024]{1,0:T(8,128)(2,1)} %collective-permute-done.2), kind=kOutput, calls=%fused_computation.17 | convolution fusion | flops 273676288 | bytes 5906432 | tf_op jit(solution)/shard_map/qhd,khd->hqk/dot_general | solution.py:102
  51.0 1.6 %fusion.14 = f32[8,256]{1,0:T(8,128)S(1)} fusion(f32[8,256,512]{2,1,0:T(8,128)S(1)} %get-tuple-element.30, f32[8,256]{1,0:T(8,128)S(1)} %get-tuple-element.29, pred[256,512]{1,0:T(8,128)(4,1)S(1)} %get-tuple-element.24), kind=kLoop, calls=%fused_computation.19 | loop fusion | flops 5240832 | bytes 4341760 | tf_op jit(solution)/shard_map/reduce_sum | solution.py:108
  52.6 1.6 %fusion.37 = bf16[8,128,256]{2,1,0:T(8,128)(2,1)S(1)} fusion(f32[8,256,512]{2,1,0:T(8,128)S(1)} %get-tuple-element.30, f32[8,256]{1,0:T(8,128)S(1)} %get-tuple-element.29, pred[256,512]{1,0:T(8,128)(4,1)S(1)} %get-tuple-element.24, bf16[256,8,128]{0,2,1:T(8,128)(2,1)S(1)} %bitcast.71, bf16[256,8,128]{0,2,1:T(8,128)(2,1)S(1)} %bitcast.77), kind=kOutput, calls=%fused_computation.34 | convolution fusion | flops 276037632 | bytes 5906432 | tf_op jit(solution)/shard_map/hqk,khd->qhd/dot_general | solution.py:109
  57.7 7.0 %fusion = f32[64,16,128]{2,1,0:T(8,128)S(1)} fusion(bf16[256,64,16]{0,2,1:T(8,128)(2,1)S(1)} %bitcast.62, pred[128,256]{1,0:T(8,128)(4,1)S(1)} %get-tuple-element.27, f32[64,128,256]{2,1,0:T(8,128)} %shard_map.113), kind=kOutput, calls=%fused_computation.3 | convolution fusion | flops 77594624 | bytes 9469952 | tf_op jit(solution)/shard_map/dot_general | solution.py:80
  64.7 4.7 %fusion.43 = f32[64,16,128]{2,1,0:T(8,128)S(1)} fusion(f32[64,16,128]{2,1,0:T(8,128)S(1)} %fusion, bf16[256,64,16]{0,2,1:T(8,128)(2,1)S(1)} %bitcast.63, pred[128,256]{1,0:T(8,128)(4,1)S(1)} %get-tuple-element.27, f32[64,128,256]{2,1,0:T(8,128)} %shard_map.113), kind=kOutput, calls=%fused_computation.36 | convolution fusion | flops 71434240 | bytes 9994240 | tf_op jit(solution)/shard_map/dot_general | solution.py:79
  70.0 1.9 %collective-permute-start.6 = (bf16[256,1152]{0,1:T(8,128)(2,1)}, bf16[256,1152]{0,1:T(8,128)(2,1)S(1)}, u32[]{:S(2)}, u32[]{:S(2)}) collective-permute-start(bf16[256,1152]{0,1:T(8,128)(2,1)} %broadcast_dynamic-update-slice_fusion), channel_id=1, source_target_pairs={{0,16},{8,24},{16,32},{24,40},{32,48},{40,56},{48,64},{56,72},{64,... | collective-permute-start | bytes 1769480 | tf_op jit(solution)/shard_map/ppermute | solution.py:19
  71.9 1.8 %collective-permute-start.4 = (f32[256]{0:T(256)S(1)}, f32[256]{0:T(256)S(1)}, u32[]{:S(2)}, u32[]{:S(2)}) collective-permute-start(f32[256]{0:T(256)S(1)} %add.106), channel_id=1, source_target_pairs={{0,2},{1,3},{2,0},{3,1},{4,6},{5,7},{6,4},{7,5},{8,10},{9,11},{10,... | collective-permute-start | bytes 3080 | tf_op jit(solution)/shard_map/ppermute | solution.py:91
  73.7 2.3 %fusion.13 = (f32[8,256]{1,0:T(8,128)S(1)}, f32[8,256,512]{2,1,0:T(8,128)S(1)}) fusion(pred[256,512]{1,0:T(8,128)(4,1)S(1)} %get-tuple-element.23, bf16[256,8,128]{2,0,1:T(8,128)(2,1)} %copy-done.3, bf16[256,8,128]{2,0,1:T(8,128)(2,1)} %copy.39, bf16[256,1024]{1,0:T(8,128)(2,1)} %param.16), kind=kOutput, calls=%fused_computation.18 | convolution fusion | flops 273676288 | bytes 5906432 | tf_op jit(solution)/shard_map/qhd,khd->hqk/dot_general | solution.py:102
  76.0 2.8 %collective-permute-start.5 = (f32[256]{0:T(256)S(1)}, f32[256]{0:T(256)S(1)}, u32[]{:S(2)}, u32[]{:S(2)}) collective-permute-start(f32[256]{0:T(256)S(1)} %add.107), channel_id=1, source_target_pairs={{0,4},{1,5},{2,6},{3,7},{4,0},{5,1},{6,2},{7,3},{8,12},{9,13},{10,... | collective-permute-start | bytes 3080 | tf_op jit(solution)/shard_map/ppermute | solution.py:91
  78.9 1.5 %fusion.16 = f32[8,256]{1,0:T(8,128)S(1)} fusion(f32[8,256,512]{2,1,0:T(8,128)S(1)} %get-tuple-element.32, f32[8,256]{1,0:T(8,128)S(1)} %get-tuple-element.31, pred[256,512]{1,0:T(8,128)(4,1)S(1)} %get-tuple-element.23), kind=kLoop, calls=%fused_computation.21 | loop fusion | flops 5240832 | bytes 4341760 | tf_op jit(solution)/shard_map/reduce_sum | solution.py:108
  82.2 20.6 %collective-permute-done.6 = bf16[256,1152]{0,1:T(8,128)(2,1)S(1)} collective-permute-done((bf16[256,1152]{0,1:T(8,128)(2,1)}, bf16[256,1152]{0,1:T(8,128)(2,1)S(1)}, u32[]{:S(2)}, u32[]{:S(2)}) %collective-permute-start.6) | collective-permute-done | bytes 589856 | tf_op jit(solution)/shard_map/ppermute | solution.py:19
  103.0 1.7 %divide_convert_fusion = bf16[256,8,128]{0,2,1:T(8,128)(2,1)S(1)} fusion(bf16[256,8,128]{0,2,1:T(8,128)(2,1)S(1)} %bitcast.74, f32[8,256,512]{2,1,0:T(8,128)S(1)} %get-tuple-element.32, f32[8,256]{1,0:T(8,128)S(1)} %get-tuple-element.31, pred[256,512]{1,0:T(8,128)(4,1)S(1)} %get-tuple-element.23, bf16[256,8,128]{0,2,1:T(8,128)(2,1)S(1)} %bitcast.72, ...), kind=kOutput, calls=%fused_computation.43 | convolution fusion | flops 277348352 | bytes 6455296 | tf_op jit(solution)/shard_map/hqk,khd->qhd/dot_general | solution.py:109
  (61 shorter events, 11.7 us)
Async XLA Ops:
  0.6 18.4 %copy-start.8 = (s32[32]{0:T(128)S(1)}, s32[32]{0:T(128)}, u32[]{:S(2)}) copy-start(s32[32]{0:T(128)} %param.19) | copy-start | bytes 388
  0.6 18.8 %copy-start.6 = (f32[64,128]{1,0:T(8,128)S(1)}, f32[64,128]{1,0:T(8,128)}, u32[]{:S(2)}) copy-start(f32[64,128]{1,0:T(8,128)} %param.14) | copy-start | bytes 98308
  2.1 25.5 %collective-permute-start = (bf16[127,1024]{1,0:T(8,128)(2,1)S(1)}, bf16[127,1024]{1,0:T(8,128)(2,1)S(1)}, u32[]{:S(2)}, u32[]{:S(2)}) collective-permute-start(bf16[127,1024]{1,0:T(8,128)(2,1)S(1)} %slice.56), channel_id=1, source_target_pairs={{0,8},{8,16},{16,24},{24,32},{32,40},{40,48},{48,56},{56,64},{64,7... | collective-permute-start | bytes 780296 | tf_op jit(solution)/shard_map/ppermute | solution.py:19
  6.0 31.8 %collective-permute-start.2 = (bf16[256,1024]{1,0:T(8,128)(2,1)}, bf16[256,1024]{1,0:T(8,128)(2,1)}, u32[]{:S(2)}, u32[]{:S(2)}) collective-permute-start(bf16[256,1024]{1,0:T(8,128)(2,1)} %param.16), channel_id=1, source_target_pairs={{16,0},{24,8},{32,16},{40,24},{48,32},{56,40},{64,48},{72,56},{80,... | collective-permute-start | bytes 1572872 | tf_op jit(solution)/shard_map/ppermute | solution.py:19
  17.1 28.6 %collective-permute-start.1 = (bf16[2,256,1024]{1,2,0:T(8,128)(2,1)}, bf16[2,256,1024]{1,2,0:T(8,128)(2,1)}, u32[]{:S(2)}, u32[]{:S(2)}) collective-permute-start(bf16[2,256,1024]{1,2,0:T(8,128)(2,1)} %pad_maximum_fusion), channel_id=1, source_target_pairs={{0,8},{8,16},{16,24},{24,32},{32,40},{40,48},{48,56},{56,64},{64,7... | collective-permute-start | bytes 3145736 | tf_op jit(solution)/shard_map/ppermute | solution.py:19
  19.8 29.0 %copy-start.3 = (bf16[256,8,128]{2,0,1:T(8,128)(2,1)}, bf16[256,8,128]{2,0,1:T(8,128)(2,1)S(1)}, u32[]{:S(2)}) copy-start(bf16[256,8,128]{2,0,1:T(8,128)(2,1)S(1)} %copy.40) | copy-start | bytes 1572868
  27.9 8.2 %copy-start = (f32[64,128,256]{2,1,0:T(8,128)S(1)}, f32[64,128,256]{2,1,0:T(8,128)}, u32[]{:S(2)}) copy-start(f32[64,128,256]{2,1,0:T(8,128)} %shard_map.113) | copy-start | bytes 25165828
  48.8 3.7 %copy-start.4 = (bf16[1,256,1024]{1,2,0:T(8,128)(2,1)S(1)}, bf16[1,256,1024]{1,2,0:T(8,128)(2,1)}, u32[]{:S(2)}) copy-start(bf16[1,256,1024]{1,2,0:T(8,128)(2,1)} %get-tuple-element.21) | copy-start | bytes 1572868
  64.7 4.9 %copy-start.1 = (bf16[256,1024]{1,0:T(8,128)(2,1)S(1)}, bf16[256,1024]{1,0:T(8,128)(2,1)}, u32[]{:S(2)}) copy-start(bf16[256,1024]{1,0:T(8,128)(2,1)} %param.11) | copy-start | bytes 1572868
  64.7 4.9 %copy-start.2 = (bf16[256,1024]{1,0:T(8,128)(2,1)S(1)}, bf16[256,1024]{1,0:T(8,128)(2,1)}, u32[]{:S(2)}) copy-start(bf16[256,1024]{1,0:T(8,128)(2,1)} %param.10) | copy-start | bytes 1572868
  69.9 2.0 %collective-permute-start.3 = (f32[256]{0:T(256)S(1)}, f32[256]{0:T(256)S(1)}, u32[]{:S(2)}, u32[]{:S(2)}) collective-permute-start(f32[256]{0:T(256)S(1)} %multiply_reduce_fusion), channel_id=1, source_target_pairs={{0,1},{1,0},{2,3},{3,2},{4,5},{5,4},{6,7},{7,6},{8,9},{9,8},{10,11... | collective-permute-start | bytes 3080 | tf_op jit(solution)/shard_map/ppermute | solution.py:91
  70.0 32.9 %collective-permute-start.6 = (bf16[256,1152]{0,1:T(8,128)(2,1)}, bf16[256,1152]{0,1:T(8,128)(2,1)S(1)}, u32[]{:S(2)}, u32[]{:S(2)}) collective-permute-start(bf16[256,1152]{0,1:T(8,128)(2,1)} %broadcast_dynamic-update-slice_fusion), channel_id=1, source_target_pairs={{0,16},{8,24},{16,32},{24,40},{32,48},{40,56},{48,64},{56,72},{64,... | collective-permute-start | bytes 1769480 | tf_op jit(solution)/shard_map/ppermute | solution.py:19
  71.9 4.1 %collective-permute-start.4 = (f32[256]{0:T(256)S(1)}, f32[256]{0:T(256)S(1)}, u32[]{:S(2)}, u32[]{:S(2)}) collective-permute-start(f32[256]{0:T(256)S(1)} %add.106), channel_id=1, source_target_pairs={{0,2},{1,3},{2,0},{3,1},{4,6},{5,7},{6,4},{7,5},{8,10},{9,11},{10,... | collective-permute-start | bytes 3080 | tf_op jit(solution)/shard_map/ppermute | solution.py:91
  73.7 7.5 %copy-start.7 = (f32[1024]{0:T(1024)S(1)}, f32[1024]{0:T(1024)}, u32[]{:S(2)}) copy-start(f32[1024]{0:T(1024)} %param.15) | copy-start | bytes 12292
  76.0 27.0 %copy-start.5 = (bf16[1,256,1024]{1,2,0:T(8,128)(2,1)S(1)}, bf16[1,256,1024]{1,2,0:T(8,128)(2,1)}, u32[]{:S(2)}) copy-start(bf16[1,256,1024]{1,2,0:T(8,128)(2,1)} %get-tuple-element.21) | copy-start | bytes 1572868
  76.0 5.2 %collective-permute-start.5 = (f32[256]{0:T(256)S(1)}, f32[256]{0:T(256)S(1)}, u32[]{:S(2)}, u32[]{:S(2)}) collective-permute-start(f32[256]{0:T(256)S(1)} %add.107), channel_id=1, source_target_pairs={{0,4},{1,5},{2,6},{3,7},{4,0},{5,1},{6,2},{7,3},{8,12},{9,13},{10,... | collective-permute-start | bytes 3080 | tf_op jit(solution)/shard_map/ppermute | solution.py:91

commit v7 on v6

--- a/solution.py
+++ b/solution.py
@@ -7,7 +7,6 @@
 
 D = 8192
 HEAD_DIM = 128
-REACH = 3
 
 
 norm_epsilon = 1e-05
@@ -112,7 +111,7 @@
     return summed, top[:, :, 0].T, denominator.T
 
 
-def on_device(
+def block_body(
     residual,
     hyena_gate,
     hyena_key,
@@ -213,7 +212,7 @@
         P(),
     )
     return jax.shard_map(
-        on_device,
+        block_body,
         mesh=mesh,
         in_specs=placed,
         out_specs=(P("ctx", "tp"), P("ctx", "tp")),

time: 107 us -> 107 us (level)
  no operation moved by 1% of the time
where the time goes in v7:
time: 107 us; the launch traced here: 106 us
  waiting for transfers between devices  29.5 us (28%)
  matrix products  27.7 us (26%)
  starting transfers between devices  19.8 us (19%)
  local copies, waits for them, and re-layouts  11.2 us (10%)
  other arithmetic  9.72 us (9%)
  Pallas kernels  6.73 us (6%)
    ppermute x4, waiting for transfers between devices, shifted(): lax.ppermute(value, axis, [(source, source + steps) for source in range(f...  28.7 us
    ppermute x4, starting transfers between devices, shifted(): lax.ppermute(value, axis, [(source, source + steps) for source in range(f...  15.1 us
    dot_general x2, matrix products, causal_filter(): lax.dot_general(sources, kernel_lower, numbers, preferred_element_type=jn...  14.1 us
    pallas_call x1, Pallas kernels, build_toeplitz(): pl.pallas_call(toeplitz_rows, grid=(groups // step,), in_specs=[pl.BlockS...  6.73 us
    dot_general x2, matrix products, causal_filter(): lax.dot_general(sources, kernel_upper, numbers, preferred_element_type=jn...  5.88 us
    unnamed x22, local copies, waits for them, and re-layouts  5.45 us
    ppermute x3, starting transfers between devices, tp_sum(): lax.ppermute(value, 'tp', [(i, i ^ stride) for i in range(count)])  4.66 us
    dot_general x2, matrix products, attend_block(): jnp.einsum('qhd,khd->hqk', query_heads, key_heads, preferred_element_type...  4.47 us
  transfers between devices with their start and end apart: 7, of which 3 were waited for; matrix products, arithmetic and copies ran while one was open for 18% of the time, Pallas kernels for 6%

profile of v7, /device:TPU:24, one launch (start us, length us, event | category | flops | bytes accessed | tf_op | source)
XLA Modules:
  0.0 105.7 jit_solution(7117075195241472997)
XLA Ops:
  0.7 1.4 %multiply_convert_fusion.1 = bf16[256,1024]{1,0:T(8,128)(2,1)S(1)} fusion(bf16[256,1024]{1,0:T(8,128)(2,1)} %param.13, bf16[256,1024]{1,0:T(8,128)(2,1)} %param.12), kind=kLoop, calls=%fused_computation.46 | loop fusion | flops 1048576 | bytes 1572864 | tf_op jit(solution)/shard_map/convert_element_type | solution.py:132
  2.1 3.8 %collective-permute-start = (bf16[127,1024]{1,0:T(8,128)(2,1)S(1)}, bf16[127,1024]{1,0:T(8,128)(2,1)S(1)}, u32[]{:S(2)}, u32[]{:S(2)}) collective-permute-start(bf16[127,1024]{1,0:T(8,128)(2,1)S(1)} %slice.56), channel_id=1, source_target_pairs={{0,8},{8,16},{16,24},{24,32},{32,40},{40,48},{48,56},{56,64},{64,7... | collective-permute-start | bytes 780296 | tf_op jit(solution)/shard_map/ppermute | solution.py:18
  6.0 7.5 %collective-permute-start.2 = (bf16[256,1024]{1,0:T(8,128)(2,1)}, bf16[256,1024]{1,0:T(8,128)(2,1)}, u32[]{:S(2)}, u32[]{:S(2)}) collective-permute-start(bf16[256,1024]{1,0:T(8,128)(2,1)} %param.16), channel_id=1, source_target_pairs={{16,0},{24,8},{32,16},{40,24},{48,32},{56,40},{64,48},{72,56},{80,... | collective-permute-start | bytes 1572872 | tf_op jit(solution)/shard_map/ppermute | solution.py:18
  13.5 1.2 %copy.35 = bf16[256,1024]{0,1:T(8,128)(2,1)S(1)} copy(bf16[256,1024]{1,0:T(8,128)(2,1)} %param.17) | data formatting | bytes 1048576 | tf_op args[7]
  14.7 1.2 %copy.36 = bf16[256,1024]{0,1:T(8,128)(2,1)S(1)} copy(bf16[256,1024]{1,0:T(8,128)(2,1)} %param.18) | data formatting | bytes 1048576 | tf_op args[8]
  16.0 1.1 %pad_maximum_fusion = bf16[2,256,1024]{1,2,0:T(8,128)(2,1)} fusion(bf16[1,256,1024]{1,2,0:T(8,128)(2,1)S(1)} %bitcast.70, bf16[1,256,1024]{1,2,0:T(8,128)(2,1)S(1)} %bitcast.66), kind=kLoop, calls=%fused_computation.37 | loop fusion | flops 524288 | bytes 2097152 | tf_op jit(solution)/shard_map/stack | solution.py:136
  17.1 1.9 %collective-permute-start.1 = (bf16[2,256,1024]{1,2,0:T(8,128)(2,1)}, bf16[2,256,1024]{1,2,0:T(8,128)(2,1)}, u32[]{:S(2)}, u32[]{:S(2)}) collective-permute-start(bf16[2,256,1024]{1,2,0:T(8,128)(2,1)} %pad_maximum_fusion), channel_id=1, source_target_pairs={{0,8},{8,16},{16,24},{24,32},{32,40},{40,48},{48,56},{56,64},{64,7... | collective-permute-start | bytes 3145736 | tf_op jit(solution)/shard_map/ppermute | solution.py:18
  20.5 6.7 %shard_map.113 = f32[64,128,256]{2,1,0:T(8,128)} custom-call(f32[64,256]{1,0:T(8,128)} %concatenate.36.reversed_ref), custom_call_target="tpu_custom_call" | custom-call | tf_op jit(solution)/shard_map/pallas_call | solution.py:43
  27.9 7.1 %fusion.4 = f32[64,16,128]{2,1,0:T(8,128)S(1)} fusion(bf16[256,64,16]{0,2,1:T(8,128)(2,1)S(1)} %bitcast.64, pred[128,256]{1,0:T(8,128)(4,1)S(1)} %get-tuple-element.28, f32[64,128,256]{2,1,0:T(8,128)} %shard_map.113), kind=kOutput, calls=%fused_computation.9 | convolution fusion | flops 77594624 | bytes 9469952 | tf_op jit(solution)/shard_map/dot_general | solution.py:79
  36.0 1.2 %fusion.40 = f32[64,16,128]{2,1,0:T(8,128)S(1)} fusion(f32[64,16,128]{2,1,0:T(8,128)S(1)} %fusion.4, bf16[256,64,16]{0,2,1:T(8,128)(2,1)S(1)} %bitcast.65, pred[128,256]{1,0:T(8,128)(4,1)S(1)} %get-tuple-element.28, f32[64,128,256]{2,1,0:T(8,128)S(1)} %copy-done), kind=kOutput, calls=%fused_computation.35 | convolution fusion | flops 71434240 | bytes 9994240 | tf_op jit(solution)/shard_map/dot_general | solution.py:78
  37.7 8.0 %collective-permute-done.1 = bf16[2,256,1024]{1,2,0:T(8,128)(2,1)} collective-permute-done((bf16[2,256,1024]{1,2,0:T(8,128)(2,1)}, bf16[2,256,1024]{1,2,0:T(8,128)(2,1)}, u32[]{:S(2)}, u32[]{:S(2)}) %collective-permute-start.1) | collective-permute-done | bytes 1048608 | tf_op jit(solution)/shard_map/ppermute | solution.py:18
  45.8 2.1 %fusion.83 = (bf16[1,256,1024]{1,2,0:T(8,128)(2,1)}, bf16[1,256,1024]{1,2,0:T(8,128)(2,1)S(1)}) fusion(bf16[2,256,1024]{1,2,0:T(8,128)(2,1)} %collective-permute-done.1), kind=kLoop, calls=%fused_computation.106 | loop fusion | bytes 2097152 | tf_op jit(solution)/shard_map/slice | solution.py:140
  48.8 2.2 %fusion.12 = (f32[8,256]{1,0:T(8,128)S(1)}, f32[8,256,512]{2,1,0:T(8,128)S(1)}) fusion(pred[256,512]{1,0:T(8,128)(4,1)S(1)} %get-tuple-element.24, bf16[256,8,128]{2,0,1:T(8,128)(2,1)S(1)} %copy.40, bf16[256,8,128]{2,0,1:T(8,128)(2,1)} %copy.39, bf16[256,1024]{1,0:T(8,128)(2,1)} %collective-permute-done.2), kind=kOutput, calls=%fused_computation.17 | convolution fusion | flops 273676288 | bytes 5906432 | tf_op jit(solution)/shard_map/qhd,khd->hqk/dot_general | solution.py:101
  51.0 1.6 %fusion.14 = f32[8,256]{1,0:T(8,128)S(1)} fusion(f32[8,256,512]{2,1,0:T(8,128)S(1)} %get-tuple-element.30, f32[8,256]{1,0:T(8,128)S(1)} %get-tuple-element.29, pred[256,512]{1,0:T(8,128)(4,1)S(1)} %get-tuple-element.24), kind=kLoop, calls=%fused_computation.19 | loop fusion | flops 5240832 | bytes 4341760 | tf_op jit(solution)/shard_map/reduce_sum | solution.py:107
  52.6 1.6 %fusion.37 = bf16[8,128,256]{2,1,0:T(8,128)(2,1)S(1)} fusion(f32[8,256,512]{2,1,0:T(8,128)S(1)} %get-tuple-element.30, f32[8,256]{1,0:T(8,128)S(1)} %get-tuple-element.29, pred[256,512]{1,0:T(8,128)(4,1)S(1)} %get-tuple-element.24, bf16[256,8,128]{0,2,1:T(8,128)(2,1)S(1)} %bitcast.71, bf16[256,8,128]{0,2,1:T(8,128)(2,1)S(1)} %bitcast.77), kind=kOutput, calls=%fused_computation.34 | convolution fusion | flops 276037632 | bytes 5906432 | tf_op jit(solution)/shard_map/hqk,khd->qhd/dot_general | solution.py:108
  57.7 7.0 %fusion = f32[64,16,128]{2,1,0:T(8,128)S(1)} fusion(bf16[256,64,16]{0,2,1:T(8,128)(2,1)S(1)} %bitcast.62, pred[128,256]{1,0:T(8,128)(4,1)S(1)} %get-tuple-element.27, f32[64,128,256]{2,1,0:T(8,128)} %shard_map.113), kind=kOutput, calls=%fused_computation.3 | convolution fusion | flops 77594624 | bytes 9469952 | tf_op jit(solution)/shard_map/dot_general | solution.py:79
  64.7 4.7 %fusion.43 = f32[64,16,128]{2,1,0:T(8,128)S(1)} fusion(f32[64,16,128]{2,1,0:T(8,128)S(1)} %fusion, bf16[256,64,16]{0,2,1:T(8,128)(2,1)S(1)} %bitcast.63, pred[128,256]{1,0:T(8,128)(4,1)S(1)} %get-tuple-element.27, f32[64,128,256]{2,1,0:T(8,128)} %shard_map.113), kind=kOutput, calls=%fused_computation.36 | convolution fusion | flops 71434240 | bytes 9994240 | tf_op jit(solution)/shard_map/dot_general | solution.py:78
  70.0 1.9 %collective-permute-start.6 = (bf16[256,1152]{0,1:T(8,128)(2,1)}, bf16[256,1152]{0,1:T(8,128)(2,1)S(1)}, u32[]{:S(2)}, u32[]{:S(2)}) collective-permute-start(bf16[256,1152]{0,1:T(8,128)(2,1)} %broadcast_dynamic-update-slice_fusion), channel_id=1, source_target_pairs={{0,16},{8,24},{16,32},{24,40},{32,48},{40,56},{48,64},{56,72},{64,... | collective-permute-start | bytes 1769480 | tf_op jit(solution)/shard_map/ppermute | solution.py:18
  71.9 1.8 %collective-permute-start.4 = (f32[256]{0:T(256)S(1)}, f32[256]{0:T(256)S(1)}, u32[]{:S(2)}, u32[]{:S(2)}) collective-permute-start(f32[256]{0:T(256)S(1)} %add.106), channel_id=1, source_target_pairs={{0,2},{1,3},{2,0},{3,1},{4,6},{5,7},{6,4},{7,5},{8,10},{9,11},{10,... | collective-permute-start | bytes 3080 | tf_op jit(solution)/shard_map/ppermute | solution.py:90
  73.7 2.3 %fusion.13 = (f32[8,256]{1,0:T(8,128)S(1)}, f32[8,256,512]{2,1,0:T(8,128)S(1)}) fusion(pred[256,512]{1,0:T(8,128)(4,1)S(1)} %get-tuple-element.23, bf16[256,8,128]{2,0,1:T(8,128)(2,1)} %copy-done.3, bf16[256,8,128]{2,0,1:T(8,128)(2,1)} %copy.39, bf16[256,1024]{1,0:T(8,128)(2,1)} %param.16), kind=kOutput, calls=%fused_computation.18 | convolution fusion | flops 273676288 | bytes 5906432 | tf_op jit(solution)/shard_map/qhd,khd->hqk/dot_general | solution.py:101
  76.0 2.8 %collective-permute-start.5 = (f32[256]{0:T(256)S(1)}, f32[256]{0:T(256)S(1)}, u32[]{:S(2)}, u32[]{:S(2)}) collective-permute-start(f32[256]{0:T(256)S(1)} %add.107), channel_id=1, source_target_pairs={{0,4},{1,5},{2,6},{3,7},{4,0},{5,1},{6,2},{7,3},{8,12},{9,13},{10,... | collective-permute-start | bytes 3080 | tf_op jit(solution)/shard_map/ppermute | solution.py:90
  78.9 1.5 %fusion.16 = f32[8,256]{1,0:T(8,128)S(1)} fusion(f32[8,256,512]{2,1,0:T(8,128)S(1)} %get-tuple-element.32, f32[8,256]{1,0:T(8,128)S(1)} %get-tuple-element.31, pred[256,512]{1,0:T(8,128)(4,1)S(1)} %get-tuple-element.23), kind=kLoop, calls=%fused_computation.21 | loop fusion | flops 5240832 | bytes 4341760 | tf_op jit(solution)/shard_map/reduce_sum | solution.py:107
  82.2 20.6 %collective-permute-done.6 = bf16[256,1152]{0,1:T(8,128)(2,1)S(1)} collective-permute-done((bf16[256,1152]{0,1:T(8,128)(2,1)}, bf16[256,1152]{0,1:T(8,128)(2,1)S(1)}, u32[]{:S(2)}, u32[]{:S(2)}) %collective-permute-start.6) | collective-permute-done | bytes 589856 | tf_op jit(solution)/shard_map/ppermute | solution.py:18
  103.0 1.7 %divide_convert_fusion = bf16[256,8,128]{0,2,1:T(8,128)(2,1)S(1)} fusion(bf16[256,8,128]{0,2,1:T(8,128)(2,1)S(1)} %bitcast.74, f32[8,256,512]{2,1,0:T(8,128)S(1)} %get-tuple-element.32, f32[8,256]{1,0:T(8,128)S(1)} %get-tuple-element.31, pred[256,512]{1,0:T(8,128)(4,1)S(1)} %get-tuple-element.23, bf16[256,8,128]{0,2,1:T(8,128)(2,1)S(1)} %bitcast.72, ...), kind=kOutput, calls=%fused_computation.43 | convolution fusion | flops 277348352 | bytes 6455296 | tf_op jit(solution)/shard_map/hqk,khd->qhd/dot_general | solution.py:108
  (61 shorter events, 11.7 us)
Async XLA Ops:
  0.6 18.4 %copy-start.8 = (s32[32]{0:T(128)S(1)}, s32[32]{0:T(128)}, u32[]{:S(2)}) copy-start(s32[32]{0:T(128)} %param.19) | copy-start | bytes 388
  0.6 18.8 %copy-start.6 = (f32[64,128]{1,0:T(8,128)S(1)}, f32[64,128]{1,0:T(8,128)}, u32[]{:S(2)}) copy-start(f32[64,128]{1,0:T(8,128)} %param.14) | copy-start | bytes 98308
  2.1 25.5 %collective-permute-start = (bf16[127,1024]{1,0:T(8,128)(2,1)S(1)}, bf16[127,1024]{1,0:T(8,128)(2,1)S(1)}, u32[]{:S(2)}, u32[]{:S(2)}) collective-permute-start(bf16[127,1024]{1,0:T(8,128)(2,1)S(1)} %slice.56), channel_id=1, source_target_pairs={{0,8},{8,16},{16,24},{24,32},{32,40},{40,48},{48,56},{56,64},{64,7... | collective-permute-start | bytes 780296 | tf_op jit(solution)/shard_map/ppermute | solution.py:18
  6.0 31.8 %collective-permute-start.2 = (bf16[256,1024]{1,0:T(8,128)(2,1)}, bf16[256,1024]{1,0:T(8,128)(2,1)}, u32[]{:S(2)}, u32[]{:S(2)}) collective-permute-start(bf16[256,1024]{1,0:T(8,128)(2,1)} %param.16), channel_id=1, source_target_pairs={{16,0},{24,8},{32,16},{40,24},{48,32},{56,40},{64,48},{72,56},{80,... | collective-permute-start | bytes 1572872 | tf_op jit(solution)/shard_map/ppermute | solution.py:18
  17.1 28.6 %collective-permute-start.1 = (bf16[2,256,1024]{1,2,0:T(8,128)(2,1)}, bf16[2,256,1024]{1,2,0:T(8,128)(2,1)}, u32[]{:S(2)}, u32[]{:S(2)}) collective-permute-start(bf16[2,256,1024]{1,2,0:T(8,128)(2,1)} %pad_maximum_fusion), channel_id=1, source_target_pairs={{0,8},{8,16},{16,24},{24,32},{32,40},{40,48},{48,56},{56,64},{64,7... | collective-permute-start | bytes 3145736 | tf_op jit(solution)/shard_map/ppermute | solution.py:18
  19.8 29.0 %copy-start.3 = (bf16[256,8,128]{2,0,1:T(8,128)(2,1)}, bf16[256,8,128]{2,0,1:T(8,128)(2,1)S(1)}, u32[]{:S(2)}) copy-start(bf16[256,8,128]{2,0,1:T(8,128)(2,1)S(1)} %copy.40) | copy-start | bytes 1572868
  27.9 8.2 %copy-start = (f32[64,128,256]{2,1,0:T(8,128)S(1)}, f32[64,128,256]{2,1,0:T(8,128)}, u32[]{:S(2)}) copy-start(f32[64,128,256]{2,1,0:T(8,128)} %shard_map.113) | copy-start | bytes 25165828
  48.8 3.7 %copy-start.4 = (bf16[1,256,1024]{1,2,0:T(8,128)(2,1)S(1)}, bf16[1,256,1024]{1,2,0:T(8,128)(2,1)}, u32[]{:S(2)}) copy-start(bf16[1,256,1024]{1,2,0:T(8,128)(2,1)} %get-tuple-element.21) | copy-start | bytes 1572868
  64.7 4.9 %copy-start.1 = (bf16[256,1024]{1,0:T(8,128)(2,1)S(1)}, bf16[256,1024]{1,0:T(8,128)(2,1)}, u32[]{:S(2)}) copy-start(bf16[256,1024]{1,0:T(8,128)(2,1)} %param.11) | copy-start | bytes 1572868
  64.7 4.9 %copy-start.2 = (bf16[256,1024]{1,0:T(8,128)(2,1)S(1)}, bf16[256,1024]{1,0:T(8,128)(2,1)}, u32[]{:S(2)}) copy-start(bf16[256,1024]{1,0:T(8,128)(2,1)} %param.10) | copy-start | bytes 1572868
  69.9 2.0 %collective-permute-start.3 = (f32[256]{0:T(256)S(1)}, f32[256]{0:T(256)S(1)}, u32[]{:S(2)}, u32[]{:S(2)}) collective-permute-start(f32[256]{0:T(256)S(1)} %multiply_reduce_fusion), channel_id=1, source_target_pairs={{0,1},{1,0},{2,3},{3,2},{4,5},{5,4},{6,7},{7,6},{8,9},{9,8},{10,11... | collective-permute-start | bytes 3080 | tf_op jit(solution)/shard_map/ppermute | solution.py:90
  70.0 32.9 %collective-permute-start.6 = (bf16[256,1152]{0,1:T(8,128)(2,1)}, bf16[256,1152]{0,1:T(8,128)(2,1)S(1)}, u32[]{:S(2)}, u32[]{:S(2)}) collective-permute-start(bf16[256,1152]{0,1:T(8,128)(2,1)} %broadcast_dynamic-update-slice_fusion), channel_id=1, source_target_pairs={{0,16},{8,24},{16,32},{24,40},{32,48},{40,56},{48,64},{56,72},{64,... | collective-permute-start | bytes 1769480 | tf_op jit(solution)/shard_map/ppermute | solution.py:18
  71.9 4.1 %collective-permute-start.4 = (f32[256]{0:T(256)S(1)}, f32[256]{0:T(256)S(1)}, u32[]{:S(2)}, u32[]{:S(2)}) collective-permute-start(f32[256]{0:T(256)S(1)} %add.106), channel_id=1, source_target_pairs={{0,2},{1,3},{2,0},{3,1},{4,6},{5,7},{6,4},{7,5},{8,10},{9,11},{10,... | collective-permute-start | bytes 3080 | tf_op jit(solution)/shard_map/ppermute | solution.py:90
  73.7 7.5 %copy-start.7 = (f32[1024]{0:T(1024)S(1)}, f32[1024]{0:T(1024)}, u32[]{:S(2)}) copy-start(f32[1024]{0:T(1024)} %param.15) | copy-start | bytes 12292
  76.0 27.0 %copy-start.5 = (bf16[1,256,1024]{1,2,0:T(8,128)(2,1)S(1)}, bf16[1,256,1024]{1,2,0:T(8,128)(2,1)}, u32[]{:S(2)}) copy-start(bf16[1,256,1024]{1,2,0:T(8,128)(2,1)} %get-tuple-element.21) | copy-start | bytes 1572868
  76.0 5.2 %collective-permute-start.5 = (f32[256]{0:T(256)S(1)}, f32[256]{0:T(256)S(1)}, u32[]{:S(2)}, u32[]{:S(2)}) collective-permute-start(f32[256]{0:T(256)S(1)} %add.107), channel_id=1, source_target_pairs={{0,4},{1,5},{2,6},{3,7},{4,0},{5,1},{6,2},{7,3},{8,12},{9,13},{10,... | collective-permute-start | bytes 3080 | tf_op jit(solution)/shard_map/ppermute | solution.py:90

commit v8 on v7

--- a/solution.py
+++ b/solution.py
@@ -145,9 +145,13 @@
     far_begin = document_begin(doc_lengths, far_pos)
     far_visible = (key_pos[None, :] <= far_pos[:, None]) & (key_pos[None, :] >= far_begin[:, None])
     held = {}
+    visible = (key_pos[None, :] <= positions[:, None]) & (key_pos[None, :] >= doc_begin[:, None])
+    near_sum, near_top, near_den = attend_block(att_query, key_rows, value_rows, visible, scale)
 
     def far_part(first_rows, extended):
-        first_rows, queries = lax.optimization_barrier((first_rows, later_query))
+        first_rows, queries, held["near"] = lax.optimization_barrier(
+            (first_rows, later_query, (near_sum, near_top, near_den))
+        )
         far_sum, far_top, far_den = attend_block(queries, key_rows, value_rows, far_visible, scale)
         far_stats = jnp.concatenate([far_top, far_den], axis=1)
         stat_cols = far_stats.shape[1]
@@ -160,9 +164,7 @@
             [far_sum.astype(jnp.bfloat16).reshape(tok_rows, -1), stat_high, stat_mid, stat_low, stat_pad],
             axis=1,
         )
-        far_packet, extended, held["query"] = lax.optimization_barrier(
-            (far_packet, extended, att_query)
-        )
+        far_packet, extended = lax.optimization_barrier((far_packet, extended))
         held["packet"] = shifted(far_packet, "ctx", 2)
         held["shape"] = far_sum.shape
         held["stat_cols"] = stat_cols
@@ -176,7 +178,8 @@
     normed = (hidden * lax.rsqrt(mean_square + norm_epsilon)[:, None] * norm_gain[None, :]).astype(
         jnp.bfloat16
     )
-    far_packet, near_query, stat_cols = held["packet"], held["query"], held["stat_cols"]
+    far_packet, stat_cols = held["packet"], held["stat_cols"]
+    near_sum, near_top, near_den = held["near"]
     sum_shape = held["shape"]
     sum_cols = sum_shape[1] * sum_shape[2]
     far_sum = far_packet[:, :sum_cols].reshape(sum_shape)
@@ -186,8 +189,6 @@
     )
     head_count = sum_shape[1]
     far_top, far_den = far_stats[:, :head_count], far_stats[:, head_count:]
-    visible = (key_pos[None, :] <= positions[:, None]) & (key_pos[None, :] >= doc_begin[:, None])
-    near_sum, near_top, near_den = attend_block(near_query, key_rows, value_rows, visible, scale)
     far_top = jnp.where(far_den > 0, far_top, jnp.float32(-1e30))
     top = jnp.maximum(near_top, far_top)
     near_scale = jnp.exp(near_top - top)

time: 107 us -> 102 us (0.953)
  waiting for transfers between devices: 29.5 us -> 27.5 us
  local copies, waits for them, and re-layouts: 11.2 us -> 9.35 us
    ppermute x4, waiting for transfers between devices: 28.7 us -> 22.2 us  [shifted(): lax.ppermute(value, axis, [(source, source + steps) for source in range(f...]
    ppermute x3, waiting for transfers between devices: 0.83 us -> 5.29 us  [tp_sum(): lax.ppermute(value, 'tp', [(i, i ^ stride) for i in range(count)])]
    unnamed x3, other arithmetic: 1.8 us -> 0.02 us
    slice x1, local copies, waits for them, and re-layouts: 2.06 us -> 0.86 us  [block_body(): value_rows = jnp.concatenate([previous[1], att_value], axis=0)]
    unnamed x22 -> x36, local copies, waits for them, and re-layouts: 5.45 us -> 5.46 us
  transfers between devices with their start and end apart: 7 -> 7, of which waited for: 3 -> 5; matrix products, arithmetic and copies ran while one was open for 18% -> 25% of each run, Pallas kernels for 6% -> 7%
where the time goes in v8:
time: 102 us; the launch traced here: 101 us
  waiting for transfers between devices  27.5 us (27%)
  matrix products  27.5 us (27%)
  starting transfers between devices  20.1 us (20%)
  local copies, waits for them, and re-layouts  9.35 us (9%)
  other arithmetic  9.34 us (9%)
  Pallas kernels  6.75 us (7%)
  between operations  1.06 us (1%)
    ppermute x4, waiting for transfers between devices, shifted(): lax.ppermute(value, axis, [(source, source + steps) for source in range(f...  22.2 us
    ppermute x4, starting transfers between devices, shifted(): lax.ppermute(value, axis, [(source, source + steps) for source in range(f...  15.5 us
    dot_general x2, matrix products, causal_filter(): lax.dot_general(sources, kernel_lower, numbers, preferred_element_type=jn...  14.1 us
    pallas_call x1, Pallas kernels, build_toeplitz(): pl.pallas_call(toeplitz_rows, grid=(groups // step,), in_specs=[pl.BlockS...  6.75 us
    dot_general x2, matrix products, causal_filter(): lax.dot_general(sources, kernel_upper, numbers, preferred_element_type=jn...  5.9 us
    unnamed x36, local copies, waits for them, and re-layouts  5.46 us
    ppermute x3, waiting for transfers between devices, tp_sum(): lax.ppermute(value, 'tp', [(i, i ^ stride) for i in range(count)])  5.29 us
    ppermute x3, starting transfers between devices, tp_sum(): lax.ppermute(value, 'tp', [(i, i ^ stride) for i in range(count)])  4.6 us
  transfers between devices with their start and end apart: 7, of which 5 were waited for; matrix products, arithmetic and copies ran while one was open for 25% of the time, Pallas kernels for 7%

profile of v8, /device:TPU:24, one launch (start us, length us, event | category | flops | bytes accessed | tf_op | source)
XLA Modules:
  0.0 101.5 jit_solution(12896475576195736894)
XLA Ops:
  0.7 1.4 %multiply_convert_fusion.1 = bf16[256,1024]{1,0:T(8,128)(2,1)S(1)} fusion(bf16[256,1024]{1,0:T(8,128)(2,1)} %param.13, bf16[256,1024]{1,0:T(8,128)(2,1)} %param.12), kind=kLoop, calls=%fused_computation.46 | loop fusion | flops 1048576 | bytes 1572864 | tf_op jit(solution)/shard_map/convert_element_type | solution.py:132
  2.1 3.8 %collective-permute-start = (bf16[127,1024]{1,0:T(8,128)(2,1)S(1)}, bf16[127,1024]{1,0:T(8,128)(2,1)S(1)}, u32[]{:S(2)}, u32[]{:S(2)}) collective-permute-start(bf16[127,1024]{1,0:T(8,128)(2,1)S(1)} %slice.56), channel_id=1, source_target_pairs={{0,8},{8,16},{16,24},{24,32},{32,40},{40,48},{48,56},{56,64},{64,7... | collective-permute-start | bytes 780296 | tf_op jit(solution)/shard_map/ppermute | solution.py:18
  6.0 7.5 %collective-permute-start.2 = (bf16[256,1024]{1,0:T(8,128)(2,1)}, bf16[256,1024]{1,0:T(8,128)(2,1)}, u32[]{:S(2)}, u32[]{:S(2)}) collective-permute-start(bf16[256,1024]{1,0:T(8,128)(2,1)} %param.16), channel_id=1, source_target_pairs={{16,0},{24,8},{32,16},{40,24},{48,32},{56,40},{64,48},{72,56},{80,... | collective-permute-start | bytes 1572872 | tf_op jit(solution)/shard_map/ppermute | solution.py:18
  13.5 1.2 %copy.41 = bf16[256,1024]{0,1:T(8,128)(2,1)S(1)} copy(bf16[256,1024]{1,0:T(8,128)(2,1)} %param.17) | data formatting | bytes 1048576 | tf_op args[7]
  14.7 1.2 %copy.42 = bf16[256,1024]{0,1:T(8,128)(2,1)S(1)} copy(bf16[256,1024]{1,0:T(8,128)(2,1)} %param.18) | data formatting | bytes 1048576 | tf_op args[8]
  16.0 1.2 %pad_maximum_fusion = bf16[2,256,1024]{1,2,0:T(8,128)(2,1)} fusion(bf16[1,256,1024]{1,2,0:T(8,128)(2,1)S(1)} %bitcast.70, bf16[1,256,1024]{1,2,0:T(8,128)(2,1)S(1)} %bitcast.66), kind=kLoop, calls=%fused_computation.35 | loop fusion | flops 524288 | bytes 2097152 | tf_op jit(solution)/shard_map/stack | solution.py:136
  17.1 1.9 %collective-permute-start.1 = (bf16[2,256,1024]{1,2,0:T(8,128)(2,1)}, bf16[2,256,1024]{1,2,0:T(8,128)(2,1)S(1)}, u32[]{:S(2)}, u32[]{:S(2)}) collective-permute-start(bf16[2,256,1024]{1,2,0:T(8,128)(2,1)} %pad_maximum_fusion), channel_id=1, source_target_pairs={{0,8},{8,16},{16,24},{24,32},{32,40},{40,48},{48,56},{56,64},{64,7... | collective-permute-start | bytes 3145736 | tf_op jit(solution)/shard_map/ppermute | solution.py:18
  21.8 6.7 %shard_map.113 = f32[64,128,256]{2,1,0:T(8,128)} custom-call(f32[64,256]{1,0:T(8,128)} %concatenate.36.reversed_ref), custom_call_target="tpu_custom_call" | custom-call | tf_op jit(solution)/shard_map/pallas_call | solution.py:43
  29.8 7.1 %fusion.4 = f32[64,16,128]{2,1,0:T(8,128)S(1)} fusion(bf16[256,64,16]{0,2,1:T(8,128)(2,1)S(1)} %bitcast.64, pred[128,256]{1,0:T(8,128)(4,1)} %get-tuple-element.32, f32[64,128,256]{2,1,0:T(8,128)} %shard_map.113), kind=kOutput, calls=%fused_computation.9 | convolution fusion | flops 77594624 | bytes 9469952 | tf_op jit(solution)/shard_map/dot_general | solution.py:79
  38.0 1.2 %fusion.34 = f32[64,16,128]{2,1,0:T(8,128)S(1)} fusion(f32[64,16,128]{2,1,0:T(8,128)S(1)} %fusion.4, bf16[256,64,16]{0,2,1:T(8,128)(2,1)S(1)} %bitcast.65, pred[128,256]{1,0:T(8,128)(4,1)S(1)} %copy-done.12, f32[64,128,256]{2,1,0:T(8,128)S(1)} %copy-done), kind=kOutput, calls=%fused_computation.33 | convolution fusion | flops 71434240 | bytes 9994240 | tf_op jit(solution)/shard_map/dot_general | solution.py:78
  39.4 1.2 %maximum_maximum_fusion = bf16[384,1024]{1,0:T(8,128)(2,1)S(1)} fusion(bf16[256,1024]{1,0:T(8,128)(2,1)S(1)} %multiply_convert_fusion.1, bf16[127,1024]{1,0:T(8,128)(2,1)} %copy-done.4, bf16[384]{0:T(512)(128)(2,1)S(1)} %pad.5.clone), kind=kLoop, calls=%fused_computation.47 | loop fusion | flops 2359296 | bytes 1571584 | tf_op jit(solution)/shard_map/concatenate | solution.py:67
  40.6 5.0 %collective-permute-done.1 = bf16[2,256,1024]{1,2,0:T(8,128)(2,1)S(1)} collective-permute-done((bf16[2,256,1024]{1,2,0:T(8,128)(2,1)}, bf16[2,256,1024]{1,2,0:T(8,128)(2,1)S(1)}, u32[]{:S(2)}, u32[]{:S(2)}) %collective-permute-start.1) | collective-permute-done | bytes 1048608 | tf_op jit(solution)/shard_map/ppermute | solution.py:18
  46.8 2.1 %fusion.13 = (f32[8,256]{1,0:T(8,128)S(1)}, f32[8,512,256]{2,1,0:T(8,128)S(1)}) fusion(pred[256,512]{0,1:T(8,128)(4,1)} %get-tuple-element.28, bf16[256,8,128]{2,0,1:T(8,128)(2,1)} %copy.46, bf16[256,8,128]{2,0,1:T(8,128)(2,1)S(1)} %copy.45, bf16[256,1024]{1,0:T(8,128)(2,1)} %param.16), kind=kOutput, calls=%fused_computation.18 | convolution fusion | flops 273676288 | bytes 5906432 | tf_op jit(solution)/shard_map/qhd,khd->hqk/dot_general | solution.py:101
  49.9 2.3 %fusion.28 = f32[256,8,128]{0,2,1:T(8,128)} fusion(f32[8,512,256]{2,1,0:T(8,128)S(1)} %get-tuple-element.34, f32[8,256]{1,0:T(8,128)S(1)} %get-tuple-element.33, pred[256,512]{0,1:T(8,128)(4,1)S(1)} %copy-done.5, bf16[256,8,128]{0,2,1:T(8,128)(2,1)S(1)} %bitcast.71, bf16[256,8,128]{0,2,1:T(8,128)(2,1)S(1)} %bitcast.77), kind=kOutput, calls=%fused_computation.31 | convolution fusion | flops 275775488 | bytes 6430720 | tf_op jit(solution)/shard_map/hqk,khd->qhd/dot_general | solution.py:108
  52.2 1.8 %fusion.12 = (f32[8,256]{1,0:T(8,128)S(1)}, f32[8,256,512]{1,2,0:T(8,128)S(1)}) fusion(pred[256,512]{0,1:T(8,128)(4,1)S(1)} %get-tuple-element.27, bf16[256,8,128]{2,0,1:T(8,128)(2,1)S(1)} %copy-done.6, bf16[256,8,128]{2,0,1:T(8,128)(2,1)S(1)} %copy.45, bf16[256,1024]{1,0:T(8,128)(2,1)} %collective-permute-done.2), kind=kOutput, calls=%fused_computation.17 | convolution fusion | flops 273676288 | bytes 5906432 | tf_op jit(solution)/shard_map/qhd,khd->hqk/dot_general | solution.py:101
  54.1 1.3 %fusion.31 = bf16[8,128,256]{2,1,0:T(8,128)(2,1)S(1)} fusion(f32[8,256,512]{1,2,0:T(8,128)S(1)} %get-tuple-element.36, f32[8,256]{1,0:T(8,128)S(1)} %get-tuple-element.35, pred[256,512]{0,1:T(8,128)(4,1)S(1)} %get-tuple-element.27, bf16[256,8,128]{0,2,1:T(8,128)(2,1)S(1)} %bitcast.72, bf16[256,8,128]{0,2,1:T(8,128)(2,1)S(1)} %bitcast.78), kind=kOutput, calls=%fused_computation.32 | convolution fusion | flops 276037632 | bytes 5906432 | tf_op jit(solution)/shard_map/hqk,khd->qhd/dot_general | solution.py:108
  57.6 7.0 %fusion = f32[64,16,128]{2,1,0:T(8,128)S(1)} fusion(bf16[256,64,16]{0,2,1:T(8,128)(2,1)S(1)} %bitcast.62, pred[128,256]{1,0:T(8,128)(4,1)S(1)} %copy-done.10, f32[64,128,256]{2,1,0:T(8,128)} %shard_map.113), kind=kOutput, calls=%fused_computation.2 | convolution fusion | flops 77594624 | bytes 9469952 | tf_op jit(solution)/shard_map/dot_general | solution.py:79
  64.6 4.7 %fusion.37 = f32[64,16,128]{2,1,0:T(8,128)S(1)} fusion(f32[64,16,128]{2,1,0:T(8,128)S(1)} %fusion, bf16[256,64,16]{0,2,1:T(8,128)(2,1)S(1)} %bitcast.63, pred[128,256]{1,0:T(8,128)(4,1)S(1)} %copy-done.11, f32[64,128,256]{2,1,0:T(8,128)} %shard_map.113), kind=kOutput, calls=%fused_computation.34 | convolution fusion | flops 71434240 | bytes 9994240 | tf_op jit(solution)/shard_map/dot_general | solution.py:78
  69.5 2.2 %collective-permute-start.6 = (bf16[256,1152]{0,1:T(8,128)(2,1)S(1)}, bf16[256,1152]{0,1:T(8,128)(2,1)S(1)}, u32[]{:S(2)}, u32[]{:S(2)}) collective-permute-start(bf16[256,1152]{0,1:T(8,128)(2,1)S(1)} %copy-done.9), channel_id=1, source_target_pairs={{0,16},{8,24},{16,32},{24,40},{32,48},{40,56},{48,64},{56,72},{64,... | collective-permute-start | bytes 1769480 | tf_op jit(solution)/shard_map/ppermute | solution.py:18
  73.3 1.5 %collective-permute-start.4 = (f32[256]{0:T(256)S(1)}, f32[256]{0:T(256)S(1)}, u32[]{:S(2)}, u32[]{:S(2)}) collective-permute-start(f32[256]{0:T(256)S(1)} %add.106), channel_id=1, source_target_pairs={{0,2},{1,3},{2,0},{3,1},{4,6},{5,7},{6,4},{7,5},{8,10},{9,11},{10,... | collective-permute-start | bytes 3080 | tf_op jit(solution)/shard_map/ppermute | solution.py:90
  74.8 2.1 %collective-permute-done.4 = f32[256]{0:T(256)S(1)} collective-permute-done((f32[256]{0:T(256)S(1)}, f32[256]{0:T(256)S(1)}, u32[]{:S(2)}, u32[]{:S(2)}) %collective-permute-start.4) | collective-permute-done | bytes 1056 | tf_op jit(solution)/shard_map/ppermute | solution.py:90
  76.9 3.0 %collective-permute-start.5 = (f32[256]{0:T(256)S(1)}, f32[256]{0:T(256)S(1)}, u32[]{:S(2)}, u32[]{:S(2)}) collective-permute-start(f32[256]{0:T(256)S(1)} %add.107), channel_id=1, source_target_pairs={{0,4},{1,5},{2,6},{3,7},{4,0},{5,1},{6,2},{7,3},{8,12},{9,13},{10,... | collective-permute-start | bytes 3080 | tf_op jit(solution)/shard_map/ppermute | solution.py:90
  79.9 2.1 %collective-permute-done.5 = f32[256]{0:T(256)S(1)} collective-permute-done((f32[256]{0:T(256)S(1)}, f32[256]{0:T(256)S(1)}, u32[]{:S(2)}, u32[]{:S(2)}) %collective-permute-start.5) | collective-permute-done | bytes 1056 | tf_op jit(solution)/shard_map/ppermute | solution.py:90
  83.0 17.1 %collective-permute-done.6 = bf16[256,1152]{0,1:T(8,128)(2,1)S(1)} collective-permute-done((bf16[256,1152]{0,1:T(8,128)(2,1)S(1)}, bf16[256,1152]{0,1:T(8,128)(2,1)S(1)}, u32[]{:S(2)}, u32[]{:S(2)}) %collective-permute-start.6) | collective-permute-done | bytes 589856 | tf_op jit(solution)/shard_map/ppermute | solution.py:18
  (76 shorter events, 13.7 us)
Async XLA Ops:
  0.6 18.4 %copy-start.15 = (s32[32]{0:T(128)S(1)}, s32[32]{0:T(128)}, u32[]{:S(2)}) copy-start(s32[32]{0:T(128)} %param.19) | copy-start | bytes 388
  0.6 19.4 %copy-start.13 = (f32[64,128]{1,0:T(8,128)S(1)}, f32[64,128]{1,0:T(8,128)}, u32[]{:S(2)}) copy-start(f32[64,128]{1,0:T(8,128)} %param.14) | copy-start | bytes 98308
  2.1 27.4 %collective-permute-start = (bf16[127,1024]{1,0:T(8,128)(2,1)S(1)}, bf16[127,1024]{1,0:T(8,128)(2,1)S(1)}, u32[]{:S(2)}, u32[]{:S(2)}) collective-permute-start(bf16[127,1024]{1,0:T(8,128)(2,1)S(1)} %slice.56), channel_id=1, source_target_pairs={{0,8},{8,16},{16,24},{24,32},{32,40},{40,48},{48,56},{56,64},{64,7... | collective-permute-start | bytes 780296 | tf_op jit(solution)/shard_map/ppermute | solution.py:18
  6.0 46.3 %collective-permute-start.2 = (bf16[256,1024]{1,0:T(8,128)(2,1)}, bf16[256,1024]{1,0:T(8,128)(2,1)}, u32[]{:S(2)}, u32[]{:S(2)}) collective-permute-start(bf16[256,1024]{1,0:T(8,128)(2,1)} %param.16), channel_id=1, source_target_pairs={{16,0},{24,8},{32,16},{40,24},{48,32},{56,40},{64,48},{72,56},{80,... | collective-permute-start | bytes 1572872 | tf_op jit(solution)/shard_map/ppermute | solution.py:18
  17.1 28.5 %collective-permute-start.1 = (bf16[2,256,1024]{1,2,0:T(8,128)(2,1)}, bf16[2,256,1024]{1,2,0:T(8,128)(2,1)S(1)}, u32[]{:S(2)}, u32[]{:S(2)}) collective-permute-start(bf16[2,256,1024]{1,2,0:T(8,128)(2,1)} %pad_maximum_fusion), channel_id=1, source_target_pairs={{0,8},{8,16},{16,24},{24,32},{32,40},{40,48},{48,56},{56,64},{64,7... | collective-permute-start | bytes 3145736 | tf_op jit(solution)/shard_map/ppermute | solution.py:18
  29.5 7.4 %copy-start.4 = (bf16[127,1024]{1,0:T(8,128)(2,1)}, bf16[127,1024]{1,0:T(8,128)(2,1)S(1)}, u32[]{:S(2)}) copy-start(bf16[127,1024]{1,0:T(8,128)(2,1)S(1)} %collective-permute-done) | copy-start | bytes 780292
  29.8 8.2 %copy-start = (f32[64,128,256]{2,1,0:T(8,128)S(1)}, f32[64,128,256]{2,1,0:T(8,128)}, u32[]{:S(2)}) copy-start(f32[64,128,256]{2,1,0:T(8,128)} %shard_map.113) | copy-start | bytes 25165828
  29.8 8.2 %copy-start.12 = (pred[128,256]{1,0:T(8,128)(4,1)S(1)}, pred[128,256]{1,0:T(8,128)(4,1)}, u32[]{:S(2)}) copy-start(pred[128,256]{1,0:T(8,128)(4,1)} %get-tuple-element.32) | copy-start | bytes 98308
  46.5 2.4 %copy-start.5 = (pred[256,512]{0,1:T(8,128)(4,1)S(1)}, pred[256,512]{0,1:T(8,128)(4,1)}, u32[]{:S(2)}) copy-start(pred[256,512]{0,1:T(8,128)(4,1)} %get-tuple-element.28) | copy-start | bytes 393220
  46.8 3.1 %copy-start.7 = (bf16[1,256,1024]{1,2,0:T(8,128)(2,1)S(1)}, bf16[1,256,1024]{1,2,0:T(8,128)(2,1)}, u32[]{:S(2)}) copy-start(bf16[1,256,1024]{1,2,0:T(8,128)(2,1)} %get-tuple-element.25) | copy-start | bytes 1572868
  49.9 2.3 %copy-start.6 = (bf16[256,8,128]{2,0,1:T(8,128)(2,1)S(1)}, bf16[256,8,128]{2,0,1:T(8,128)(2,1)}, u32[]{:S(2)}) copy-start(bf16[256,8,128]{2,0,1:T(8,128)(2,1)} %copy.46) | copy-start | bytes 1572868
  55.3 2.2 %copy-start.10 = (pred[128,256]{1,0:T(8,128)(4,1)S(1)}, pred[128,256]{1,0:T(8,128)(4,1)}, u32[]{:S(2)}) copy-start(pred[128,256]{1,0:T(8,128)(4,1)} %get-tuple-element.31) | copy-start | bytes 98308
  56.5 0.8 copy-start.8
  57.6 7.0 %copy-start.11 = (pred[128,256]{1,0:T(8,128)(4,1)S(1)}, pred[128,256]{1,0:T(8,128)(4,1)}, u32[]{:S(2)}) copy-start(pred[128,256]{1,0:T(8,128)(4,1)} %get-tuple-element.31) | copy-start | bytes 98308
  64.5 5.0 %copy-start.9 = (bf16[256,1152]{0,1:T(8,128)(2,1)S(1)}, bf16[256,1152]{0,1:T(8,128)(2,1)}, u32[]{:S(2)}) copy-start(bf16[256,1152]{0,1:T(8,128)(2,1)} %copy-done.8) | copy-start | bytes 1769476
  64.5 7.2 %copy-start.1 = (bf16[256,1024]{1,0:T(8,128)(2,1)S(1)}, bf16[256,1024]{1,0:T(8,128)(2,1)}, u32[]{:S(2)}) copy-start(bf16[256,1024]{1,0:T(8,128)(2,1)} %param.11) | copy-start | bytes 1572868
  64.6 7.2 %copy-start.2 = (bf16[256,1024]{1,0:T(8,128)(2,1)S(1)}, bf16[256,1024]{1,0:T(8,128)(2,1)}, u32[]{:S(2)}) copy-start(bf16[256,1024]{1,0:T(8,128)(2,1)} %param.10) | copy-start | bytes 1572868
  64.6 17.4 %copy-start.14 = (f32[1024]{0:T(1024)S(1)}, f32[1024]{0:T(1024)}, u32[]{:S(2)}) copy-start(f32[1024]{0:T(1024)} %param.15) | copy-start | bytes 12292
  69.5 30.7 %copy-start.3 = (f32[256,8,128]{0,2,1:T(8,128)S(1)}, f32[256,8,128]{0,2,1:T(8,128)}, u32[]{:S(2)}) copy-start(f32[256,8,128]{0,2,1:T(8,128)} %fusion.28) | copy-start | bytes 3145732
  69.5 30.6 %collective-permute-start.6 = (bf16[256,1152]{0,1:T(8,128)(2,1)S(1)}, bf16[256,1152]{0,1:T(8,128)(2,1)S(1)}, u32[]{:S(2)}, u32[]{:S(2)}) collective-permute-start(bf16[256,1152]{0,1:T(8,128)(2,1)S(1)} %copy-done.9), channel_id=1, source_target_pairs={{0,16},{8,24},{16,32},{24,40},{32,48},{40,56},{48,64},{56,72},{64,... | collective-permute-start | bytes 1769480 | tf_op jit(solution)/shard_map/ppermute | solution.py:18
  72.1 1.2 %collective-permute-start.3 = (f32[256]{0:T(256)S(1)}, f32[256]{0:T(256)S(1)}, u32[]{:S(2)}, u32[]{:S(2)}) collective-permute-start(f32[256]{0:T(256)S(1)} %multiply_reduce_fusion), channel_id=1, source_target_pairs={{0,1},{1,0},{2,3},{3,2},{4,5},{5,4},{6,7},{7,6},{8,9},{9,8},{10,11... | collective-permute-start | bytes 3080 | tf_op jit(solution)/shard_map/ppermute | solution.py:90
  73.3 3.6 %collective-permute-start.4 = (f32[256]{0:T(256)S(1)}, f32[256]{0:T(256)S(1)}, u32[]{:S(2)}, u32[]{:S(2)}) collective-permute-start(f32[256]{0:T(256)S(1)} %add.106), channel_id=1, source_target_pairs={{0,2},{1,3},{2,0},{3,1},{4,6},{5,7},{6,4},{7,5},{8,10},{9,11},{10,... | collective-permute-start | bytes 3080 | tf_op jit(solution)/shard_map/ppermute | solution.py:90
  76.9 5.1 %collective-permute-start.5 = (f32[256]{0:T(256)S(1)}, f32[256]{0:T(256)S(1)}, u32[]{:S(2)}, u32[]{:S(2)}) collective-permute-start(f32[256]{0:T(256)S(1)} %add.107), channel_id=1, source_target_pairs={{0,4},{1,5},{2,6},{3,7},{4,0},{5,1},{6,2},{7,3},{8,12},{9,13},{10,... | collective-permute-start | bytes 3080 | tf_op jit(solution)/shard_map/ppermute | solution.py:90

commit v9 on v8

--- a/solution.py
+++ b/solution.py
@@ -49,9 +49,9 @@
     )(reversed_taps)
 
 
-def causal_filter(extended, filter_taps, reach_back, out_rows, between):
+def causal_filter(mixed_rows, rim_rows, filter_taps, reach_back, out_rows, between):
     groups, taps = filter_taps.shape
-    channels = extended.shape[1]
+    channels = mixed_rows.shape[1]
     width = channels // groups
     span = 2 * taps
     lag_table = (
@@ -64,14 +64,19 @@
     lower_part = (toeplitz - upper_part.astype(jnp.float32)).astype(jnp.bfloat16)
     zero_half = jnp.zeros((), jnp.bfloat16)
     numbers = (((0,), (2,)), ((1,), (0,)))
-    extended = jnp.concatenate([extended, jnp.zeros((1, channels), extended.dtype)], axis=0)
-    results = []
-    for block_index in range(out_rows // taps):
-        if block_index == 1:
-            extended = between(results[0], extended)
-        first = block_index * taps
-        sources = extended[first : first + span].reshape(span, groups, width)
-        limits = reach_back[first : first + taps]
+    padded = jnp.concatenate([mixed_rows, jnp.zeros((1, channels), mixed_rows.dtype)], axis=0)
+    block_count = out_rows // taps
+    results = [None] * block_count
+    for step, block_index in enumerate(range(block_count - 1, -1, -1)):
+        if step == 1:
+            rim_rows, padded = between(results[block_count - 1], (rim_rows, padded))
+        first = block_index * taps - (taps - 1)
+        if first >= 0:
+            sources = padded[first : first + span]
+        else:
+            sources = jnp.concatenate([rim_rows[first + taps - 1 :], padded[: first + span]], axis=0)
+        sources = sources.reshape(span, groups, width)
+        limits = reach_back[block_index * taps : (block_index + 1) * taps]
         valid = (lag_table <= limits[:, None])[None]
         kernel_upper = jnp.where(valid, upper_part, zero_half)
         kernel_lower = jnp.where(valid, lower_part, zero_half)
@@ -79,7 +84,7 @@
         result = result + lax.dot_general(
             sources, kernel_lower, numbers, preferred_element_type=jnp.float32
         )
-        results.append(result.transpose(2, 0, 1).reshape(taps, channels))
+        results[block_index] = result.transpose(2, 0, 1).reshape(taps, channels)
     return jnp.concatenate(results, axis=0)
 
 
@@ -132,9 +137,10 @@
     mixed_rows = (hyena_key.astype(jnp.float32) * hyena_value.astype(jnp.float32)).astype(
         jnp.bfloat16
     )
-    rim_rows = shifted(mixed_rows[tok_rows - (taps - 1) :], "ctx", 1)
-    key_pair = jnp.stack([att_key, att_value])
-    previous = shifted(key_pair, "ctx", 1)
+    packet = jnp.concatenate([att_key, att_value, mixed_rows[tok_rows - (taps - 1) :]], axis=0)
+    received = shifted(packet, "ctx", 1)
+    previous = (received[:tok_rows], received[tok_rows : 2 * tok_rows])
+    rim_rows = received[2 * tok_rows :]
     later_query = shifted(att_query, "ctx", -2)
     key_rows = jnp.concatenate([previous[0], att_key], axis=0)
     value_rows = jnp.concatenate([previous[1], att_value], axis=0)
@@ -170,8 +176,9 @@
         held["stat_cols"] = stat_cols
         return extended
 
-    extended = jnp.concatenate([rim_rows, mixed_rows], axis=0)
-    filtered = causal_filter(extended, filter_taps, positions - doc_begin, tok_rows, far_part)
+    filtered = causal_filter(
+        mixed_rows, rim_rows, filter_taps, positions - doc_begin, tok_rows, far_part
+    )
     hidden = residual.astype(jnp.float32) + hyena_gate.astype(jnp.float32) * filtered
     local_sum = jnp.sum(hidden * hidden, axis=1)
     mean_square = tp_sum(local_sum) / D

time: 102 us -> 95.7 us (0.938)
  matrix products: 27.5 us -> 17.1 us
  waiting for transfers between devices: 27.5 us -> 34.6 us
  other arithmetic: 9.34 us -> 6.05 us
  starting transfers between devices: 20.1 us -> 18.2 us
  local copies, waits for them, and re-layouts: 9.35 us -> 11.1 us
    ppermute x4 -> x3, waiting for transfers between devices: 22.2 us -> 29.3 us  [shifted(): lax.ppermute(value, axis, [(source, source + steps) for source in range(f...]
    dot_general x2, matrix products: 14.1 us -> 8.31 us  [causal_filter(): lax.dot_general(sources, kernel_lower, numbers, preferred_element_type=jn...]
    dot_general x2, matrix products: 5.9 us -> 2.41 us  [causal_filter(): lax.dot_general(sources, kernel_upper, numbers, preferred_element_type=jn...]
    ppermute x4 -> x3, starting transfers between devices: 15.5 us -> 13.5 us  [shifted(): lax.ppermute(value, axis, [(source, source + steps) for source in range(f...]
    unnamed x36 -> x26, local copies, waits for them, and re-layouts: 5.46 us -> 7.1 us
    slice x6, local copies, waits for them, and re-layouts: 1.37 us -> 2.72 us  [the longest x1 1.28 us: block_body(): previous = (received[:tok_rows], received[tok_rows:2 * tok_rows])]
    concatenate x3 -> x1, local copies, waits for them, and re-layouts: 1.35 us -> 0.07 us  [causal_filter(): jnp.concatenate([mixed_rows, jnp.zeros((1, channels), mixed_rows.dtype)],...]
    convert_element_type x1, other arithmetic: 1.4 us -> 0.13 us  [block_body(): (hyena_key.astype(jnp.float32) * hyena_value.astype(jnp.float32)).astype(...]
  transfers between devices with their start and end apart: 7 -> 6, of which waited for: 5 -> 5; matrix products, arithmetic and copies ran while one was open for 25% -> 25% of each run, Pallas kernels for 7% -> 7%
where the time goes in v9:
time: 95.7 us; the launch traced here: 94.8 us
  waiting for transfers between devices  34.6 us (36%)
  starting transfers between devices  18.2 us (19%)
  matrix products  17.1 us (18%)
  local copies, waits for them, and re-layouts  11.1 us (12%)
  Pallas kernels  6.73 us (7%)
  other arithmetic  6.05 us (6%)
  between operations  1.03 us (1%)
    ppermute x3, waiting for transfers between devices, shifted(): lax.ppermute(value, axis, [(source, source + steps) for source in range(f...  29.3 us
    ppermute x3, starting transfers between devices, shifted(): lax.ppermute(value, axis, [(source, source + steps) for source in range(f...  13.5 us
    dot_general x2, matrix products, causal_filter(): lax.dot_general(sources, kernel_lower, numbers, preferred_element_type=jn...  8.31 us
    unnamed x26, local copies, waits for them, and re-layouts  7.1 us
    pallas_call x1, Pallas kernels, build_toeplitz(): pl.pallas_call(toeplitz_rows, grid=(groups // step,), in_specs=[pl.BlockS...  6.73 us
    ppermute x3, waiting for transfers between devices, tp_sum(): lax.ppermute(value, 'tp', [(i, i ^ stride) for i in range(count)])  5.28 us
    ppermute x3, starting transfers between devices, tp_sum(): lax.ppermute(value, 'tp', [(i, i ^ stride) for i in range(count)])  4.61 us
    dot_general x2, matrix products, attend_block(): jnp.einsum('hqk,khd->qhd', expo.astype(jnp.bfloat16), value_heads, prefer...  3.49 us
  transfers between devices with their start and end apart: 6, of which 5 were waited for; matrix products, arithmetic and copies ran while one was open for 25% of the time, Pallas kernels for 7%

profile of v9, /device:TPU:24, one launch (start us, length us, event | category | flops | bytes accessed | tf_op | source)
XLA Modules:
  0.0 94.8 jit_solution(9647762764551261094)
XLA Ops:
  0.6 8.4 %collective-permute-start.1 = (bf16[256,1024]{1,0:T(8,128)(2,1)}, bf16[256,1024]{1,0:T(8,128)(2,1)}, u32[]{:S(2)}, u32[]{:S(2)}) collective-permute-start(bf16[256,1024]{1,0:T(8,128)(2,1)} %param.16), channel_id=1, source_target_pairs={{16,0},{24,8},{32,16},{40,24},{48,32},{56,40},{64,48},{72,56},{80,... | collective-permute-start | bytes 1572872 | tf_op jit(solution)/shard_map/ppermute | solution.py:18
  9.0 1.2 %copy.41 = bf16[256,1024]{0,1:T(8,128)(2,1)S(1)} copy(bf16[256,1024]{1,0:T(8,128)(2,1)} %param.17) | data formatting | bytes 1048576 | tf_op args[7]
  10.3 1.2 %copy.42 = bf16[256,1024]{0,1:T(8,128)(2,1)S(1)} copy(bf16[256,1024]{1,0:T(8,128)(2,1)} %param.18) | data formatting | bytes 1048576 | tf_op args[8]
  11.6 1.3 %copy.39 = bf16[256,1024]{0,1:T(8,128)(2,1)S(1)} copy(bf16[256,1024]{1,0:T(8,128)(2,1)} %param.12) | data formatting | bytes 1048576 | tf_op args[2]
  12.8 1.2 %copy.40 = bf16[256,1024]{0,1:T(8,128)(2,1)S(1)} copy(bf16[256,1024]{1,0:T(8,128)(2,1)} %param.13) | data formatting | bytes 1048576 | tf_op args[3]
  14.3 1.2 %pad_maximum_fusion = bf16[639,1024]{0,1:T(8,128)(2,1)} fusion(bf16[127,1024]{0,1:T(8,128)(2,1)S(1)} %slice.60, bf16[256,1024]{0,1:T(8,128)(2,1)S(1)} %copy.42, bf16[256,1024]{0,1:T(8,128)(2,1)S(1)} %copy.41), kind=kLoop, calls=%fused_computation.32 | loop fusion | flops 3926016 | bytes 2617344 | tf_op jit(solution)/shard_map/concatenate | solution.py:140
  15.5 2.9 %collective-permute-start = (bf16[639,1024]{0,1:T(8,128)(2,1)}, bf16[639,1024]{0,1:T(8,128)(2,1)}, u32[]{:S(2)}, u32[]{:S(2)}) collective-permute-start(bf16[639,1024]{0,1:T(8,128)(2,1)} %pad_maximum_fusion), channel_id=1, source_target_pairs={{0,8},{8,16},{16,24},{24,32},{32,40},{40,48},{48,56},{56,64},{64,7... | collective-permute-start | bytes 3926024 | tf_op jit(solution)/shard_map/ppermute | solution.py:18
  19.8 6.7 %shard_map.113 = f32[64,128,256]{2,1,0:T(8,128)} custom-call(f32[64,256]{1,0:T(8,128)} %concatenate.30.reversed_ref), custom_call_target="tpu_custom_call" | custom-call | tf_op jit(solution)/shard_map/pallas_call | solution.py:43
  26.6 7.1 %fusion.4 = f32[64,16,128]{2,1,0:T(8,128)S(1)} fusion(bf16[256,64,16]{0,2,1:T(8,128)(2,1)S(1)} %bitcast.65, pred[128,256]{1,0:T(8,128)(4,1)S(1)} %get-tuple-element.34, f32[64,128,256]{2,1,0:T(8,128)} %shard_map.113), kind=kOutput, calls=%fused_computation.9 | convolution fusion | flops 77594624 | bytes 9469952 | tf_op jit(solution)/shard_map/dot_general | solution.py:84
  34.8 1.2 %fusion.34 = f32[64,16,128]{2,1,0:T(8,128)S(1)} fusion(f32[64,16,128]{2,1,0:T(8,128)S(1)} %fusion.4, bf16[256,64,16]{0,2,1:T(8,128)(2,1)S(1)} %bitcast.66, pred[128,256]{1,0:T(8,128)(4,1)S(1)} %get-tuple-element.34, f32[64,128,256]{2,1,0:T(8,128)S(1)} %copy-done), kind=kOutput, calls=%fused_computation.34 | convolution fusion | flops 71434240 | bytes 9994240 | tf_op jit(solution)/shard_map/dot_general | solution.py:83
  36.5 13.6 %collective-permute-done = bf16[639,1024]{0,1:T(8,128)(2,1)} collective-permute-done((bf16[639,1024]{0,1:T(8,128)(2,1)}, bf16[639,1024]{0,1:T(8,128)(2,1)}, u32[]{:S(2)}, u32[]{:S(2)}) %collective-permute-start) | collective-permute-done | bytes 1308704 | tf_op jit(solution)/shard_map/ppermute | solution.py:18
  50.1 1.3 %fusion.73 = (bf16[256,1024]{0,1:T(8,128)(2,1)S(1)}, bf16[256,1024]{0,1:T(8,128)(2,1)S(1)}) fusion(bf16[639,1024]{0,1:T(8,128)(2,1)} %collective-permute-done), kind=kLoop, calls=%fused_computation.101 | loop fusion | bytes 2097152 | tf_op jit(solution)/shard_map/slice | solution.py:142
  53.5 2.2 %fusion.28 = f32[256,8,128]{0,2,1:T(8,128)} fusion(bf16[512,8,128]{0,2,1:T(8,128)(2,1)S(1)} %bitcast.73, f32[8,512,256]{2,1,0:T(8,128)S(1)} %get-tuple-element.36, f32[8,256]{1,0:T(8,128)S(1)} %get-tuple-element.35, pred[256,512]{0,1:T(8,128)(4,1)S(1)} %get-tuple-element.30), kind=kOutput, calls=%fused_computation.31 | convolution fusion | flops 273678336 | bytes 6430720 | tf_op jit(solution)/shard_map/hqk,khd->qhd/dot_general | solution.py:113
  55.7 2.0 %fusion.12 = (f32[8,256]{1,0:T(8,128)S(1)}, f32[8,256,512]{1,2,0:T(8,128)S(1)}) fusion(pred[256,512]{0,1:T(8,128)(4,1)S(1)} %get-tuple-element.29, bf16[512,8,128]{0,2,1:T(8,128)(2,1)S(1)} %bitcast.64, bf16[256,1024]{1,0:T(8,128)(2,1)} %collective-permute-done.1), kind=kOutput, calls=%fused_computation.17 | convolution fusion | flops 271579136 | bytes 5906432 | tf_op jit(solution)/shard_map/qhd,khd->hqk/dot_general | solution.py:106
  57.8 1.3 %fusion.31 = bf16[8,128,256]{2,1,0:T(8,128)(2,1)S(1)} fusion(bf16[512,8,128]{0,2,1:T(8,128)(2,1)S(1)} %bitcast.74, f32[8,256,512]{1,2,0:T(8,128)S(1)} %get-tuple-element.38, f32[8,256]{1,0:T(8,128)S(1)} %get-tuple-element.37, pred[256,512]{0,1:T(8,128)(4,1)S(1)} %get-tuple-element.29), kind=kOutput, calls=%fused_computation.33 | convolution fusion | flops 273940480 | bytes 5906432 | tf_op jit(solution)/shard_map/hqk,khd->qhd/dot_general | solution.py:113
  61.6 1.2 %fusion = f32[64,16,128]{2,1,0:T(8,128)S(1)} fusion(bf16[256,64,16]{0,2,1:T(8,128)(2,1)S(1)} %bitcast.67, pred[128,256]{1,0:T(8,128)(4,1)S(1)} %get-tuple-element.33, f32[64,128,256]{2,1,0:T(8,128)S(1)} %bitcast.62), kind=kOutput, calls=%fused_computation.2 | convolution fusion | flops 77594624 | bytes 9469952 | tf_op jit(solution)/shard_map/dot_general | solution.py:84
  62.8 1.2 %fusion.37 = f32[64,16,128]{2,1,0:T(8,128)S(1)} fusion(f32[64,16,128]{2,1,0:T(8,128)S(1)} %fusion, bf16[256,64,16]{0,2,1:T(8,128)(2,1)S(1)} %bitcast.68, pred[128,256]{1,0:T(8,128)(4,1)S(1)} %get-tuple-element.33, f32[64,128,256]{2,1,0:T(8,128)S(1)} %bitcast.62), kind=kOutput, calls=%fused_computation.35 | convolution fusion | flops 71434240 | bytes 9994240 | tf_op jit(solution)/shard_map/dot_general | solution.py:83
  64.2 2.2 %collective-permute-start.5 = (bf16[256,1152]{0,1:T(8,128)(2,1)S(1)}, bf16[256,1152]{0,1:T(8,128)(2,1)S(1)}, u32[]{:S(2)}, u32[]{:S(2)}) collective-permute-start(bf16[256,1152]{0,1:T(8,128)(2,1)S(1)} %broadcast_dynamic-update-slice_fusion), channel_id=1, source_target_pairs={{0,16},{8,24},{16,32},{24,40},{32,48},{40,56},{48,64},{56,72},{64,... | collective-permute-start | bytes 1769480 | tf_op jit(solution)/shard_map/ppermute | solution.py:18
  66.8 1.1 %collective-permute-done.2 = f32[256]{0:T(256)S(1)} collective-permute-done((f32[256]{0:T(256)S(1)}, f32[256]{0:T(256)S(1)}, u32[]{:S(2)}, u32[]{:S(2)}) %collective-permute-start.2) | collective-permute-done | bytes 1056 | tf_op jit(solution)/shard_map/ppermute | solution.py:95
  68.0 1.5 %collective-permute-start.3 = (f32[256]{0:T(256)S(1)}, f32[256]{0:T(256)S(1)}, u32[]{:S(2)}, u32[]{:S(2)}) collective-permute-start(f32[256]{0:T(256)S(1)} %add.108), channel_id=1, source_target_pairs={{0,2},{1,3},{2,0},{3,1},{4,6},{5,7},{6,4},{7,5},{8,10},{9,11},{10,... | collective-permute-start | bytes 3080 | tf_op jit(solution)/shard_map/ppermute | solution.py:95
  69.5 2.1 %collective-permute-done.3 = f32[256]{0:T(256)S(1)} collective-permute-done((f32[256]{0:T(256)S(1)}, f32[256]{0:T(256)S(1)}, u32[]{:S(2)}, u32[]{:S(2)}) %collective-permute-start.3) | collective-permute-done | bytes 1056 | tf_op jit(solution)/shard_map/ppermute | solution.py:95
  71.6 3.0 %collective-permute-start.4 = (f32[256]{0:T(256)S(1)}, f32[256]{0:T(256)S(1)}, u32[]{:S(2)}, u32[]{:S(2)}) collective-permute-start(f32[256]{0:T(256)S(1)} %add.109), channel_id=1, source_target_pairs={{0,4},{1,5},{2,6},{3,7},{4,0},{5,1},{6,2},{7,3},{8,12},{9,13},{10,... | collective-permute-start | bytes 3080 | tf_op jit(solution)/shard_map/ppermute | solution.py:95
  74.6 2.0 %collective-permute-done.4 = f32[256]{0:T(256)S(1)} collective-permute-done((f32[256]{0:T(256)S(1)}, f32[256]{0:T(256)S(1)}, u32[]{:S(2)}, u32[]{:S(2)}) %collective-permute-start.4) | collective-permute-done | bytes 1056 | tf_op jit(solution)/shard_map/ppermute | solution.py:95
  77.7 15.7 %collective-permute-done.5 = bf16[256,1152]{0,1:T(8,128)(2,1)S(1)} collective-permute-done((bf16[256,1152]{0,1:T(8,128)(2,1)S(1)}, bf16[256,1152]{0,1:T(8,128)(2,1)S(1)}, u32[]{:S(2)}, u32[]{:S(2)}) %collective-permute-start.5) | collective-permute-done | bytes 589856 | tf_op jit(solution)/shard_map/ppermute | solution.py:18
  (63 shorter events, 10.7 us)
Async XLA Ops:
  0.6 55.1 %collective-permute-start.1 = (bf16[256,1024]{1,0:T(8,128)(2,1)}, bf16[256,1024]{1,0:T(8,128)(2,1)}, u32[]{:S(2)}, u32[]{:S(2)}) collective-permute-start(bf16[256,1024]{1,0:T(8,128)(2,1)} %param.16), channel_id=1, source_target_pairs={{16,0},{24,8},{32,16},{40,24},{48,32},{56,40},{64,48},{72,56},{80,... | collective-permute-start | bytes 1572872 | tf_op jit(solution)/shard_map/ppermute | solution.py:18
  11.5 7.2 %copy-start.7 = (s32[32]{0:T(128)S(1)}, s32[32]{0:T(128)}, u32[]{:S(2)}) copy-start(s32[32]{0:T(128)} %param.19) | copy-start | bytes 388
  11.5 7.4 %copy-start.5 = (f32[64,128]{1,0:T(8,128)S(1)}, f32[64,128]{1,0:T(8,128)}, u32[]{:S(2)}) copy-start(f32[64,128]{1,0:T(8,128)} %param.14) | copy-start | bytes 98308
  15.5 34.5 %collective-permute-start = (bf16[639,1024]{0,1:T(8,128)(2,1)}, bf16[639,1024]{0,1:T(8,128)(2,1)}, u32[]{:S(2)}, u32[]{:S(2)}) collective-permute-start(bf16[639,1024]{0,1:T(8,128)(2,1)} %pad_maximum_fusion), channel_id=1, source_target_pairs={{0,8},{8,16},{16,24},{24,32},{32,40},{40,48},{48,56},{56,64},{64,7... | collective-permute-start | bytes 3926024 | tf_op jit(solution)/shard_map/ppermute | solution.py:18
  26.6 8.2 %copy-start = (f32[64,128,256]{2,1,0:T(8,128)S(1)}, f32[64,128,256]{2,1,0:T(8,128)}, u32[]{:S(2)}) copy-start(f32[64,128,256]{2,1,0:T(8,128)} %shard_map.113) | copy-start | bytes 25165828
  36.0 15.5 %copy-start.4 = (bf16[256,1024]{1,0:T(8,128)(2,1)S(1)}, bf16[256,1024]{1,0:T(8,128)(2,1)}, u32[]{:S(2)}) copy-start(bf16[256,1024]{1,0:T(8,128)(2,1)} %param.16) | copy-start | bytes 1572868
  57.7 3.8 %slice-start = ((s8[8388608]{0:T(1024)(128)(4,1)}), s8[4194304]{0:T(1024)(128)(4,1)S(1)}, s32[]{:S(2)}) async-start(s8[8388608]{0:T(1024)(128)(4,1)} %bitcast.61), calls=%async_computation | async-start | bytes 8388608
  57.7 3.8 %slice-start.1 = ((s8[8388608]{0:T(1024)(128)(4,1)}), s8[4194304]{0:T(1024)(128)(4,1)S(1)}, s32[]{:S(2)}) async-start(s8[8388608]{0:T(1024)(128)(4,1)} %bitcast.61), calls=%async_computation.1 | async-start | bytes 8388608
  62.7 3.7 %copy-start.1 = (bf16[256,1024]{1,0:T(8,128)(2,1)S(1)}, bf16[256,1024]{1,0:T(8,128)(2,1)}, u32[]{:S(2)}) copy-start(bf16[256,1024]{1,0:T(8,128)(2,1)} %param.11) | copy-start | bytes 1572868
  62.8 3.7 %copy-start.2 = (bf16[256,1024]{1,0:T(8,128)(2,1)S(1)}, bf16[256,1024]{1,0:T(8,128)(2,1)}, u32[]{:S(2)}) copy-start(bf16[256,1024]{1,0:T(8,128)(2,1)} %param.10) | copy-start | bytes 1572868
  62.8 13.9 %copy-start.6 = (f32[1024]{0:T(1024)S(1)}, f32[1024]{0:T(1024)}, u32[]{:S(2)}) copy-start(f32[1024]{0:T(1024)} %param.15) | copy-start | bytes 12292
  64.2 29.3 %copy-start.3 = (f32[256,8,128]{0,2,1:T(8,128)S(1)}, f32[256,8,128]{0,2,1:T(8,128)}, u32[]{:S(2)}) copy-start(f32[256,8,128]{0,2,1:T(8,128)} %fusion.28) | copy-start | bytes 3145732
  64.2 29.2 %collective-permute-start.5 = (bf16[256,1152]{0,1:T(8,128)(2,1)S(1)}, bf16[256,1152]{0,1:T(8,128)(2,1)S(1)}, u32[]{:S(2)}, u32[]{:S(2)}) collective-permute-start(bf16[256,1152]{0,1:T(8,128)(2,1)S(1)} %broadcast_dynamic-update-slice_fusion), channel_id=1, source_target_pairs={{0,16},{8,24},{16,32},{24,40},{32,48},{40,56},{48,64},{56,72},{64,... | collective-permute-start | bytes 1769480 | tf_op jit(solution)/shard_map/ppermute | solution.py:18
  66.7 1.2 %collective-permute-start.2 = (f32[256]{0:T(256)S(1)}, f32[256]{0:T(256)S(1)}, u32[]{:S(2)}, u32[]{:S(2)}) collective-permute-start(f32[256]{0:T(256)S(1)} %multiply_reduce_fusion), channel_id=1, source_target_pairs={{0,1},{1,0},{2,3},{3,2},{4,5},{5,4},{6,7},{7,6},{8,9},{9,8},{10,11... | collective-permute-start | bytes 3080 | tf_op jit(solution)/shard_map/ppermute | solution.py:95
  68.0 3.6 %collective-permute-start.3 = (f32[256]{0:T(256)S(1)}, f32[256]{0:T(256)S(1)}, u32[]{:S(2)}, u32[]{:S(2)}) collective-permute-start(f32[256]{0:T(256)S(1)} %add.108), channel_id=1, source_target_pairs={{0,2},{1,3},{2,0},{3,1},{4,6},{5,7},{6,4},{7,5},{8,10},{9,11},{10,... | collective-permute-start | bytes 3080 | tf_op jit(solution)/shard_map/ppermute | solution.py:95
  71.6 5.1 %collective-permute-start.4 = (f32[256]{0:T(256)S(1)}, f32[256]{0:T(256)S(1)}, u32[]{:S(2)}, u32[]{:S(2)}) collective-permute-start(f32[256]{0:T(256)S(1)} %add.109), channel_id=1, source_target_pairs={{0,4},{1,5},{2,6},{3,7},{4,0},{5,1},{6,2},{7,3},{8,12},{9,13},{10,... | collective-permute-start | bytes 3080 | tf_op jit(solution)/shard_map/ppermute | solution.py:95

commit v10 on v8

--- a/solution.py
+++ b/solution.py
@@ -146,11 +146,14 @@
     far_visible = (key_pos[None, :] <= far_pos[:, None]) & (key_pos[None, :] >= far_begin[:, None])
     held = {}
     visible = (key_pos[None, :] <= positions[:, None]) & (key_pos[None, :] >= doc_begin[:, None])
-    near_sum, near_top, near_den = attend_block(att_query, key_rows, value_rows, visible, scale)
+    split = (att_query.shape[1] // HEAD_DIM // 2) * HEAD_DIM
+    near_first = attend_block(
+        att_query[:, :split], key_rows[:, :split], value_rows[:, :split], visible, scale
+    )
 
     def far_part(first_rows, extended):
         first_rows, queries, held["near"] = lax.optimization_barrier(
-            (first_rows, later_query, (near_sum, near_top, near_den))
+            (first_rows, later_query, near_first)
         )
         far_sum, far_top, far_den = attend_block(queries, key_rows, value_rows, far_visible, scale)
         far_stats = jnp.concatenate([far_top, far_den], axis=1)
@@ -164,7 +167,9 @@
             [far_sum.astype(jnp.bfloat16).reshape(tok_rows, -1), stat_high, stat_mid, stat_low, stat_pad],
             axis=1,
         )
-        far_packet, extended = lax.optimization_barrier((far_packet, extended))
+        far_packet, extended, held["late"] = lax.optimization_barrier(
+            (far_packet, extended, (att_query[:, split:], key_rows[:, split:], value_rows[:, split:]))
+        )
         held["packet"] = shifted(far_packet, "ctx", 2)
         held["shape"] = far_sum.shape
         held["stat_cols"] = stat_cols
@@ -179,7 +184,11 @@
         jnp.bfloat16
     )
     far_packet, stat_cols = held["packet"], held["stat_cols"]
-    near_sum, near_top, near_den = held["near"]
+    late_query, late_key, late_value = held["late"]
+    near_second = attend_block(late_query, late_key, late_value, visible, scale)
+    near_sum = jnp.concatenate([held["near"][0], near_second[0]], axis=1)
+    near_top = jnp.concatenate([held["near"][1], near_second[1]], axis=1)
+    near_den = jnp.concatenate([held["near"][2], near_second[2]], axis=1)
     sum_shape = held["shape"]
     sum_cols = sum_shape[1] * sum_shape[2]
     far_sum = far_packet[:, :sum_cols].reshape(sum_shape)

time: 102 us -> 106 us (1.039)
  local copies, waits for them, and re-layouts: 9.35 us -> 13.6 us
  waiting for transfers between devices: 27.5 us -> 26.1 us
  other arithmetic: 9.34 us -> 10.6 us
    ppermute x3, waiting for transfers between devices: 5.29 us -> 2.9 us  [tp_sum(): lax.ppermute(value, 'tp', [(i, i ^ stride) for i in range(count)])]
    concatenate x0 -> x1, other arithmetic: none -> 2.22 us  [block_body(): value_rows = jnp.concatenate([previous[1], att_value], axis=0)]
    slice x1, local copies, waits for them, and re-layouts: 0.04 us -> 1.75 us  [far_part(): att_query[:, split:]]
    slice x1, local copies, waits for them, and re-layouts: 0.86 us -> 2.3 us  [block_body(): value_rows = jnp.concatenate([previous[1], att_value], axis=0)]
    dot_general x2 -> x3, matrix products: 3.91 us -> 3.12 us  [attend_block(): jnp.einsum('qhd,khd->hqk', query_heads, key_heads, preferred_element_type...]
    reduce_sum x2 -> x3, other arithmetic: 2.02 us -> 2.62 us  [attend_block(): denominator = jnp.sum(expo, axis=2)]
    unnamed x36 -> x45, local copies, waits for them, and re-layouts: 5.46 us -> 4.94 us
    dot_general x2 -> x3, matrix products: 3.55 us -> 3.79 us  [attend_block(): jnp.einsum('hqk,khd->qhd', expo.astype(jnp.bfloat16), value_heads, prefer...]
  transfers between devices with their start and end apart: 7 -> 7, of which waited for: 5 -> 4; matrix products, arithmetic and copies ran while one was open for 25% -> 27% of each run, Pallas kernels for 7% -> 6%
where the time goes in v10:
time: 106 us; the launch traced here: 105 us
  matrix products  26.9 us (25%)
  waiting for transfers between devices  26.1 us (25%)
  starting transfers between devices  20 us (19%)
  local copies, waits for them, and re-layouts  13.6 us (13%)
  other arithmetic  10.6 us (10%)
  Pallas kernels  6.73 us (6%)
  between operations  1.09 us (1%)
    ppermute x4, waiting for transfers between devices, shifted(): lax.ppermute(value, axis, [(source, source + steps) for source in range(f...  23.2 us
    ppermute x4, starting transfers between devices, shifted(): lax.ppermute(value, axis, [(source, source + steps) for source in range(f...  15.3 us
    dot_general x2, matrix products, causal_filter(): lax.dot_general(sources, kernel_lower, numbers, preferred_element_type=jn...  14.1 us
    pallas_call x1, Pallas kernels, build_toeplitz(): pl.pallas_call(toeplitz_rows, grid=(groups // step,), in_specs=[pl.BlockS...  6.73 us
    dot_general x2, matrix products, causal_filter(): lax.dot_general(sources, kernel_upper, numbers, preferred_element_type=jn...  5.88 us
    unnamed x45, local copies, waits for them, and re-layouts  4.94 us
    ppermute x3, starting transfers between devices, tp_sum(): lax.ppermute(value, 'tp', [(i, i ^ stride) for i in range(count)])  4.68 us
    dot_general x3, matrix products, attend_block(): jnp.einsum('hqk,khd->qhd', expo.astype(jnp.bfloat16), value_heads, prefer...  3.79 us
  transfers between devices with their start and end apart: 7, of which 4 were waited for; matrix products, arithmetic and copies ran while one was open for 27% of the time, Pallas kernels for 6%

profile of v10, /device:TPU:24, one launch (start us, length us, event | category | flops | bytes accessed | tf_op | source)
XLA Modules:
  0.0 105.0 jit_solution(8481439509034644732)
XLA Ops:
  0.7 1.5 %multiply_convert_fusion.1 = bf16[256,1024]{1,0:T(8,128)(2,1)S(1)} fusion(bf16[256,1024]{1,0:T(8,128)(2,1)} %param.13, bf16[256,1024]{1,0:T(8,128)(2,1)} %param.12), kind=kLoop, calls=%fused_computation.66 | loop fusion | flops 1048576 | bytes 1572864 | tf_op jit(solution)/shard_map/convert_element_type | solution.py:132
  2.2 3.8 %collective-permute-start = (bf16[127,1024]{1,0:T(8,128)(2,1)S(1)}, bf16[127,1024]{1,0:T(8,128)(2,1)S(1)}, u32[]{:S(2)}, u32[]{:S(2)}) collective-permute-start(bf16[127,1024]{1,0:T(8,128)(2,1)S(1)} %slice.80), channel_id=1, source_target_pairs={{0,8},{8,16},{16,24},{24,32},{32,40},{40,48},{48,56},{56,64},{64,7... | collective-permute-start | bytes 780296 | tf_op jit(solution)/shard_map/ppermute | solution.py:18
  6.0 7.5 %collective-permute-start.2 = (bf16[256,1024]{1,0:T(8,128)(2,1)}, bf16[256,1024]{1,0:T(8,128)(2,1)}, u32[]{:S(2)}, u32[]{:S(2)}) collective-permute-start(bf16[256,1024]{1,0:T(8,128)(2,1)} %param.16), channel_id=1, source_target_pairs={{16,0},{24,8},{32,16},{40,24},{48,32},{56,40},{64,48},{72,56},{80,... | collective-permute-start | bytes 1572872 | tf_op jit(solution)/shard_map/ppermute | solution.py:18
  14.0 1.1 %pad_maximum_fusion = bf16[2,256,1024]{1,2,0:T(8,128)(2,1)} fusion(bf16[1,256,1024]{1,2,0:T(8,128)(2,1)S(1)} %bitcast.93, bf16[1,256,1024]{1,2,0:T(8,128)(2,1)S(1)} %bitcast.87), kind=kLoop, calls=%fused_computation.39 | loop fusion | flops 524288 | bytes 2097152 | tf_op jit(solution)/shard_map/stack | solution.py:136
  15.1 1.9 %collective-permute-start.1 = (bf16[2,256,1024]{1,2,0:T(8,128)(2,1)}, bf16[2,256,1024]{1,2,0:T(8,128)(2,1)}, u32[]{:S(2)}, u32[]{:S(2)}) collective-permute-start(bf16[2,256,1024]{1,2,0:T(8,128)(2,1)} %pad_maximum_fusion), channel_id=1, source_target_pairs={{0,8},{8,16},{16,24},{24,32},{32,40},{40,48},{48,56},{56,64},{64,7... | collective-permute-start | bytes 3145736 | tf_op jit(solution)/shard_map/ppermute | solution.py:18
  17.1 1.8 %fusion.94 = (bf16[256,512]{1,0:T(8,128)(2,1)}, bf16[256,512]{1,0:T(8,128)(2,1)S(1)}) fusion(bf16[256,1024]{1,0:T(8,128)(2,1)} %param.16), kind=kLoop, calls=%fused_computation.136 | loop fusion | bytes 1048576 | tf_op jit(solution)/shard_map/slice | solution.py:171
  22.8 6.7 %shard_map.113 = f32[64,128,256]{2,1,0:T(8,128)} custom-call(f32[64,256]{1,0:T(8,128)} %concatenate.49.reversed_ref), custom_call_target="tpu_custom_call" | custom-call | tf_op jit(solution)/shard_map/pallas_call | solution.py:43
  30.6 7.1 %fusion.4 = f32[64,16,128]{2,1,0:T(8,128)S(1)} fusion(bf16[256,64,16]{0,2,1:T(8,128)(2,1)S(1)} %bitcast.91, pred[128,256]{1,0:T(8,128)(4,1)S(1)} %get-tuple-element.44, f32[64,128,256]{2,1,0:T(8,128)} %shard_map.113), kind=kOutput, calls=%fused_computation.7 | convolution fusion | flops 77594624 | bytes 9469952 | tf_op jit(solution)/shard_map/dot_general | solution.py:79
  38.8 1.2 %fusion.31 = f32[64,16,128]{2,1,0:T(8,128)S(1)} fusion(f32[64,16,128]{2,1,0:T(8,128)S(1)} %fusion.4, bf16[256,64,16]{0,2,1:T(8,128)(2,1)S(1)} %bitcast.92, pred[128,256]{1,0:T(8,128)(4,1)S(1)} %get-tuple-element.44, f32[64,128,256]{2,1,0:T(8,128)S(1)} %copy-done), kind=kOutput, calls=%fused_computation.37 | convolution fusion | flops 71434240 | bytes 9994240 | tf_op jit(solution)/shard_map/dot_general | solution.py:78
  40.4 3.4 %collective-permute-done.1 = bf16[2,256,1024]{1,2,0:T(8,128)(2,1)} collective-permute-done((bf16[2,256,1024]{1,2,0:T(8,128)(2,1)}, bf16[2,256,1024]{1,2,0:T(8,128)(2,1)}, u32[]{:S(2)}, u32[]{:S(2)}) %collective-permute-start.1) | collective-permute-done | bytes 1048608 | tf_op jit(solution)/shard_map/ppermute | solution.py:18
  43.8 2.3 %fusion.93 = (bf16[1,256,1024]{1,2,0:T(8,128)(2,1)}, bf16[256,1024]{0,1:T(8,128)(2,1)S(1)}, bf16[256,1024]{0,1:T(8,128)(2,1)}, bf16[1,256,1024]{1,2,0:T(8,128)(2,1)S(1)}) fusion(bf16[2,256,1024]{1,2,0:T(8,128)(2,1)} %collective-permute-done.1), kind=kLoop, calls=%fused_computation.135 | loop fusion | bytes 3145728 | tf_op jit(solution)/shard_map/slice | solution.py:140
  47.1 2.2 %pad_maximum_fusion.1 = (bf16[512,512]{0,1:T(8,128)(2,1)}, bf16[512,512]{0,1:T(8,128)(2,1)S(1)}, bf16[512,512]{0,1:T(8,128)(2,1)S(1)}, bf16[512,512]{0,1:T(8,128)(2,1)}) fusion(bf16[256,1024]{0,1:T(8,128)(2,1)S(1)} %copy.86, bf16[256,1024]{0,1:T(8,128)(2,1)S(1)} %get-tuple-element.34, bf16[256,1024]{0,1:T(8,128)(2,1)S(1)} %copy.85, ...), kind=kLoop, calls=%fused_computation.74 | loop fusion | flops 4194304 | bytes 4194304 | tf_op jit(solution)/shard_map/concatenate | solution.py:140
  50.5 1.5 %convolution_bitcast_fusion.1 = f32[256,4,128]{0,2,1:T(8,128)} fusion(bf16[512,4,128]{0,2,1:T(8,128)(2,1)S(1)} %bitcast.104, f32[4,512,256]{2,1,0:T(8,128)S(1)} %get-tuple-element.46, f32[4,256]{1,0:T(4,128)S(1)} %get-tuple-element.45, pred[256,512]{0,1:T(8,128)(4,1)S(1)} %get-tuple-element.40), kind=kOutput, calls=%fused_computation.36 | convolution fusion | flops 136839168 | bytes 3280896 | tf_op jit(solution)/shard_map/hqk,khd->qhd/dot_general | solution.py:108
  52.0 2.0 %fusion.12 = (f32[8,256]{1,0:T(8,128)S(1)}, f32[8,256,512]{2,1,0:T(8,128)S(1)}) fusion(pred[256,512]{1,0:T(8,128)(4,1)S(1)} %copy-done.6, bf16[256,8,128]{2,0,1:T(8,128)(2,1)S(1)} %copy-done.9, bf16[256,8,128]{2,0,1:T(8,128)(2,1)S(1)} %copy-done.10, bf16[256,1024]{1,0:T(8,128)(2,1)} %collective-permute-done.2), kind=kOutput, calls=%fused_computation.15 | convolution fusion | flops 273676288 | bytes 5906432 | tf_op jit(solution)/shard_map/qhd,khd->hqk/dot_general | solution.py:101
  54.0 1.6 %fusion.13 = f32[8,256]{1,0:T(8,128)S(1)} fusion(f32[8,256,512]{2,1,0:T(8,128)S(1)} %get-tuple-element.48, f32[8,256]{1,0:T(8,128)S(1)} %get-tuple-element.47, pred[256,512]{1,0:T(8,128)(4,1)S(1)} %copy-done.6), kind=kLoop, calls=%fused_computation.16 | loop fusion | flops 5240832 | bytes 4341760 | tf_op jit(solution)/shard_map/reduce_sum | solution.py:107
  55.6 1.6 %fusion.28 = bf16[8,128,256]{2,1,0:T(8,128)(2,1)S(1)} fusion(f32[8,256,512]{2,1,0:T(8,128)S(1)} %get-tuple-element.48, f32[8,256]{1,0:T(8,128)S(1)} %get-tuple-element.47, pred[256,512]{1,0:T(8,128)(4,1)S(1)} %copy-done.6, bf16[256,8,128]{0,2,1:T(8,128)(2,1)S(1)} %bitcast.94, bf16[256,8,128]{0,2,1:T(8,128)(2,1)S(1)} %bitcast.102), kind=kOutput, calls=%fused_computation.34 | convolution fusion | flops 276037632 | bytes 5906432 | tf_op jit(solution)/shard_map/hqk,khd->qhd/dot_general | solution.py:108
  58.4 7.0 %fusion = f32[64,16,128]{2,1,0:T(8,128)S(1)} fusion(bf16[256,64,16]{0,2,1:T(8,128)(2,1)S(1)} %bitcast.89, pred[128,256]{1,0:T(8,128)(4,1)S(1)} %copy-done.16, f32[64,128,256]{2,1,0:T(8,128)} %shard_map.113), kind=kOutput, calls=%fused_computation.1 | convolution fusion | flops 77594624 | bytes 9469952 | tf_op jit(solution)/shard_map/dot_general | solution.py:79
  65.4 4.7 %fusion.34 = f32[64,16,128]{2,1,0:T(8,128)S(1)} fusion(f32[64,16,128]{2,1,0:T(8,128)S(1)} %fusion, bf16[256,64,16]{0,2,1:T(8,128)(2,1)S(1)} %bitcast.90, pred[128,256]{1,0:T(8,128)(4,1)S(1)} %copy-done.16, f32[64,128,256]{2,1,0:T(8,128)} %shard_map.113), kind=kOutput, calls=%fused_computation.38 | convolution fusion | flops 71434240 | bytes 9994240 | tf_op jit(solution)/shard_map/dot_general | solution.py:78
  71.4 2.1 %collective-permute-start.6 = (bf16[256,1152]{0,1:T(8,128)(2,1)S(1)}, bf16[256,1152]{0,1:T(8,128)(2,1)S(1)}, u32[]{:S(2)}, u32[]{:S(2)}) collective-permute-start(bf16[256,1152]{0,1:T(8,128)(2,1)S(1)} %copy-done.15), channel_id=1, source_target_pairs={{0,16},{8,24},{16,32},{24,40},{32,48},{40,56},{48,64},{56,72},{64,... | collective-permute-start | bytes 1769480 | tf_op jit(solution)/shard_map/ppermute | solution.py:18
  74.1 1.6 %collective-permute-start.4 = (f32[256]{0:T(256)S(1)}, f32[256]{0:T(256)S(1)}, u32[]{:S(2)}, u32[]{:S(2)}) collective-permute-start(f32[256]{0:T(256)S(1)} %add.107), channel_id=1, source_target_pairs={{0,2},{1,3},{2,0},{3,1},{4,6},{5,7},{6,4},{7,5},{8,10},{9,11},{10,... | collective-permute-start | bytes 3080 | tf_op jit(solution)/shard_map/ppermute | solution.py:90
  76.4 1.4 %collective-permute-done.4 = f32[256]{0:T(256)S(1)} collective-permute-done((f32[256]{0:T(256)S(1)}, f32[256]{0:T(256)S(1)}, u32[]{:S(2)}, u32[]{:S(2)}) %collective-permute-start.4) | collective-permute-done | bytes 1056 | tf_op jit(solution)/shard_map/ppermute | solution.py:90
  77.8 3.0 %collective-permute-start.5 = (f32[256]{0:T(256)S(1)}, f32[256]{0:T(256)S(1)}, u32[]{:S(2)}, u32[]{:S(2)}) collective-permute-start(f32[256]{0:T(256)S(1)} %add.108), channel_id=1, source_target_pairs={{0,4},{1,5},{2,6},{3,7},{4,0},{5,1},{6,2},{7,3},{8,12},{9,13},{10,... | collective-permute-start | bytes 3080 | tf_op jit(solution)/shard_map/ppermute | solution.py:90
  81.3 1.5 %collective-permute-done.5 = f32[256]{0:T(256)S(1)} collective-permute-done((f32[256]{0:T(256)S(1)}, f32[256]{0:T(256)S(1)}, u32[]{:S(2)}, u32[]{:S(2)}) %collective-permute-start.5) | collective-permute-done | bytes 1056 | tf_op jit(solution)/shard_map/ppermute | solution.py:90
  83.9 19.8 %collective-permute-done.6 = bf16[256,1152]{0,1:T(8,128)(2,1)S(1)} collective-permute-done((bf16[256,1152]{0,1:T(8,128)(2,1)S(1)}, bf16[256,1152]{0,1:T(8,128)(2,1)S(1)}, u32[]{:S(2)}, u32[]{:S(2)}) %collective-permute-start.6) | collective-permute-done | bytes 589856 | tf_op jit(solution)/shard_map/ppermute | solution.py:18
  (91 shorter events, 15.7 us)
Async XLA Ops:
  0.6 12.9 %copy-start.7 = (bf16[256,1024]{1,0:T(8,128)(2,1)S(1)}, bf16[256,1024]{1,0:T(8,128)(2,1)}, u32[]{:S(2)}) copy-start(bf16[256,1024]{1,0:T(8,128)(2,1)} %param.17) | copy-start | bytes 1572868
  0.6 13.1 %copy-start.8 = (bf16[256,1024]{1,0:T(8,128)(2,1)S(1)}, bf16[256,1024]{1,0:T(8,128)(2,1)}, u32[]{:S(2)}) copy-start(bf16[256,1024]{1,0:T(8,128)(2,1)} %param.18) | copy-start | bytes 1572868
  2.2 28.1 %collective-permute-start = (bf16[127,1024]{1,0:T(8,128)(2,1)S(1)}, bf16[127,1024]{1,0:T(8,128)(2,1)S(1)}, u32[]{:S(2)}, u32[]{:S(2)}) collective-permute-start(bf16[127,1024]{1,0:T(8,128)(2,1)S(1)} %slice.80), channel_id=1, source_target_pairs={{0,8},{8,16},{16,24},{24,32},{32,40},{40,48},{48,56},{56,64},{64,7... | collective-permute-start | bytes 780296 | tf_op jit(solution)/shard_map/ppermute | solution.py:18
  6.0 45.9 %collective-permute-start.2 = (bf16[256,1024]{1,0:T(8,128)(2,1)}, bf16[256,1024]{1,0:T(8,128)(2,1)}, u32[]{:S(2)}, u32[]{:S(2)}) collective-permute-start(bf16[256,1024]{1,0:T(8,128)(2,1)} %param.16), channel_id=1, source_target_pairs={{16,0},{24,8},{32,16},{40,24},{48,32},{56,40},{64,48},{72,56},{80,... | collective-permute-start | bytes 1572872 | tf_op jit(solution)/shard_map/ppermute | solution.py:18
  13.8 5.1 %copy-start.19 = (s32[32]{0:T(128)S(1)}, s32[32]{0:T(128)}, u32[]{:S(2)}) copy-start(s32[32]{0:T(128)} %param.19) | copy-start | bytes 388
  13.8 5.6 %copy-start.17 = (f32[64,128]{1,0:T(8,128)S(1)}, f32[64,128]{1,0:T(8,128)}, u32[]{:S(2)}) copy-start(f32[64,128]{1,0:T(8,128)} %param.14) | copy-start | bytes 98308
  15.1 28.6 %collective-permute-start.1 = (bf16[2,256,1024]{1,2,0:T(8,128)(2,1)}, bf16[2,256,1024]{1,2,0:T(8,128)(2,1)}, u32[]{:S(2)}, u32[]{:S(2)}) collective-permute-start(bf16[2,256,1024]{1,2,0:T(8,128)(2,1)} %pad_maximum_fusion), channel_id=1, source_target_pairs={{0,8},{8,16},{16,24},{24,32},{32,40},{40,48},{48,56},{56,64},{64,7... | collective-permute-start | bytes 3145736 | tf_op jit(solution)/shard_map/ppermute | solution.py:18
  30.6 8.2 %copy-start = (f32[64,128,256]{2,1,0:T(8,128)S(1)}, f32[64,128,256]{2,1,0:T(8,128)}, u32[]{:S(2)}) copy-start(f32[64,128,256]{2,1,0:T(8,128)} %shard_map.113) | copy-start | bytes 25165828
  47.1 2.2 %copy-start.4 = (bf16[256,512]{0,1:T(8,128)(2,1)S(1)}, bf16[256,512]{0,1:T(8,128)(2,1)}, u32[]{:S(2)}) copy-start(bf16[256,512]{0,1:T(8,128)(2,1)} %copy.113) | copy-start | bytes 786436
  50.5 1.5 %copy-start.6 = (pred[256,512]{1,0:T(8,128)(4,1)S(1)}, pred[256,512]{1,0:T(8,128)(4,1)}, u32[]{:S(2)}) copy-start(pred[256,512]{1,0:T(8,128)(4,1)} %copy.88) | copy-start | bytes 393220
  50.5 1.5 %copy-start.9 = (bf16[256,8,128]{2,0,1:T(8,128)(2,1)S(1)}, bf16[256,8,128]{2,0,1:T(8,128)(2,1)}, u32[]{:S(2)}) copy-start(bf16[256,8,128]{2,0,1:T(8,128)(2,1)} %copy.97) | copy-start | bytes 1572868
  50.5 1.5 %copy-start.10 = (bf16[256,8,128]{2,0,1:T(8,128)(2,1)S(1)}, bf16[256,8,128]{2,0,1:T(8,128)(2,1)}, u32[]{:S(2)}) copy-start(bf16[256,8,128]{2,0,1:T(8,128)(2,1)} %copy.96) | copy-start | bytes 1572868
  54.0 1.6 %copy-start.12 = (bf16[1,256,1024]{1,2,0:T(8,128)(2,1)S(1)}, bf16[1,256,1024]{1,2,0:T(8,128)(2,1)}, u32[]{:S(2)}) copy-start(bf16[1,256,1024]{1,2,0:T(8,128)(2,1)} %get-tuple-element.33) | copy-start | bytes 1572868
  65.4 4.9 %copy-start.1 = (bf16[256,1024]{1,0:T(8,128)(2,1)S(1)}, bf16[256,1024]{1,0:T(8,128)(2,1)}, u32[]{:S(2)}) copy-start(bf16[256,1024]{1,0:T(8,128)(2,1)} %param.11) | copy-start | bytes 1572868
  65.4 4.9 %copy-start.2 = (bf16[256,1024]{1,0:T(8,128)(2,1)S(1)}, bf16[256,1024]{1,0:T(8,128)(2,1)}, u32[]{:S(2)}) copy-start(bf16[256,1024]{1,0:T(8,128)(2,1)} %param.10) | copy-start | bytes 1572868
  70.0 3.4 %copy-start.3 = (bf16[512,512]{0,1:T(8,128)(2,1)S(1)}, bf16[512,512]{0,1:T(8,128)(2,1)}, u32[]{:S(2)}) copy-start(bf16[512,512]{0,1:T(8,128)(2,1)} %get-tuple-element.16) | copy-start | bytes 1572868
  70.0 3.4 %copy-start.5 = (bf16[256,512]{1,0:T(8,128)(2,1)S(1)}, bf16[256,512]{1,0:T(8,128)(2,1)}, u32[]{:S(2)}) copy-start(bf16[256,512]{1,0:T(8,128)(2,1)} %get-tuple-element.15) | copy-start | bytes 786436
  70.3 5.4 %copy-start.13 = (bf16[512,512]{0,1:T(8,128)(2,1)S(1)}, bf16[512,512]{0,1:T(8,128)(2,1)}, u32[]{:S(2)}) copy-start(bf16[512,512]{0,1:T(8,128)(2,1)} %get-tuple-element.14) | copy-start | bytes 1572868
  70.6 3.5 %collective-permute-start.3 = (f32[256]{0:T(256)S(1)}, f32[256]{0:T(256)S(1)}, u32[]{:S(2)}, u32[]{:S(2)}) collective-permute-start(f32[256]{0:T(256)S(1)} %multiply_reduce_fusion), channel_id=1, source_target_pairs={{0,1},{1,0},{2,3},{3,2},{4,5},{5,4},{6,7},{7,6},{8,9},{9,8},{10,11... | collective-permute-start | bytes 3080 | tf_op jit(solution)/shard_map/ppermute | solution.py:90
  71.4 32.3 %collective-permute-start.6 = (bf16[256,1152]{0,1:T(8,128)(2,1)S(1)}, bf16[256,1152]{0,1:T(8,128)(2,1)S(1)}, u32[]{:S(2)}, u32[]{:S(2)}) collective-permute-start(bf16[256,1152]{0,1:T(8,128)(2,1)S(1)} %copy-done.15), channel_id=1, source_target_pairs={{0,16},{8,24},{16,32},{24,40},{32,48},{40,56},{48,64},{56,72},{64,... | collective-permute-start | bytes 1769480 | tf_op jit(solution)/shard_map/ppermute | solution.py:18
  74.1 3.7 %collective-permute-start.4 = (f32[256]{0:T(256)S(1)}, f32[256]{0:T(256)S(1)}, u32[]{:S(2)}, u32[]{:S(2)}) collective-permute-start(f32[256]{0:T(256)S(1)} %add.107), channel_id=1, source_target_pairs={{0,2},{1,3},{2,0},{3,1},{4,6},{5,7},{6,4},{7,5},{8,10},{9,11},{10,... | collective-permute-start | bytes 3080 | tf_op jit(solution)/shard_map/ppermute | solution.py:90
  76.4 6.5 %copy-start.18 = (f32[1024]{0:T(1024)S(1)}, f32[1024]{0:T(1024)}, u32[]{:S(2)}) copy-start(f32[1024]{0:T(1024)} %param.15) | copy-start | bytes 12292
  77.8 26.0 %copy-start.11 = (f32[256,4,128]{0,2,1:T(8,128)S(1)}, f32[256,4,128]{0,2,1:T(8,128)}, u32[]{:S(2)}) copy-start(f32[256,4,128]{0,2,1:T(8,128)} %convolution_bitcast_fusion.1) | copy-start | bytes 1572868
  77.8 5.1 %collective-permute-start.5 = (f32[256]{0:T(256)S(1)}, f32[256]{0:T(256)S(1)}, u32[]{:S(2)}, u32[]{:S(2)}) collective-permute-start(f32[256]{0:T(256)S(1)} %add.108), channel_id=1, source_target_pairs={{0,4},{1,5},{2,6},{3,7},{4,0},{5,1},{6,2},{7,3},{8,12},{9,13},{10,... | collective-permute-start | bytes 3080 | tf_op jit(solution)/shard_map/ppermute | solution.py:90
  (3 other events, 3.2 us)

commit v11 on v8

--- a/solution.py
+++ b/solution.py
@@ -26,11 +26,14 @@
     return jnp.max(jnp.where(starts[None, :] <= positions[:, None], starts[None, :], 0), axis=1)
 
 
-def toeplitz_rows(reversed_ref, out_ref):
-    rows = out_ref.shape[1]
-    for group in range(out_ref.shape[0]):
+def toeplitz_rows(reversed_ref, upper_ref, lower_ref):
+    rows = upper_ref.shape[1]
+    for group in range(upper_ref.shape[0]):
         line = jnp.broadcast_to(reversed_ref[group : group + 1, :], (rows, reversed_ref.shape[1]))
-        out_ref[group] = pltpu.roll(line, 0, 1, stride=1, stride_axis=0)
+        rolled = pltpu.roll(line, 0, 1, stride=1, stride_axis=0)
+        upper = rolled.astype(jnp.bfloat16)
+        upper_ref[group] = upper
+        lower_ref[group] = (rolled - upper.astype(jnp.float32)).astype(jnp.bfloat16)
 
 
 def build_toeplitz(filter_taps):
@@ -39,13 +42,14 @@
     reversed_taps = jnp.concatenate(
         [filter_taps[:, ::-1], jnp.zeros((groups, span - taps), jnp.float32)], axis=1
     )
-    step = 8
+    step = 32
+    part = jax.ShapeDtypeStruct((groups, taps, span), jnp.bfloat16)
     return pl.pallas_call(
         toeplitz_rows,
         grid=(groups // step,),
         in_specs=[pl.BlockSpec((step, span), lambda i: (i, 0))],
-        out_specs=pl.BlockSpec((step, taps, span), lambda i: (i, 0, 0)),
-        out_shape=jax.ShapeDtypeStruct((groups, taps, span), jnp.float32),
+        out_specs=[pl.BlockSpec((step, taps, span), lambda i: (i, 0, 0))] * 2,
+        out_shape=[part, part],
     )(reversed_taps)
 
 
@@ -59,9 +63,7 @@
         + (taps - 1)
         - jnp.arange(span, dtype=jnp.int32)[None, :]
     )
-    toeplitz = build_toeplitz(filter_taps)
-    upper_part = toeplitz.astype(jnp.bfloat16)
-    lower_part = (toeplitz - upper_part.astype(jnp.float32)).astype(jnp.bfloat16)
+    upper_part, lower_part = build_toeplitz(filter_taps)
     zero_half = jnp.zeros((), jnp.bfloat16)
     numbers = (((0,), (2,)), ((1,), (0,)))
     extended = jnp.concatenate([extended, jnp.zeros((1, channels), extended.dtype)], axis=0)

time: 102 us -> 96.1 us (0.942)
  matrix products: 27.5 us -> 17 us
  waiting for transfers between devices: 27.5 us -> 33.1 us
  Pallas kernels: 6.75 us -> 5.13 us
    dot_general x2, matrix products: 14.1 us -> 7.2 us  [causal_filter(): lax.dot_general(sources, kernel_lower, numbers, preferred_element_type=jn...]
    ppermute x4, waiting for transfers between devices: 22.2 us -> 27.8 us  [shifted(): lax.ppermute(value, axis, [(source, source + steps) for source in range(f...]
    dot_general x2, matrix products: 5.9 us -> 3.2 us  [causal_filter(): lax.dot_general(sources, kernel_upper, numbers, preferred_element_type=jn...]
    pallas_call x1, Pallas kernels: 6.75 us -> 5.13 us  [build_toeplitz(): pl.pallas_call(toeplitz_rows, grid=(groups // step,), in_specs=[pl.BlockS...]
    dot_general x2, matrix products: 3.55 us -> 2.49 us  [attend_block(): jnp.einsum('hqk,khd->qhd', expo.astype(jnp.bfloat16), value_heads, prefer...]
    reshape x2, local copies, waits for them, and re-layouts: 0.42 us -> 1.46 us  [causal_filter(): results.append(result.transpose(2, 0, 1).reshape(taps, channels))]
  transfers between devices with their start and end apart: 7 -> 7, of which waited for: 5 -> 5; matrix products, arithmetic and copies ran while one was open for 25% -> 23% of each run, Pallas kernels for 7% -> 5%
where the time goes in v11:
time: 96.1 us; the launch traced here: 95.5 us
  waiting for transfers between devices  33.1 us (34%)
  starting transfers between devices  19.7 us (20%)
  matrix products  17 us (18%)
  local copies, waits for them, and re-layouts  10.3 us (11%)
  other arithmetic  9.26 us (10%)
  Pallas kernels  5.13 us (5%)
  between operations  1.06 us (1%)
    ppermute x4, waiting for transfers between devices, shifted(): lax.ppermute(value, axis, [(source, source + steps) for source in range(f...  27.8 us
    ppermute x4, starting transfers between devices, shifted(): lax.ppermute(value, axis, [(source, source + steps) for source in range(f...  15.1 us
    dot_general x2, matrix products, causal_filter(): lax.dot_general(sources, kernel_lower, numbers, preferred_element_type=jn...  7.2 us
    ppermute x3, waiting for transfers between devices, tp_sum(): lax.ppermute(value, 'tp', [(i, i ^ stride) for i in range(count)])  5.3 us
    pallas_call x1, Pallas kernels, build_toeplitz(): pl.pallas_call(toeplitz_rows, grid=(groups // step,), in_specs=[pl.BlockS...  5.13 us
    ppermute x3, starting transfers between devices, tp_sum(): lax.ppermute(value, 'tp', [(i, i ^ stride) for i in range(count)])  4.59 us
    unnamed x36, local copies, waits for them, and re-layouts  4.55 us
    dot_general x2, matrix products, attend_block(): jnp.einsum('qhd,khd->hqk', query_heads, key_heads, preferred_element_type...  4.07 us
  transfers between devices with their start and end apart: 7, of which 5 were waited for; matrix products, arithmetic and copies ran while one was open for 23% of the time, Pallas kernels for 5%

profile of v11, /device:TPU:24, one launch (start us, length us, event | category | flops | bytes accessed | tf_op | source)
XLA Modules:
  0.0 95.5 jit_solution(12519569177212677529)
XLA Ops:
  0.7 1.4 %multiply_convert_fusion.1 = bf16[256,1024]{1,0:T(8,128)(2,1)S(1)} fusion(bf16[256,1024]{1,0:T(8,128)(2,1)} %param.13, bf16[256,1024]{1,0:T(8,128)(2,1)} %param.12), kind=kLoop, calls=%fused_computation.45 | loop fusion | flops 1048576 | bytes 1572864 | tf_op jit(solution)/shard_map/convert_element_type | solution.py:134
  2.1 3.8 %collective-permute-start = (bf16[127,1024]{1,0:T(8,128)(2,1)S(1)}, bf16[127,1024]{1,0:T(8,128)(2,1)S(1)}, u32[]{:S(2)}, u32[]{:S(2)}) collective-permute-start(bf16[127,1024]{1,0:T(8,128)(2,1)S(1)} %slice.56), channel_id=1, source_target_pairs={{0,8},{8,16},{16,24},{24,32},{32,40},{40,48},{48,56},{56,64},{64,7... | collective-permute-start | bytes 780296 | tf_op jit(solution)/shard_map/ppermute | solution.py:18
  6.0 7.5 %collective-permute-start.2 = (bf16[256,1024]{1,0:T(8,128)(2,1)}, bf16[256,1024]{1,0:T(8,128)(2,1)}, u32[]{:S(2)}, u32[]{:S(2)}) collective-permute-start(bf16[256,1024]{1,0:T(8,128)(2,1)} %param.16), channel_id=1, source_target_pairs={{16,0},{24,8},{32,16},{40,24},{48,32},{56,40},{64,48},{72,56},{80,... | collective-permute-start | bytes 1572872 | tf_op jit(solution)/shard_map/ppermute | solution.py:18
  13.5 1.2 %copy.41 = bf16[256,1024]{0,1:T(8,128)(2,1)S(1)} copy(bf16[256,1024]{1,0:T(8,128)(2,1)} %param.17) | data formatting | bytes 1048576 | tf_op args[7]
  14.7 1.2 %copy.42 = bf16[256,1024]{0,1:T(8,128)(2,1)S(1)} copy(bf16[256,1024]{1,0:T(8,128)(2,1)} %param.18) | data formatting | bytes 1048576 | tf_op args[8]
  17.1 1.9 %collective-permute-start.1 = (bf16[2,256,1024]{1,2,0:T(8,128)(2,1)}, bf16[2,256,1024]{1,2,0:T(8,128)(2,1)S(1)}, u32[]{:S(2)}, u32[]{:S(2)}) collective-permute-start(bf16[2,256,1024]{1,2,0:T(8,128)(2,1)} %pad_maximum_fusion), channel_id=1, source_target_pairs={{0,8},{8,16},{16,24},{24,32},{32,40},{40,48},{48,56},{56,64},{64,7... | collective-permute-start | bytes 3145736 | tf_op jit(solution)/shard_map/ppermute | solution.py:18
  21.7 5.1 %shard_map.113 = (bf16[64,128,256]{2,1,0:T(8,128)(2,1)}, bf16[64,128,256]{2,1,0:T(8,128)(2,1)}) custom-call(f32[64,256]{1,0:T(8,128)} %concatenate.36.reversed_ref), custom_call_target="tpu_custom_call" | custom-call | tf_op jit(solution)/shard_map/pallas_call | solution.py:47
  29.0 3.7 %fusion.4 = f32[64,16,128]{2,1,0:T(8,128)S(1)} fusion(bf16[256,64,16]{0,2,1:T(8,128)(2,1)} %bitcast.73, bf16[64,128,256]{2,1,0:T(8,128)(2,1)} %get-tuple-element.11, pred[128,256]{1,0:T(8,128)(4,1)S(1)} %get-tuple-element.36), kind=kOutput, calls=%fused_computation.8 | convolution fusion | flops 69206016 | bytes 5275648 | tf_op jit(solution)/shard_map/dot_general | solution.py:81
  32.7 1.2 %fusion.34 = f32[64,16,128]{2,1,0:T(8,128)S(1)} fusion(f32[64,16,128]{2,1,0:T(8,128)S(1)} %fusion.4, bf16[256,64,16]{0,2,1:T(8,128)(2,1)S(1)} %bitcast.74, bf16[64,128,256]{2,1,0:T(8,128)(2,1)S(1)} %copy-done.13, pred[128,256]{1,0:T(8,128)(4,1)S(1)} %get-tuple-element.36), kind=kOutput, calls=%fused_computation.32 | convolution fusion | flops 69337088 | bytes 5799936 | tf_op jit(solution)/shard_map/dot_general | solution.py:80
  34.1 1.2 %maximum_maximum_fusion = bf16[384,1024]{1,0:T(8,128)(2,1)S(1)} fusion(bf16[256,1024]{1,0:T(8,128)(2,1)S(1)} %multiply_convert_fusion.1, bf16[127,1024]{1,0:T(8,128)(2,1)} %copy-done.2, bf16[384]{0:T(512)(128)(2,1)S(1)} %pad.5.clone), kind=kLoop, calls=%fused_computation.46 | loop fusion | flops 2359296 | bytes 1571584 | tf_op jit(solution)/shard_map/concatenate | solution.py:69
  35.3 10.3 %collective-permute-done.1 = bf16[2,256,1024]{1,2,0:T(8,128)(2,1)S(1)} collective-permute-done((bf16[2,256,1024]{1,2,0:T(8,128)(2,1)}, bf16[2,256,1024]{1,2,0:T(8,128)(2,1)S(1)}, u32[]{:S(2)}, u32[]{:S(2)}) %collective-permute-start.1) | collective-permute-done | bytes 1048608 | tf_op jit(solution)/shard_map/ppermute | solution.py:18
  46.8 2.2 %fusion.13 = (f32[8,256]{1,0:T(8,128)S(1)}, f32[8,512,256]{2,1,0:T(8,128)S(1)}) fusion(pred[256,512]{0,1:T(8,128)(4,1)} %get-tuple-element.32, bf16[256,8,128]{2,0,1:T(8,128)(2,1)} %copy.46, bf16[256,8,128]{2,0,1:T(8,128)(2,1)S(1)} %copy.45, bf16[256,1024]{1,0:T(8,128)(2,1)} %param.16), kind=kOutput, calls=%fused_computation.17 | convolution fusion | flops 273676288 | bytes 5906432 | tf_op jit(solution)/shard_map/qhd,khd->hqk/dot_general | solution.py:103
  50.1 1.2 %fusion.28 = f32[256,8,128]{0,2,1:T(8,128)S(1)} fusion(f32[8,512,256]{2,1,0:T(8,128)S(1)} %get-tuple-element.38, f32[8,256]{1,0:T(8,128)S(1)} %get-tuple-element.37, pred[256,512]{0,1:T(8,128)(4,1)S(1)} %copy-done.3, bf16[256,8,128]{0,2,1:T(8,128)(2,1)S(1)} %bitcast.65, bf16[256,8,128]{0,2,1:T(8,128)(2,1)S(1)} %bitcast.77), kind=kOutput, calls=%fused_computation.30 | convolution fusion | flops 275775488 | bytes 6430720 | tf_op jit(solution)/shard_map/hqk,khd->qhd/dot_general | solution.py:110
  51.4 1.9 %fusion.12 = (f32[8,256]{1,0:T(8,128)S(1)}, f32[8,256,512]{1,2,0:T(8,128)S(1)}) fusion(pred[256,512]{0,1:T(8,128)(4,1)S(1)} %get-tuple-element.31, bf16[256,8,128]{2,0,1:T(8,128)(2,1)S(1)} %copy-done.4, bf16[256,8,128]{2,0,1:T(8,128)(2,1)S(1)} %copy-done.6, bf16[256,1024]{1,0:T(8,128)(2,1)} %collective-permute-done.2), kind=kOutput, calls=%fused_computation.16 | convolution fusion | flops 273676288 | bytes 5906432 | tf_op jit(solution)/shard_map/qhd,khd->hqk/dot_general | solution.py:103
  53.2 1.3 %fusion.31 = bf16[8,128,256]{2,1,0:T(8,128)(2,1)S(1)} fusion(f32[8,256,512]{1,2,0:T(8,128)S(1)} %get-tuple-element.40, f32[8,256]{1,0:T(8,128)S(1)} %get-tuple-element.39, pred[256,512]{0,1:T(8,128)(4,1)S(1)} %get-tuple-element.31, bf16[256,8,128]{0,2,1:T(8,128)(2,1)S(1)} %bitcast.66, bf16[256,8,128]{0,2,1:T(8,128)(2,1)S(1)} %bitcast.78), kind=kOutput, calls=%fused_computation.31 | convolution fusion | flops 276037632 | bytes 5906432 | tf_op jit(solution)/shard_map/hqk,khd->qhd/dot_general | solution.py:110
  56.7 3.5 %fusion = f32[64,16,128]{2,1,0:T(8,128)S(1)} fusion(bf16[256,64,16]{0,2,1:T(8,128)(2,1)S(1)} %bitcast.70, bf16[64,128,256]{2,1,0:T(8,128)(2,1)} %get-tuple-element.11, pred[128,256]{1,0:T(8,128)(4,1)} %get-tuple-element.35), kind=kOutput, calls=%fused_computation.1 | convolution fusion | flops 69206016 | bytes 5275648 | tf_op jit(solution)/shard_map/dot_general | solution.py:81
  60.3 2.0 %fusion.37 = f32[64,16,128]{2,1,0:T(8,128)} fusion(f32[64,16,128]{2,1,0:T(8,128)S(1)} %fusion, bf16[256,64,16]{0,2,1:T(8,128)(2,1)S(1)} %bitcast.71, bf16[64,128,256]{2,1,0:T(8,128)(2,1)S(1)} %copy-done.14, pred[128,256]{1,0:T(8,128)(4,1)S(1)} %copy-done.11), kind=kOutput, calls=%fused_computation.33 | convolution fusion | flops 69337088 | bytes 5799936 | tf_op jit(solution)/shard_map/dot_general | solution.py:80
  62.3 1.2 %copy.54 = f32[128,1024]{1,0:T(8,128)S(1)} copy(f32[128,1024]{0,1:T(8,128)} %bitcast.75) | data formatting | bytes 1048576 | tf_op jit(solution)/shard_map/reshape | solution.py:84
  63.6 1.9 %collective-permute-start.6 = (bf16[256,1152]{0,1:T(8,128)(2,1)}, bf16[256,1152]{0,1:T(8,128)(2,1)S(1)}, u32[]{:S(2)}, u32[]{:S(2)}) collective-permute-start(bf16[256,1152]{0,1:T(8,128)(2,1)} %copy-done.9), channel_id=1, source_target_pairs={{0,16},{8,24},{16,32},{24,40},{32,48},{40,56},{48,64},{56,72},{64,... | collective-permute-start | bytes 1769480 | tf_op jit(solution)/shard_map/ppermute | solution.py:18
  67.1 1.5 %collective-permute-start.4 = (f32[256]{0:T(256)S(1)}, f32[256]{0:T(256)S(1)}, u32[]{:S(2)}, u32[]{:S(2)}) collective-permute-start(f32[256]{0:T(256)S(1)} %add.106), channel_id=1, source_target_pairs={{0,2},{1,3},{2,0},{3,1},{4,6},{5,7},{6,4},{7,5},{8,10},{9,11},{10,... | collective-permute-start | bytes 3080 | tf_op jit(solution)/shard_map/ppermute | solution.py:92
  68.5 2.1 %collective-permute-done.4 = f32[256]{0:T(256)S(1)} collective-permute-done((f32[256]{0:T(256)S(1)}, f32[256]{0:T(256)S(1)}, u32[]{:S(2)}, u32[]{:S(2)}) %collective-permute-start.4) | collective-permute-done | bytes 1056 | tf_op jit(solution)/shard_map/ppermute | solution.py:92
  70.6 3.0 %collective-permute-start.5 = (f32[256]{0:T(256)S(1)}, f32[256]{0:T(256)S(1)}, u32[]{:S(2)}, u32[]{:S(2)}) collective-permute-start(f32[256]{0:T(256)S(1)} %add.107), channel_id=1, source_target_pairs={{0,4},{1,5},{2,6},{3,7},{4,0},{5,1},{6,2},{7,3},{8,12},{9,13},{10,... | collective-permute-start | bytes 3080 | tf_op jit(solution)/shard_map/ppermute | solution.py:92
  73.7 2.1 %collective-permute-done.5 = f32[256]{0:T(256)S(1)} collective-permute-done((f32[256]{0:T(256)S(1)}, f32[256]{0:T(256)S(1)}, u32[]{:S(2)}, u32[]{:S(2)}) %collective-permute-start.5) | collective-permute-done | bytes 1056 | tf_op jit(solution)/shard_map/ppermute | solution.py:92
  76.7 17.5 %collective-permute-done.6 = bf16[256,1152]{0,1:T(8,128)(2,1)S(1)} collective-permute-done((bf16[256,1152]{0,1:T(8,128)(2,1)}, bf16[256,1152]{0,1:T(8,128)(2,1)S(1)}, u32[]{:S(2)}, u32[]{:S(2)}) %collective-permute-start.6) | collective-permute-done | bytes 589856 | tf_op jit(solution)/shard_map/ppermute | solution.py:18
  (76 shorter events, 14.5 us)
Async XLA Ops:
  0.6 18.4 %copy-start.15 = (s32[32]{0:T(128)S(1)}, s32[32]{0:T(128)}, u32[]{:S(2)}) copy-start(s32[32]{0:T(128)} %param.19) | copy-start | bytes 388
  0.6 19.4 %copy-start.10 = (f32[64,128]{1,0:T(8,128)S(1)}, f32[64,128]{1,0:T(8,128)}, u32[]{:S(2)}) copy-start(f32[64,128]{1,0:T(8,128)} %param.14) | copy-start | bytes 98308
  2.1 25.7 %collective-permute-start = (bf16[127,1024]{1,0:T(8,128)(2,1)S(1)}, bf16[127,1024]{1,0:T(8,128)(2,1)S(1)}, u32[]{:S(2)}, u32[]{:S(2)}) collective-permute-start(bf16[127,1024]{1,0:T(8,128)(2,1)S(1)} %slice.56), channel_id=1, source_target_pairs={{0,8},{8,16},{16,24},{24,32},{32,40},{40,48},{48,56},{56,64},{64,7... | collective-permute-start | bytes 780296 | tf_op jit(solution)/shard_map/ppermute | solution.py:18
  6.0 45.4 %collective-permute-start.2 = (bf16[256,1024]{1,0:T(8,128)(2,1)}, bf16[256,1024]{1,0:T(8,128)(2,1)}, u32[]{:S(2)}, u32[]{:S(2)}) collective-permute-start(bf16[256,1024]{1,0:T(8,128)(2,1)} %param.16), channel_id=1, source_target_pairs={{16,0},{24,8},{32,16},{40,24},{48,32},{56,40},{64,48},{72,56},{80,... | collective-permute-start | bytes 1572872 | tf_op jit(solution)/shard_map/ppermute | solution.py:18
  17.1 28.5 %collective-permute-start.1 = (bf16[2,256,1024]{1,2,0:T(8,128)(2,1)}, bf16[2,256,1024]{1,2,0:T(8,128)(2,1)S(1)}, u32[]{:S(2)}, u32[]{:S(2)}) collective-permute-start(bf16[2,256,1024]{1,2,0:T(8,128)(2,1)} %pad_maximum_fusion), channel_id=1, source_target_pairs={{0,8},{8,16},{16,24},{24,32},{32,40},{40,48},{48,56},{56,64},{64,7... | collective-permute-start | bytes 3145736 | tf_op jit(solution)/shard_map/ppermute | solution.py:18
  27.9 4.8 %copy-start.2 = (bf16[127,1024]{1,0:T(8,128)(2,1)}, bf16[127,1024]{1,0:T(8,128)(2,1)S(1)}, u32[]{:S(2)}) copy-start(bf16[127,1024]{1,0:T(8,128)(2,1)S(1)} %collective-permute-done) | copy-start | bytes 780292
  29.0 3.7 %copy-start.7 = (bf16[256,1024]{0,1:T(8,128)(2,1)S(1)}, bf16[256,1024]{0,1:T(8,128)(2,1)}, u32[]{:S(2)}) copy-start(bf16[256,1024]{0,1:T(8,128)(2,1)} %copy.40) | copy-start | bytes 1572868
  29.0 3.8 %copy-start.13 = (bf16[64,128,256]{2,1,0:T(8,128)(2,1)S(1)}, bf16[64,128,256]{2,1,0:T(8,128)(2,1)}, u32[]{:S(2)}) copy-start(bf16[64,128,256]{2,1,0:T(8,128)(2,1)} %get-tuple-element.10) | copy-start | bytes 12582916
  46.5 2.5 %copy-start.3 = (pred[256,512]{0,1:T(8,128)(4,1)S(1)}, pred[256,512]{0,1:T(8,128)(4,1)}, u32[]{:S(2)}) copy-start(pred[256,512]{0,1:T(8,128)(4,1)} %get-tuple-element.32) | copy-start | bytes 393220
  46.8 3.3 %copy-start.5 = (bf16[256,8,128]{2,0,1:T(8,128)(2,1)}, bf16[256,8,128]{2,0,1:T(8,128)(2,1)S(1)}, u32[]{:S(2)}) copy-start(bf16[256,8,128]{2,0,1:T(8,128)(2,1)S(1)} %copy.45) | copy-start | bytes 1572868
  46.8 3.3 %copy-start.8 = (bf16[1,256,1024]{1,2,0:T(8,128)(2,1)S(1)}, bf16[1,256,1024]{1,2,0:T(8,128)(2,1)}, u32[]{:S(2)}) copy-start(bf16[1,256,1024]{1,2,0:T(8,128)(2,1)} %get-tuple-element.29) | copy-start | bytes 1572868
  50.1 1.3 %copy-start.4 = (bf16[256,8,128]{2,0,1:T(8,128)(2,1)S(1)}, bf16[256,8,128]{2,0,1:T(8,128)(2,1)}, u32[]{:S(2)}) copy-start(bf16[256,8,128]{2,0,1:T(8,128)(2,1)} %copy.46) | copy-start | bytes 1572868
  50.1 1.3 %copy-start.6 = (bf16[256,8,128]{2,0,1:T(8,128)(2,1)S(1)}, bf16[256,8,128]{2,0,1:T(8,128)(2,1)}, u32[]{:S(2)}) copy-start(bf16[256,8,128]{2,0,1:T(8,128)(2,1)} %copy-done.5) | copy-start | bytes 1572868
  55.6 0.9 copy-start.9
  56.5 3.8 %copy-start.11 = (pred[128,256]{1,0:T(8,128)(4,1)S(1)}, pred[128,256]{1,0:T(8,128)(4,1)}, u32[]{:S(2)}) copy-start(pred[128,256]{1,0:T(8,128)(4,1)} %get-tuple-element.35) | copy-start | bytes 98308
  56.7 3.5 %copy-start.14 = (bf16[64,128,256]{2,1,0:T(8,128)(2,1)S(1)}, bf16[64,128,256]{2,1,0:T(8,128)(2,1)}, u32[]{:S(2)}) copy-start(bf16[64,128,256]{2,1,0:T(8,128)(2,1)} %get-tuple-element.10) | copy-start | bytes 12582916
  60.3 5.2 %copy-start = (bf16[256,1024]{1,0:T(8,128)(2,1)S(1)}, bf16[256,1024]{1,0:T(8,128)(2,1)}, u32[]{:S(2)}) copy-start(bf16[256,1024]{1,0:T(8,128)(2,1)} %param.11) | copy-start | bytes 1572868
  60.3 5.2 %copy-start.1 = (bf16[256,1024]{1,0:T(8,128)(2,1)S(1)}, bf16[256,1024]{1,0:T(8,128)(2,1)}, u32[]{:S(2)}) copy-start(bf16[256,1024]{1,0:T(8,128)(2,1)} %param.10) | copy-start | bytes 1572868
  60.3 15.4 %copy-start.12 = (f32[1024]{0:T(1024)S(1)}, f32[1024]{0:T(1024)}, u32[]{:S(2)}) copy-start(f32[1024]{0:T(1024)} %param.15) | copy-start | bytes 12292
  63.6 30.7 %collective-permute-start.6 = (bf16[256,1152]{0,1:T(8,128)(2,1)}, bf16[256,1152]{0,1:T(8,128)(2,1)S(1)}, u32[]{:S(2)}, u32[]{:S(2)}) collective-permute-start(bf16[256,1152]{0,1:T(8,128)(2,1)} %copy-done.9), channel_id=1, source_target_pairs={{0,16},{8,24},{16,32},{24,40},{32,48},{40,56},{48,64},{56,72},{64,... | collective-permute-start | bytes 1769480 | tf_op jit(solution)/shard_map/ppermute | solution.py:18
  65.8 1.2 %collective-permute-start.3 = (f32[256]{0:T(256)S(1)}, f32[256]{0:T(256)S(1)}, u32[]{:S(2)}, u32[]{:S(2)}) collective-permute-start(f32[256]{0:T(256)S(1)} %multiply_reduce_fusion), channel_id=1, source_target_pairs={{0,1},{1,0},{2,3},{3,2},{4,5},{5,4},{6,7},{7,6},{8,9},{9,8},{10,11... | collective-permute-start | bytes 3080 | tf_op jit(solution)/shard_map/ppermute | solution.py:92
  67.1 3.6 %collective-permute-start.4 = (f32[256]{0:T(256)S(1)}, f32[256]{0:T(256)S(1)}, u32[]{:S(2)}, u32[]{:S(2)}) collective-permute-start(f32[256]{0:T(256)S(1)} %add.106), channel_id=1, source_target_pairs={{0,2},{1,3},{2,0},{3,1},{4,6},{5,7},{6,4},{7,5},{8,10},{9,11},{10,... | collective-permute-start | bytes 3080 | tf_op jit(solution)/shard_map/ppermute | solution.py:92
  70.6 5.1 %collective-permute-start.5 = (f32[256]{0:T(256)S(1)}, f32[256]{0:T(256)S(1)}, u32[]{:S(2)}, u32[]{:S(2)}) collective-permute-start(f32[256]{0:T(256)S(1)} %add.107), channel_id=1, source_target_pairs={{0,4},{1,5},{2,6},{3,7},{4,0},{5,1},{6,2},{7,3},{8,12},{9,13},{10,... | collective-permute-start | bytes 3080 | tf_op jit(solution)/shard_map/ppermute | solution.py:92
